TPU v7x, 256 devices: a whole 4x4x8 slice. The times are simulated.
256 devices in a mesh: obs: 4 (over y), blk: 64 (over x, z, core).
Axes of the slice: x: 4, y: 4, z: 8, core: 2. Of those that a mesh axis runs over, the one named last changes fastest.
Arguments:
- design_tiles: float32 [32768, 8, 128], P(('obs', 'blk')), may hold values from -8 to 8
- block_ids: int32 [32768, 8], P(('obs', 'blk')), may hold values from 0 to 63, as said below
- obs_weight: float32 [32768], P(('obs', 'blk')), may hold values from 4.8828126e-05 to 0.00048828125
- block_owner: int32 [64], replicated, may hold values from 0 to 63, each once
- prior_weight: float32 [512], replicated, may hold values from 0.25 to 1
Outputs:
- panel_factor: float32 [8192, 256], P('blk')
- panel_update: float32 [8192, 256], P('blk')
Inputs may be any that keep to these rules, and one draw needn't show every extreme that they name: `block_ids`: the 8 blocks of an observation are distinct. Among the 128 observations of one device (aligned blocks of rows) no block is named by more than 24 of them, and in every draw some device has a block named by exactly 24. `block_owner`: A permutation: each owner index once.
All inputs are finite; a program needn't handle non-finite values.
Results may differ from a plain program's by a relative error of at most 0.0003.
Values sent between devices are 32-bit elements; how exact they have to be, the bound alone decides.
No kernel may reach another device: no remote copies, remote signals or barrier semaphores. Data moves between devices by JAX's collectives and lax.ppermute only.
A program may use at most 64 MiB of HBM per device.

v0:
```python
import jax
import jax.numpy as jnp
from jax import lax
from jax.sharding import PartitionSpec as P

CAP = 24
HI = lax.Precision.HIGHEST
FIRST = 8


def dot(a, b):
    return jnp.dot(a, b, precision=HI, preferred_element_type=jnp.float32)


def factor_inverse(mirrored):
    n = mirrored.shape[0] // 2
    eye = jnp.eye(n, dtype=jnp.float32)
    low = jnp.linalg.cholesky(mirrored[:n, :n])
    low_inv = jax.scipy.linalg.solve_triangular(low, eye, lower=True)
    left = dot(mirrored[n:, :n], low_inv.T)
    high = jnp.linalg.cholesky(mirrored[n:, n:] - dot(left, left.T))
    high_inv = jax.scipy.linalg.solve_triangular(high, eye, lower=True)
    corner = -dot(high_inv, dot(left, low_inv))
    return jnp.concatenate(
        [jnp.concatenate([low_inv, jnp.zeros_like(low_inv)], axis=1), jnp.concatenate([corner, high_inv], axis=1)],
        axis=0,
    )


def select_columns(labels, design_tiles, wanted):
    touched = design_tiles.shape[1]
    columns = jnp.zeros(
        (design_tiles.shape[0], wanted.shape[0], design_tiles.shape[2]), jnp.float32
    )
    for entry in range(touched):
        hit = labels[:, entry, None] == wanted[None, :]
        columns = columns + jnp.where(hit[:, :, None], design_tiles[:, entry, None, :], 0.0)
    return columns.reshape(design_tiles.shape[0], wanted.shape[0] * design_tiles.shape[2])


def butterfly(x, axis):
    n = lax.axis_size(axis)
    step = 1
    while step < n:
        perm = [(i, i ^ step) for i in range(n)]
        x = x + lax.ppermute(x, axis, perm)
        step *= 2
    return x


def local(design_tiles, block_ids, obs_weight, block_owner, prior_weight):
    n_obs, touched, bw = design_tiles.shape
    nblk = block_owner.shape[0]
    panel_cols = prior_weight.shape[0]
    half = panel_cols // 2
    panel_blocks = panel_cols // bw
    nb = lax.axis_size("blk")
    my_j = lax.axis_index("blk")
    block_range = jnp.arange(nblk, dtype=jnp.int32)
    dest_range = jnp.arange(nb, dtype=jnp.int32)

    inv_owner = jnp.sum(
        jnp.where(block_owner[None, :] == dest_range[:, None], block_range[None, :], 0), axis=1
    )
    slot_owner = jnp.sum(
        jnp.where(block_ids[:, :, None] == block_range[None, None, :], block_owner[None, None, :], 0),
        axis=2,
    )
    hit = slot_owner[:, :, None] == dest_range[None, None, :]
    touch = jnp.sum(hit.astype(jnp.int32), axis=1)
    cum = jnp.cumsum(touch, axis=0)
    rank_range = jnp.arange(CAP, dtype=jnp.int32)
    obs_sel = jnp.sum((cum[:, :, None] <= rank_range[None, None, :]).astype(jnp.int32), axis=0)
    valid = rank_range[None, :] < cum[-1][:, None]
    obs_sel = jnp.minimum(obs_sel, n_obs - 1)
    owners_sel = slot_owner[obs_sel]
    k_sel = jnp.sum(
        jnp.where(owners_sel == dest_range[:, None, None], jnp.arange(touched, dtype=jnp.int32), 0),
        axis=2,
    )
    flat_tiles = design_tiles.reshape(n_obs * touched, bw)
    tile_rows = flat_tiles[obs_sel * touched + k_sel]

    panel_design = select_columns(
        block_ids, design_tiles, jnp.arange(panel_blocks, dtype=jnp.int32)
    )
    weighted = panel_design * obs_weight[:, None]
    panel_rows = weighted[obs_sel]
    tile_rows = jnp.where(valid[:, :, None], tile_rows, 0.0)
    panel_rows = jnp.where(valid[:, :, None], panel_rows, 0.0)

    gram = jnp.einsum("op,oq->pq", weighted, panel_design[:, :half], precision=HI)
    square = butterfly(butterfly(gram, "obs"), "blk")
    diag = jnp.arange(half, dtype=jnp.int32)
    square = square + jnp.where(
        diag[None, :] == jnp.arange(panel_cols, dtype=jnp.int32)[:, None], prior_weight[None, :half], 0.0
    )

    owned = 0.0
    for lo, hi in ((0, FIRST), (FIRST, CAP)):
        payload = jnp.concatenate([tile_rows[:, lo:hi], panel_rows[:, lo:hi]], axis=2)
        got = lax.all_to_all(payload, "blk", 0, 0, tiled=True).reshape(nb * (hi - lo), bw + panel_cols)
        owned = owned + jnp.einsum("si,sp->ip", got[:, :bw], got[:, bw:], precision=HI)
    owned = butterfly(owned, "obs")

    my_block = jnp.sum(jnp.where(block_owner == my_j, block_range, 0))
    row_index = my_block * bw + jnp.arange(bw, dtype=jnp.int32)
    col_index = jnp.arange(panel_cols, dtype=jnp.int32)
    owned = owned + jnp.where(col_index[None, :] == row_index[:, None], prior_weight[None, :], 0.0)

    inverse = factor_inverse(0.5 * (square[:half] + square[:half].T))
    coupling = jnp.dot(square[half:], inverse.T, precision=HI, preferred_element_type=jnp.float32)
    first_rows = jnp.dot(owned[:, :half], inverse.T, precision=HI, preferred_element_type=jnp.float32)
    update_rows = owned[:, half:] - jnp.dot(
        first_rows, coupling.T, precision=HI, preferred_element_type=jnp.float32
    )
    return (first_rows, update_rows)


def solution(mesh):
    in_specs = (P(("obs", "blk"), None, None), P(("obs", "blk"), None), P(("obs", "blk")), P(), P())
    out_specs = (P("blk", None), P("blk", None))
    return jax.shard_map(local, mesh=mesh, in_specs=in_specs, out_specs=out_specs, check_vma=False)
```

profile of v0, /device:TPU:1, one launch (start us, length us, event | category | flops | bytes accessed | tf_op | source)
XLA Modules:
  0.0 288.8 jit_solution(11775561959726960728)
XLA Ops:
  0.6 1.0 slice_bitcast_fusion.8
  1.6 0.8 select_reduce_fusion.1
  2.9 3.4 %fusion.39 = (f32[128,1,128]{2,1,0:T(1,128)S(1)}, f32[128,1,128]{2,1,0:T(1,128)S(1)}, f32[128,1,128]{2,1,0:T(1,128)S(1)}, f32[128,1,128]{2,1,0:T(1,128)S(1)}, f3...) fusion(f32[128,8,128]{2,1,0:T(8,128)} %param.8), kind=kLoop, calls=%fused_computation.101 | loop fusion | bytes 1048576 | tf_op jit(solution)/shard_map/slice | solution.py:37
  6.4 1.2 convert_reduce_fusion
  8.1 1.4 add_add_fusion
  10.4 3.8 %gather_fusion.2 = f32[1536,512]{1,0:T(8,128)S(1)} fusion(f32[128,512]{1,0:T(8,128)S(1)} %broadcast_multiply_fusion, s32[2048]{0:T(1024)S(1)} %pad_clamp_fusion.1), kind=kCustom, calls=%fused_computation.2 | custom fusion | bytes 6297600 | tf_op jit(solution)/shard_map/gather | solution.py:88
  14.5 1.6 copy-done.1
  16.2 2.6 gather_fusion
  18.8 1.2 select_reduce_fusion
  20.1 2.6 gather_fusion.1
  23.0 1.2 pad_maximum_fusion.1
  24.2 13.0 %all-to-all-start = ((f32[64,8,640]{2,1,0:T(8,128)}), f32[64,8,640]{2,1,0:T(8,128)S(1)}, u32[]{:S(2)}, u32[]{:S(2)}) async-start(f32[64,8,640]{2,1,0:T(8,128)} %pad_maximum_fusion.1), calls=%async_computation | async-start | bytes 2621440 | tf_op jit(solution)/shard_map/all_to_all | solution.py:102
  37.8 1.4 collective-permute-start.2
  39.2 11.7 %collective-permute-done.2 = f32[512,256]{1,0:T(8,128)S(1)} collective-permute-done((f32[512,256]{1,0:T(8,128)S(1)}, f32[512,256]{1,0:T(8,128)S(1)}, u32[]{:S(2)}, u32[]{:S(2)}) %collective-permute-start.2) | collective-permute-done | bytes 524320 | tf_op jit(solution)/shard_map/ppermute | solution.py:46
  51.0 3.0 %collective-permute-start.3 = (f32[512,256]{1,0:T(8,128)S(1)}, f32[512,256]{1,0:T(8,128)S(1)}, u32[]{:S(2)}, u32[]{:S(2)}) collective-permute-start(f32[512,256]{1,0:T(8,128)S(1)} %add.148), channel_id=1, source_target_pairs={{0,128},{64,192},{128,0},{192,64},{1,129},{65,193},{129,1},{193,65... | collective-permute-start | bytes 1572872 | tf_op jit(solution)/shard_map/ppermute | solution.py:46
  54.0 10.8 %collective-permute-done.3 = f32[512,256]{1,0:T(8,128)S(1)} collective-permute-done((f32[512,256]{1,0:T(8,128)S(1)}, f32[512,256]{1,0:T(8,128)S(1)}, u32[]{:S(2)}, u32[]{:S(2)}) %collective-permute-start.3) | collective-permute-done | bytes 524320 | tf_op jit(solution)/shard_map/ppermute | solution.py:46
  64.9 2.3 collective-permute-start.4
  67.1 1.5 collective-permute-done.4
  68.7 1.5 collective-permute-start.5
  70.2 1.8 pad_maximum_fusion
  72.0 1.1 copy-done.2
  73.0 9.5 %all-to-all-start.1 = ((f32[64,16,640]{2,1,0:T(8,128)}), f32[64,16,640]{2,1,0:T(8,128)S(1)}, u32[]{:S(2)}, u32[]{:S(2)}) async-start(f32[64,16,640]{2,1,0:T(8,128)} %pad_maximum_fusion), calls=%async_computation.1 | async-start | bytes 5242880 | tf_op jit(solution)/shard_map/all_to_all | solution.py:102
  82.6 1.1 add.151
  83.7 2.3 collective-permute-start.6
  86.1 78.0 %collective-permute-done.6 = f32[512,256]{1,0:T(8,128)S(1)} collective-permute-done((f32[512,256]{1,0:T(8,128)S(1)}, f32[512,256]{1,0:T(8,128)S(1)}, u32[]{:S(2)}, u32[]{:S(2)}) %collective-permute-start.6) | collective-permute-done | bytes 524320 | tf_op jit(solution)/shard_map/ppermute | solution.py:46
  164.1 3.8 %collective-permute-start.7 = (f32[512,256]{1,0:T(8,128)S(1)}, f32[512,256]{1,0:T(8,128)S(1)}, u32[]{:S(2)}, u32[]{:S(2)}) collective-permute-start(f32[512,256]{1,0:T(8,128)S(1)} %add.152), channel_id=1, source_target_pairs={{0,8},{1,9},{2,10},{3,11},{4,12},{5,13},{6,14},{7,15},{8,0},{9,1},... | collective-permute-start | bytes 1572872 | tf_op jit(solution)/shard_map/ppermute | solution.py:46
  167.9 24.6 %collective-permute-done.7 = f32[512,256]{1,0:T(8,128)S(1)} collective-permute-done((f32[512,256]{1,0:T(8,128)S(1)}, f32[512,256]{1,0:T(8,128)S(1)}, u32[]{:S(2)}, u32[]{:S(2)}) %collective-permute-start.7) | collective-permute-done | bytes 524320 | tf_op jit(solution)/shard_map/ppermute | solution.py:46
  192.6 1.4 collective-permute-start.8
  194.1 11.2 %collective-permute-done.8 = f32[512,256]{1,0:T(8,128)S(1)} collective-permute-done((f32[512,256]{1,0:T(8,128)S(1)}, f32[512,256]{1,0:T(8,128)S(1)}, u32[]{:S(2)}, u32[]{:S(2)}) %collective-permute-start.8) | collective-permute-done | bytes 524320 | tf_op jit(solution)/shard_map/ppermute | solution.py:46
  205.4 2.8 collective-permute-start.9
  209.5 2.8 fusion.5
  212.3 6.3 %collective-permute-done.9 = f32[512,256]{1,0:T(8,128)} collective-permute-done((f32[512,256]{1,0:T(8,128)S(1)}, f32[512,256]{1,0:T(8,128)}, u32[]{:S(2)}, u32[]{:S(2)}) %collective-permute-start.9) | collective-permute-done | bytes 524320 | tf_op jit(solution)/shard_map/ppermute | solution.py:46
  218.6 1.3 select_add_fusion
  219.9 0.8 copy.24
  220.7 1.0 fusion.11
  221.8 11.7 %cholesky.44 = f32[128,128]{1,0:T(8,128)S(1)} custom-call(f32[128,128]{1,0:T(8,128)S(1)} %fusion.31), custom_call_target="Cholesky" | custom-call | tf_op jit(solution)/shard_map/jit(cholesky)/cholesky | solution.py:18
  234.9 9.8 %custom-call.6 = f32[1,128,128]{1,2,0:T(8,128)S(1)} custom-call(f32[1,128,128]{2,1,0:T(8,128)S(1)} %fusion.24), custom_call_target="InvertDiagBlocksLowerTriangular" | custom-call | tf_op jit(solution)/shard_map/jit(_solve_triangular)/triangular_solve | solution.py:19
  245.3 0.9 convolution_subtract_fusion
  246.2 0.9 copy.27
  247.1 0.9 fusion.29
  248.0 11.7 %cholesky.55 = f32[128,128]{1,0:T(8,128)S(1)} custom-call(f32[128,128]{1,0:T(8,128)S(1)} %fusion.29), custom_call_target="Cholesky" | custom-call | tf_op jit(solution)/shard_map/jit(cholesky)/cholesky | solution.py:21
  261.0 10.0 %custom-call.7 = f32[1,128,128]{1,2,0:T(8,128)S(1)} custom-call(f32[1,128,128]{2,1,0:T(8,128)S(1)} %fusion.25), custom_call_target="InvertDiagBlocksLowerTriangular" | custom-call | tf_op jit(solution)/shard_map/jit(_solve_triangular)/triangular_solve | solution.py:22
  271.0 2.3 fusion.2
  273.3 1.4 collective-permute-start
  275.2 3.5 %collective-permute-done = f32[128,512]{1,0:T(8,128)S(1)} collective-permute-done((f32[128,512]{1,0:T(8,128)S(1)}, f32[128,512]{1,0:T(8,128)S(1)}, u32[]{:S(2)}, u32[]{:S(2)}) %collective-permute-start) | collective-permute-done | bytes 262176 | tf_op jit(solution)/shard_map/ppermute | solution.py:46
  278.7 3.0 %collective-permute-start.1 = (f32[128,512]{1,0:T(8,128)S(1)}, f32[128,512]{1,0:T(8,128)S(1)}, u32[]{:S(2)}, u32[]{:S(2)}) collective-permute-start(f32[128,512]{1,0:T(8,128)S(1)} %add.143), channel_id=1, source_target_pairs={{0,128},{64,192},{128,0},{192,64},{1,129},{65,193},{129,1},{193,65... | collective-permute-start | bytes 786440 | tf_op jit(solution)/shard_map/ppermute | solution.py:46
  282.5 4.7 %collective-permute-done.1 = f32[128,512]{1,0:T(8,128)S(1)} collective-permute-done((f32[128,512]{1,0:T(8,128)S(1)}, f32[128,512]{1,0:T(8,128)S(1)}, u32[]{:S(2)}, u32[]{:S(2)}) %collective-permute-start.1) | collective-permute-done | bytes 262176 | tf_op jit(solution)/shard_map/ppermute | solution.py:46
  287.7 1.1 slice_subtract_fusion
  (78 shorter events, 9.6 us)
Async XLA Ops:
  0.6 9.7 %copy-start.8 = (f32[128]{0:T(128)S(1)}, f32[128]{0:T(128)}, u32[]{:S(2)}) copy-start(f32[128]{0:T(128)} %param.10) | copy-start | bytes 1540
  9.6 0.7 copy-start.3
  14.5 1.6 copy-start.1
  16.2 3.9 %copy-start = (f32[128,8,128]{2,1,0:T(8,128)S(1)}, f32[128,8,128]{2,1,0:T(8,128)}, u32[]{:S(2)}) copy-start(f32[128,8,128]{2,1,0:T(8,128)} %param.8) | copy-start | bytes 1572868
  23.0 14.2 %copy-start.4 = (f32[128,4,128]{2,1,0:T(4,128)S(1)}, f32[128,4,128]{2,1,0:T(4,128)}, u32[]{:S(2)}) copy-start(f32[128,4,128]{2,1,0:T(4,128)} %copy-done.3) | copy-start | bytes 786436
  24.2 47.8 %all-to-all-start = ((f32[64,8,640]{2,1,0:T(8,128)}), f32[64,8,640]{2,1,0:T(8,128)S(1)}, u32[]{:S(2)}, u32[]{:S(2)}) async-start(f32[64,8,640]{2,1,0:T(8,128)} %pad_maximum_fusion.1), calls=%async_computation | async-start | bytes 2621440 | tf_op jit(solution)/shard_map/all_to_all | solution.py:102
  37.8 13.1 %collective-permute-start.2 = (f32[512,256]{1,0:T(8,128)S(1)}, f32[512,256]{1,0:T(8,128)S(1)}, u32[]{:S(2)}, u32[]{:S(2)}) collective-permute-start(f32[512,256]{1,0:T(8,128)S(1)} %fusion.17), channel_id=1, source_target_pairs={{0,64},{64,0},{128,192},{192,128},{1,65},{65,1},{129,193},{193,129... | collective-permute-start | bytes 1572872 | tf_op jit(solution)/shard_map/ppermute | solution.py:46
  51.0 13.8 %collective-permute-start.3 = (f32[512,256]{1,0:T(8,128)S(1)}, f32[512,256]{1,0:T(8,128)S(1)}, u32[]{:S(2)}, u32[]{:S(2)}) collective-permute-start(f32[512,256]{1,0:T(8,128)S(1)} %add.148), channel_id=1, source_target_pairs={{0,128},{64,192},{128,0},{192,64},{1,129},{65,193},{129,1},{193,65... | collective-permute-start | bytes 1572872 | tf_op jit(solution)/shard_map/ppermute | solution.py:46
  64.8 5.4 %slice-start = ((f32[64,24,512]{2,1,0:T(8,128)}), f32[64,16,512]{2,1,0:T(8,128)S(1)}, s32[]{:S(2)}) async-start(f32[64,24,512]{2,1,0:T(8,128)} %copy-done.1), calls=%async_computation.2 | async-start | bytes 4194304 | tf_op jit(solution)/shard_map/slice | solution.py:101
  64.9 3.8 %collective-permute-start.4 = (f32[512,256]{1,0:T(8,128)S(1)}, f32[512,256]{1,0:T(8,128)S(1)}, u32[]{:S(2)}, u32[]{:S(2)}) collective-permute-start(f32[512,256]{1,0:T(8,128)S(1)} %add.149), channel_id=1, source_target_pairs={{0,1},{1,0},{2,3},{3,2},{4,5},{5,4},{6,7},{7,6},{8,9},{9,8},{10,11... | collective-permute-start | bytes 1572872 | tf_op jit(solution)/shard_map/ppermute | solution.py:46
  68.7 13.9 %collective-permute-start.5 = (f32[512,256]{1,0:T(8,128)S(1)}, f32[512,256]{1,0:T(8,128)}, u32[]{:S(2)}, u32[]{:S(2)}) collective-permute-start(f32[512,256]{1,0:T(8,128)S(1)} %add.150), channel_id=1, source_target_pairs={{0,2},{1,3},{2,0},{3,1},{4,6},{5,7},{6,4},{7,5},{8,10},{9,11},{10,... | collective-permute-start | bytes 1572872 | tf_op jit(solution)/shard_map/ppermute | solution.py:46
  72.0 1.1 copy-start.2
  73.0 198.0 %all-to-all-start.1 = ((f32[64,16,640]{2,1,0:T(8,128)}), f32[64,16,640]{2,1,0:T(8,128)S(1)}, u32[]{:S(2)}, u32[]{:S(2)}) async-start(f32[64,16,640]{2,1,0:T(8,128)} %pad_maximum_fusion), calls=%async_computation.1 | async-start | bytes 5242880 | tf_op jit(solution)/shard_map/all_to_all | solution.py:102
  83.7 124.5 %copy-start.9 = (s32[64]{0:T(128)S(1)}, s32[64]{0:T(128)}, u32[]{:S(2)}) copy-start(s32[64]{0:T(128)} %param.11) | copy-start | bytes 772
  83.7 80.3 %collective-permute-start.6 = (f32[512,256]{1,0:T(8,128)S(1)}, f32[512,256]{1,0:T(8,128)S(1)}, u32[]{:S(2)}, u32[]{:S(2)}) collective-permute-start(f32[512,256]{1,0:T(8,128)S(1)} %add.151), channel_id=1, source_target_pairs={{0,4},{1,5},{2,6},{3,7},{4,0},{5,1},{6,2},{7,3},{8,12},{9,13},{10,... | collective-permute-start | bytes 1572872 | tf_op jit(solution)/shard_map/ppermute | solution.py:46
  164.1 54.5 %slice-start.1 = ((f32[512]{0:T(512)}), f32[256]{0:T(256)S(1)}, s32[]{:S(2)}) async-start(f32[512]{0:T(512)} %param.12), calls=%async_computation.3 | async-start | bytes 2048 | tf_op jit(solution)/shard_map/slice | solution.py:96
  164.1 28.4 %collective-permute-start.7 = (f32[512,256]{1,0:T(8,128)S(1)}, f32[512,256]{1,0:T(8,128)S(1)}, u32[]{:S(2)}, u32[]{:S(2)}) collective-permute-start(f32[512,256]{1,0:T(8,128)S(1)} %add.152), channel_id=1, source_target_pairs={{0,8},{1,9},{2,10},{3,11},{4,12},{5,13},{6,14},{7,15},{8,0},{9,1},... | collective-permute-start | bytes 1572872 | tf_op jit(solution)/shard_map/ppermute | solution.py:46
  192.6 12.6 %collective-permute-start.8 = (f32[512,256]{1,0:T(8,128)S(1)}, f32[512,256]{1,0:T(8,128)S(1)}, u32[]{:S(2)}, u32[]{:S(2)}) collective-permute-start(f32[512,256]{1,0:T(8,128)S(1)} %add.153), channel_id=1, source_target_pairs={{0,16},{1,17},{2,18},{3,19},{4,20},{5,21},{6,22},{7,23},{8,24},{9,... | collective-permute-start | bytes 1572872 | tf_op jit(solution)/shard_map/ppermute | solution.py:46
  205.3 7.0 %copy-start.5 = (f32[512,256]{1,0:T(8,128)}, f32[512,256]{1,0:T(8,128)S(1)}, u32[]{:S(2)}) copy-start(f32[512,256]{1,0:T(8,128)S(1)} %add.154) | copy-start | bytes 1572868
  205.4 13.2 %collective-permute-start.9 = (f32[512,256]{1,0:T(8,128)S(1)}, f32[512,256]{1,0:T(8,128)}, u32[]{:S(2)}, u32[]{:S(2)}) collective-permute-start(f32[512,256]{1,0:T(8,128)S(1)} %add.154), channel_id=1, source_target_pairs={{0,32},{1,33},{2,34},{3,35},{4,36},{5,37},{6,38},{7,39},{8,40},{9,... | collective-permute-start | bytes 1572872 | tf_op jit(solution)/shard_map/ppermute | solution.py:46
  271.0 16.2 %copy-start.7 = (f32[512]{0:T(512)S(1)}, f32[512]{0:T(512)}, u32[]{:S(2)}) copy-start(f32[512]{0:T(512)} %param.12) | copy-start | bytes 6148
  273.3 5.3 %collective-permute-start = (f32[128,512]{1,0:T(8,128)S(1)}, f32[128,512]{1,0:T(8,128)S(1)}, u32[]{:S(2)}, u32[]{:S(2)}) collective-permute-start(f32[128,512]{1,0:T(8,128)S(1)} %fusion.2), channel_id=1, source_target_pairs={{0,64},{64,0},{128,192},{192,128},{1,65},{65,1},{129,193},{193,129... | collective-permute-start | bytes 786440 | tf_op jit(solution)/shard_map/ppermute | solution.py:46
  278.7 8.5 %collective-permute-start.1 = (f32[128,512]{1,0:T(8,128)S(1)}, f32[128,512]{1,0:T(8,128)S(1)}, u32[]{:S(2)}, u32[]{:S(2)}) collective-permute-start(f32[128,512]{1,0:T(8,128)S(1)} %add.143), channel_id=1, source_target_pairs={{0,128},{64,192},{128,0},{192,64},{1,129},{65,193},{129,1},{193,65... | collective-permute-start | bytes 786440 | tf_op jit(solution)/shard_map/ppermute | solution.py:46
  287.7 1.1 copy-start.6
where the time goes:
time: 293 us; the launch traced here: 289 us
  waiting for transfers between devices  152 us (52%)
  other arithmetic  60.1 us (21%)
  starting transfers between devices  45.5 us (16%)
  local copies, waits for them, and re-layouts  19.4 us (7%)
  matrix products  9.84 us (3%)
    ppermute x10, waiting for transfers between devices, butterfly(): x = x + lax.ppermute(x, axis, perm)  152 us
    ppermute x10, starting transfers between devices, butterfly(): x = x + lax.ppermute(x, axis, perm)  22.9 us
    all_to_all x2, starting transfers between devices, local(): lax.all_to_all(payload, 'blk', 0, 0, tiled=True)  22.5 us
    another operation x3, other arithmetic, factor_inverse(): high = jnp.linalg.cholesky(mirrored[n:, n:] - dot(left, left.T))  12.4 us
    another operation x3, other arithmetic, factor_inverse(): low = jnp.linalg.cholesky(mirrored[:n, :n])  12.4 us
    another operation x2, other arithmetic, factor_inverse(): high_inv = jax.scipy.linalg.solve_triangular(high, eye, lower=True)  10.6 us
    another operation x2, other arithmetic, factor_inverse(): low_inv = jax.scipy.linalg.solve_triangular(low, eye, lower=True)  10.5 us
  transfers between devices with their start and end apart: 12, of which 9 were waited for; matrix products, arithmetic and copies ran while one was open for 21% of the time, Pallas kernels for 0%

commit v1 on v0

--- a/solution.py
+++ b/solution.py
@@ -38,12 +38,12 @@
     return columns.reshape(design_tiles.shape[0], wanted.shape[0] * design_tiles.shape[2])
 
 
-def butterfly(x, axis):
-    n = lax.axis_size(axis)
+def obs_butterfly(x):
+    n = lax.axis_size("obs")
     step = 1
     while step < n:
         perm = [(i, i ^ step) for i in range(n)]
-        x = x + lax.ppermute(x, axis, perm)
+        x = x + lax.ppermute(x, "obs", perm)
         step *= 2
     return x
 
@@ -90,7 +90,11 @@
     panel_rows = jnp.where(valid[:, :, None], panel_rows, 0.0)
 
     gram = jnp.einsum("op,oq->pq", weighted, panel_design[:, :half], precision=HI)
-    square = butterfly(butterfly(gram, "obs"), "blk")
+    gram_rows = panel_cols // nb
+    got_gram = lax.all_to_all(gram.reshape(nb, gram_rows, half), "blk", 0, 0, tiled=True)
+    gram_part = obs_butterfly(jnp.sum(got_gram, axis=0))
+    spread = jnp.broadcast_to(gram_part[None], (nb, gram_rows, half))
+    square = lax.all_to_all(spread, "blk", 0, 0, tiled=True).reshape(panel_cols, half)
     diag = jnp.arange(half, dtype=jnp.int32)
     square = square + jnp.where(
         diag[None, :] == jnp.arange(panel_cols, dtype=jnp.int32)[:, None], prior_weight[None, :half], 0.0
@@ -101,7 +105,7 @@
         payload = jnp.concatenate([tile_rows[:, lo:hi], panel_rows[:, lo:hi]], axis=2)
         got = lax.all_to_all(payload, "blk", 0, 0, tiled=True).reshape(nb * (hi - lo), bw + panel_cols)
         owned = owned + jnp.einsum("si,sp->ip", got[:, :bw], got[:, bw:], precision=HI)
-    owned = butterfly(owned, "obs")
+    owned = obs_butterfly(owned)
 
     my_block = jnp.sum(jnp.where(block_owner == my_j, block_range, 0))
     row_index = my_block * bw + jnp.arange(bw, dtype=jnp.int32)

time: 293 us -> 204 us (0.70); the launches traced: 289 us -> 204 us
  waiting for transfers between devices: 152 us -> 72.6 us
  starting transfers between devices: 45.5 us -> 39.5 us
    ppermute x10 -> x4, waiting for transfers between devices: 152 us -> 14.7 us  [obs_butterfly(): x = x + lax.ppermute(x, 'obs', perm)]
    all_to_all x2, waiting for transfers between devices: 0.01 us -> 36.5 us  [local(): lax.all_to_all(payload, 'blk', 0, 0, tiled=True)]
    all_to_all x0 -> x2, waiting for transfers between devices: none -> 21.3 us  [the longest x1 15.5 us: local(): lax.all_to_all(gram.reshape(nb, gram_rows, half), 'blk', 0, 0, tiled=True)]
    all_to_all x0 -> x2, starting transfers between devices: none -> 20.9 us  [the longest x1 13 us: local(): lax.all_to_all(gram.reshape(nb, gram_rows, half), 'blk', 0, 0, tiled=True)]
    ppermute x10 -> x4, starting transfers between devices: 22.9 us -> 5.96 us  [obs_butterfly(): x = x + lax.ppermute(x, 'obs', perm)]
    all_to_all x2, starting transfers between devices: 22.5 us -> 12.6 us  [local(): lax.all_to_all(payload, 'blk', 0, 0, tiled=True)]
  transfers between devices with their start and end apart: 12 -> 8, of which waited for: 9 -> 7; matrix products, arithmetic and copies ran while one was open for 21% -> 37% of each run, Pallas kernels for 0% -> 0%
where the time goes in v1:
time: 204 us
  waiting for transfers between devices  72.6 us (36%)
  other arithmetic  60.2 us (30%)
  starting transfers between devices  39.5 us (19%)
  local copies, waits for them, and re-layouts  20.7 us (10%)
  matrix products  8.9 us (4%)
    all_to_all x2, waiting for transfers between devices, local(): lax.all_to_all(payload, 'blk', 0, 0, tiled=True)  36.5 us
    all_to_all x1, waiting for transfers between devices, local(): lax.all_to_all(gram.reshape(nb, gram_rows, half), 'blk', 0, 0, tiled=True)  15.5 us
    ppermute x4, waiting for transfers between devices, obs_butterfly(): x = x + lax.ppermute(x, 'obs', perm)  14.7 us
    all_to_all x1, starting transfers between devices, local(): lax.all_to_all(gram.reshape(nb, gram_rows, half), 'blk', 0, 0, tiled=True)  13 us
    all_to_all x2, starting transfers between devices, local(): lax.all_to_all(payload, 'blk', 0, 0, tiled=True)  12.6 us
    another operation x3, other arithmetic, factor_inverse(): low = jnp.linalg.cholesky(mirrored[:n, :n])  12.4 us
    another operation x3, other arithmetic, factor_inverse(): high = jnp.linalg.cholesky(mirrored[n:, n:] - dot(left, left.T))  12.4 us
    another operation x2, other arithmetic, factor_inverse(): high_inv = jax.scipy.linalg.solve_triangular(high, eye, lower=True)  11.3 us
  transfers between devices with their start and end apart: 8, of which 7 were waited for; matrix products, arithmetic and copies ran while one was open for 37% of the time, Pallas kernels for 0%

profile of v1, /device:TPU:1, one launch (start us, length us, event | category | flops | bytes accessed | tf_op | source)
XLA Modules:
  0.0 203.7 jit_solution(8093854011499966835)
XLA Ops:
  0.7 3.3 %fusion.39 = (f32[128,1,128]{2,1,0:T(1,128)S(1)}, f32[128,1,128]{2,1,0:T(1,128)S(1)}, f32[128,1,128]{2,1,0:T(1,128)S(1)}, f32[128,1,128]{2,1,0:T(1,128)S(1)}, f3...) fusion(f32[128,8,128]{2,1,0:T(8,128)} %param.8), kind=kLoop, calls=%fused_computation.102 | loop fusion | bytes 1048576 | tf_op jit(solution)/shard_map/slice | solution.py:37
  4.0 1.0 slice_bitcast_fusion.10
  5.4 1.4 add_add_fusion
  7.1 1.4 fusion.12
  8.5 13.0 %all-to-all-start.2 = ((f32[64,8,256]{2,1,0:T(8,128)}), f32[64,8,256]{2,1,0:T(8,128)S(1)}, u32[]{:S(2)}, u32[]{:S(2)}) async-start(f32[64,8,256]{2,1,0:T(8,128)} %fusion.12), calls=%async_computation.2 | async-start | bytes 1048576 | tf_op jit(solution)/shard_map/all_to_all | solution.py:94
  22.0 1.2 convert_reduce_fusion
  23.3 15.5 %all-to-all-done.2 = f32[64,8,256]{2,1,0:T(8,128)S(1)} async-done(((f32[64,8,256]{2,1,0:T(8,128)}), f32[64,8,256]{2,1,0:T(8,128)S(1)}, u32[]{:S(2)}, u32[]{:S(2)}) %all-to-all-start.2) | async-done | bytes 524320 | tf_op jit(solution)/shard_map/all_to_all | solution.py:94
  38.8 1.4 collective-permute-start.2
  40.4 1.0 collective-permute-done.2
  41.4 2.9 %collective-permute-start.3 = (f32[8,256]{1,0:T(8,128)S(1)}, f32[8,256]{1,0:T(8,128)S(1)}, u32[]{:S(2)}, u32[]{:S(2)}) collective-permute-start(f32[8,256]{1,0:T(8,128)S(1)} %add.130), channel_id=1, source_target_pairs={{0,128},{64,192},{128,0},{192,64},{1,129},{65,193},{129,1},{193,65... | collective-permute-start | bytes 24584 | tf_op jit(solution)/shard_map/ppermute | solution.py:46
  44.3 3.8 %gather_fusion.2 = f32[1536,512]{1,0:T(8,128)S(1)} fusion(f32[128,512]{1,0:T(8,128)S(1)} %broadcast_multiply_fusion, s32[2048]{0:T(1024)S(1)} %pad_clamp_fusion.1), kind=kCustom, calls=%fused_computation.2 | custom fusion | bytes 6297600 | tf_op jit(solution)/shard_map/gather | solution.py:88
  48.1 0.8 broadcast_in_dim.266
  49.0 7.9 %all-to-all-start.3 = ((f32[64,8,256]{2,1,0:T(8,128)}), f32[64,8,256]{2,1,0:T(8,128)}, u32[]{:S(2)}, u32[]{:S(2)}) async-start(f32[64,8,256]{2,1,0:T(8,128)} %broadcast_in_dim.266), calls=%async_computation.3 | async-start | bytes 1048576 | tf_op jit(solution)/shard_map/all_to_all | solution.py:97
  56.9 2.0 broadcast_select_fusion
  59.0 1.3 slice.177
  60.3 2.6 %gather_fusion = s32[1536,8]{1,0:T(8,128)S(1)} fusion(s32[128,8]{1,0:T(8,128)S(1)} %copy.25, s32[2048]{0:T(1024)S(1)} %pad_clamp_fusion.1), kind=kCustom, calls=%fused_computation | custom fusion | bytes 104448 | tf_op jit(solution)/shard_map/gather | solution.py:76
  62.9 1.2 select_reduce_fusion
  64.2 2.6 %gather_fusion.1 = f32[1536,128]{1,0:T(8,128)S(1)} fusion(f32[1024,128]{1,0:T(8,128)S(1)} %bitcast.94, s32[2048]{0:T(1024)S(1)} %pad_clamp_fusion), kind=kCustom, calls=%fused_computation.1 | custom fusion | bytes 1579008 | tf_op jit(solution)/shard_map/gather | solution.py:82
  67.1 1.2 pad_maximum_fusion.1
  68.2 5.8 %all-to-all-done.3 = f32[64,8,256]{2,1,0:T(8,128)} async-done(((f32[64,8,256]{2,1,0:T(8,128)}), f32[64,8,256]{2,1,0:T(8,128)}, u32[]{:S(2)}, u32[]{:S(2)}) %all-to-all-start.3) | async-done | bytes 524320 | tf_op jit(solution)/shard_map/all_to_all | solution.py:97
  74.1 6.3 %all-to-all-start = ((f32[64,8,640]{2,1,0:T(8,128)}), f32[64,8,640]{2,1,0:T(8,128)S(1)}, u32[]{:S(2)}, u32[]{:S(2)}) async-start(f32[64,8,640]{2,1,0:T(8,128)} %pad_maximum_fusion.1), calls=%async_computation | async-start | bytes 2621440 | tf_op jit(solution)/shard_map/all_to_all | solution.py:106
  80.4 1.5 slice-done
  82.0 1.8 pad_maximum_fusion
  83.7 30.8 %all-to-all-done = f32[64,8,640]{2,1,0:T(8,128)S(1)} async-done(((f32[64,8,640]{2,1,0:T(8,128)}), f32[64,8,640]{2,1,0:T(8,128)S(1)}, u32[]{:S(2)}, u32[]{:S(2)}) %all-to-all-start) | async-done | bytes 1310752 | tf_op jit(solution)/shard_map/all_to_all | solution.py:106
  114.5 1.1 copy-done.1
  115.6 6.3 %all-to-all-start.1 = ((f32[64,16,640]{2,1,0:T(8,128)}), f32[64,16,640]{2,1,0:T(8,128)S(1)}, u32[]{:S(2)}, u32[]{:S(2)}) async-start(f32[64,16,640]{2,1,0:T(8,128)} %pad_maximum_fusion), calls=%async_computation.1 | async-start | bytes 5242880 | tf_op jit(solution)/shard_map/all_to_all | solution.py:106
  122.0 0.6 fusion.32
  123.3 1.1 bitcast_add_fusion
  124.4 0.8 copy.27
  125.2 1.0 fusion.11
  126.3 11.7 %cholesky.44 = f32[128,128]{1,0:T(8,128)S(1)} custom-call(f32[128,128]{1,0:T(8,128)S(1)} %fusion.31), custom_call_target="Cholesky" | custom-call | tf_op jit(solution)/shard_map/jit(cholesky)/cholesky | solution.py:18
  138.1 0.6 compare_reduce_fusion.1
  138.7 0.7 fusion.24
  139.4 9.8 %custom-call.6 = f32[1,128,128]{1,2,0:T(8,128)S(1)} custom-call(f32[1,128,128]{2,1,0:T(8,128)S(1)} %fusion.24), custom_call_target="InvertDiagBlocksLowerTriangular" | custom-call | tf_op jit(solution)/shard_map/jit(_solve_triangular)/triangular_solve | solution.py:19
  149.8 0.9 convolution_subtract_fusion
  150.7 0.9 copy.30
  151.6 0.9 fusion.29
  152.5 11.7 %cholesky.55 = f32[128,128]{1,0:T(8,128)S(1)} custom-call(f32[128,128]{1,0:T(8,128)S(1)} %fusion.29), custom_call_target="Cholesky" | custom-call | tf_op jit(solution)/shard_map/jit(cholesky)/cholesky | solution.py:21
  164.2 0.6 compare_reduce_fusion
  164.9 0.7 fusion.25
  165.5 10.6 %custom-call.7 = f32[1,128,128]{1,2,0:T(8,128)} custom-call(f32[1,128,128]{2,1,0:T(8,128)S(1)} %fusion.25), custom_call_target="InvertDiagBlocksLowerTriangular" | custom-call | tf_op jit(solution)/shard_map/jit(_solve_triangular)/triangular_solve | solution.py:22
  176.2 2.1 %fusion.5 = f32[128,512]{1,0:T(8,128)S(1)} fusion(f32[512,640]{1,0:T(8,128)} %bitcast.97), kind=kOutput, calls=%fused_computation.11 | convolution fusion | flops 402653184 | bytes 1572864 | tf_op jit(solution)/shard_map/si,sp->ip/dot_general | solution.py:107
  178.3 5.8 %all-to-all-done.1 = f32[64,16,640]{2,1,0:T(8,128)S(1)} async-done(((f32[64,16,640]{2,1,0:T(8,128)}), f32[64,16,640]{2,1,0:T(8,128)S(1)}, u32[]{:S(2)}, u32[]{:S(2)}) %all-to-all-start.1) | async-done | bytes 2621472 | tf_op jit(solution)/shard_map/all_to_all | solution.py:106
  184.0 1.4 fusion.2
  186.4 7.0 %collective-permute-done = f32[128,512]{1,0:T(8,128)S(1)} collective-permute-done((f32[128,512]{1,0:T(8,128)S(1)}, f32[128,512]{1,0:T(8,128)S(1)}, u32[]{:S(2)}, u32[]{:S(2)}) %collective-permute-start) | collective-permute-done | bytes 262176 | tf_op jit(solution)/shard_map/ppermute | solution.py:46
  193.4 1.2 collective-permute-start.1
  195.4 6.6 %collective-permute-done.1 = f32[128,512]{1,0:T(8,128)S(1)} collective-permute-done((f32[128,512]{1,0:T(8,128)S(1)}, f32[128,512]{1,0:T(8,128)S(1)}, u32[]{:S(2)}, u32[]{:S(2)}) %collective-permute-start.1) | collective-permute-done | bytes 262176 | tf_op jit(solution)/shard_map/ppermute | solution.py:46
  202.6 1.1 slice_subtract_fusion
  (65 shorter events, 5.0 us)
Async XLA Ops:
  0.6 20.8 %copy-start.4 = (s32[128,8]{0,1:T(8,128)S(1)}, s32[128,8]{0,1:T(8,128)}, u32[]{:S(2)}) copy-start(s32[128,8]{0,1:T(8,128)} %param.9) | copy-start | bytes 12292
  0.6 6.2 %copy-start.6 = (f32[128]{0:T(128)S(1)}, f32[128]{0:T(128)}, u32[]{:S(2)}) copy-start(f32[128]{0:T(128)} %param.10) | copy-start | bytes 1540
  0.7 20.8 %copy-start.7 = (s32[64]{0:T(128)S(1)}, s32[64]{0:T(128)}, u32[]{:S(2)}) copy-start(s32[64]{0:T(128)} %param.11) | copy-start | bytes 772
  8.5 30.3 %all-to-all-start.2 = ((f32[64,8,256]{2,1,0:T(8,128)}), f32[64,8,256]{2,1,0:T(8,128)S(1)}, u32[]{:S(2)}, u32[]{:S(2)}) async-start(f32[64,8,256]{2,1,0:T(8,128)} %fusion.12), calls=%async_computation.2 | async-start | bytes 1048576 | tf_op jit(solution)/shard_map/all_to_all | solution.py:94
  38.8 2.6 %collective-permute-start.2 = (f32[8,256]{1,0:T(8,128)S(1)}, f32[8,256]{1,0:T(8,128)S(1)}, u32[]{:S(2)}, u32[]{:S(2)}) collective-permute-start(f32[8,256]{1,0:T(8,128)S(1)} %reduce_sum.62), channel_id=1, source_target_pairs={{0,64},{64,0},{128,192},{192,128},{1,65},{65,1},{129,193},{193,129... | collective-permute-start | bytes 24584 | tf_op jit(solution)/shard_map/ppermute | solution.py:46
  41.4 6.7 %collective-permute-start.3 = (f32[8,256]{1,0:T(8,128)S(1)}, f32[8,256]{1,0:T(8,128)S(1)}, u32[]{:S(2)}, u32[]{:S(2)}) collective-permute-start(f32[8,256]{1,0:T(8,128)S(1)} %add.130), channel_id=1, source_target_pairs={{0,128},{64,192},{128,0},{192,64},{1,129},{65,193},{129,1},{193,65... | collective-permute-start | bytes 24584 | tf_op jit(solution)/shard_map/ppermute | solution.py:46
  49.0 25.1 %all-to-all-start.3 = ((f32[64,8,256]{2,1,0:T(8,128)}), f32[64,8,256]{2,1,0:T(8,128)}, u32[]{:S(2)}, u32[]{:S(2)}) async-start(f32[64,8,256]{2,1,0:T(8,128)} %broadcast_in_dim.266), calls=%async_computation.3 | async-start | bytes 1048576 | tf_op jit(solution)/shard_map/all_to_all | solution.py:97
  60.3 3.9 %copy-start = (f32[128,8,128]{2,1,0:T(8,128)S(1)}, f32[128,8,128]{2,1,0:T(8,128)}, u32[]{:S(2)}) copy-start(f32[128,8,128]{2,1,0:T(8,128)} %param.8) | copy-start | bytes 1572868
  74.1 40.4 %all-to-all-start = ((f32[64,8,640]{2,1,0:T(8,128)}), f32[64,8,640]{2,1,0:T(8,128)S(1)}, u32[]{:S(2)}, u32[]{:S(2)}) async-start(f32[64,8,640]{2,1,0:T(8,128)} %pad_maximum_fusion.1), calls=%async_computation | async-start | bytes 2621440 | tf_op jit(solution)/shard_map/all_to_all | solution.py:106
  80.4 1.6 slice-start
  83.7 39.5 %slice-start.1 = ((f32[512]{0:T(512)}), f32[256]{0:T(256)S(1)}, s32[]{:S(2)}) async-start(f32[512]{0:T(512)} %param.12), calls=%async_computation.5 | async-start | bytes 2048 | tf_op jit(solution)/shard_map/slice | solution.py:100
  114.5 1.1 copy-start.1
  115.6 68.4 %all-to-all-start.1 = ((f32[64,16,640]{2,1,0:T(8,128)}), f32[64,16,640]{2,1,0:T(8,128)S(1)}, u32[]{:S(2)}, u32[]{:S(2)}) async-start(f32[64,16,640]{2,1,0:T(8,128)} %pad_maximum_fusion), calls=%async_computation.1 | async-start | bytes 5242880 | tf_op jit(solution)/shard_map/all_to_all | solution.py:106
  184.0 1.9 copy-start.3
  184.0 18.1 %copy-start.5 = (f32[512]{0:T(512)S(1)}, f32[512]{0:T(512)}, u32[]{:S(2)}) copy-start(f32[512]{0:T(512)} %param.12) | copy-start | bytes 6148
  185.4 8.0 %collective-permute-start = (f32[128,512]{1,0:T(8,128)S(1)}, f32[128,512]{1,0:T(8,128)S(1)}, u32[]{:S(2)}, u32[]{:S(2)}) collective-permute-start(f32[128,512]{1,0:T(8,128)S(1)} %fusion.2), channel_id=1, source_target_pairs={{0,64},{64,0},{128,192},{192,128},{1,65},{65,1},{129,193},{193,129... | collective-permute-start | bytes 786440 | tf_op jit(solution)/shard_map/ppermute | solution.py:46
  193.4 8.6 %collective-permute-start.1 = (f32[128,512]{1,0:T(8,128)S(1)}, f32[128,512]{1,0:T(8,128)S(1)}, u32[]{:S(2)}, u32[]{:S(2)}) collective-permute-start(f32[128,512]{1,0:T(8,128)S(1)} %add.125), channel_id=1, source_target_pairs={{0,128},{64,192},{128,0},{192,64},{1,129},{65,193},{129,1},{193,65... | collective-permute-start | bytes 786440 | tf_op jit(solution)/shard_map/ppermute | solution.py:46
  202.6 1.1 copy-start.2

commit v2 on v1

--- a/solution.py
+++ b/solution.py
@@ -94,17 +94,23 @@
     got_gram = lax.all_to_all(gram.reshape(nb, gram_rows, half), "blk", 0, 0, tiled=True)
     gram_part = obs_butterfly(jnp.sum(got_gram, axis=0))
     spread = jnp.broadcast_to(gram_part[None], (nb, gram_rows, half))
-    square = lax.all_to_all(spread, "blk", 0, 0, tiled=True).reshape(panel_cols, half)
+
+    def routed(lo, hi):
+        return [tile_rows[:, lo:hi], panel_rows[:, lo:hi]]
+
+    def owned_part(got):
+        got = got.reshape(-1, bw + panel_cols)
+        return jnp.einsum("si,sp->ip", got[:, :bw], got[:, bw:], precision=HI)
+
+    mixed = lax.all_to_all(jnp.concatenate([spread] + routed(0, FIRST), axis=2), "blk", 0, 0, tiled=True)
+    square = mixed[:, :, :half].reshape(panel_cols, half)
+    owned = owned_part(mixed[:, :, half:])
+    rest = lax.all_to_all(jnp.concatenate(routed(FIRST, CAP), axis=2), "blk", 0, 0, tiled=True)
+    owned = owned + owned_part(rest)
     diag = jnp.arange(half, dtype=jnp.int32)
     square = square + jnp.where(
         diag[None, :] == jnp.arange(panel_cols, dtype=jnp.int32)[:, None], prior_weight[None, :half], 0.0
     )
-
-    owned = 0.0
-    for lo, hi in ((0, FIRST), (FIRST, CAP)):
-        payload = jnp.concatenate([tile_rows[:, lo:hi], panel_rows[:, lo:hi]], axis=2)
-        got = lax.all_to_all(payload, "blk", 0, 0, tiled=True).reshape(nb * (hi - lo), bw + panel_cols)
-        owned = owned + jnp.einsum("si,sp->ip", got[:, :bw], got[:, bw:], precision=HI)
     owned = obs_butterfly(owned)
 
     my_block = jnp.sum(jnp.where(block_owner == my_j, block_range, 0))

time: 204 us -> 193 us (0.946)
  waiting for transfers between devices: 72.6 us -> 63.1 us
  starting transfers between devices: 39.5 us -> 36 us
  other arithmetic: 60.2 us -> 62.4 us
    all_to_all x1, waiting for transfers between devices: 15.5 us -> 2.45 us  [local(): lax.all_to_all(gram.reshape(nb, gram_rows, half), 'blk', 0, 0, tiled=True)]
    all_to_all x3 -> x2, waiting for transfers between devices: 42.4 us -> 47.7 us  [the longest x1 42 us: local(): lax.all_to_all(jnp.concatenate([spread] + routed(0, FIRST), axis=2), 'blk...]
    all_to_all x3 -> x2, starting transfers between devices: 20.5 us -> 15.5 us  [the longest x1 9.3 us: local(): lax.all_to_all(jnp.concatenate([spread] + routed(0, FIRST), axis=2), 'blk...]
  transfers between devices with their start and end apart: 8 -> 7, of which waited for: 7 -> 6; matrix products, arithmetic and copies ran while one was open for 37% -> 40% of each run, Pallas kernels for 0% -> 0%
where the time goes in v2:
time: 193 us; the launch traced here: 192 us
  waiting for transfers between devices  63.1 us (33%)
  other arithmetic  62.4 us (32%)
  starting transfers between devices  36 us (19%)
  local copies, waits for them, and re-layouts  21.5 us (11%)
  matrix products  7.61 us (4%)
    all_to_all x1, waiting for transfers between devices, local(): lax.all_to_all(jnp.concatenate([spread] + routed(0, FIRST), axis=2), 'blk...  42 us
    ppermute x4, waiting for transfers between devices, obs_butterfly(): x = x + lax.ppermute(x, 'obs', perm)  13 us
    all_to_all x1, starting transfers between devices, local(): lax.all_to_all(gram.reshape(nb, gram_rows, half), 'blk', 0, 0, tiled=True)  13 us
    another operation x3, other arithmetic, factor_inverse(): low = jnp.linalg.cholesky(mirrored[:n, :n])  12.4 us
    another operation x3, other arithmetic, factor_inverse(): high = jnp.linalg.cholesky(mirrored[n:, n:] - dot(left, left.T))  12.4 us
    another operation x2, other arithmetic, factor_inverse(): high_inv = jax.scipy.linalg.solve_triangular(high, eye, lower=True)  11.3 us
    another operation x2, other arithmetic, factor_inverse(): low_inv = jax.scipy.linalg.solve_triangular(low, eye, lower=True)  10.5 us
    all_to_all x1, starting transfers between devices, local(): lax.all_to_all(jnp.concatenate([spread] + routed(0, FIRST), axis=2), 'blk...  9.3 us
  transfers between devices with their start and end apart: 7, of which 6 were waited for; matrix products, arithmetic and copies ran while one was open for 40% of the time, Pallas kernels for 0%

profile of v2, /device:TPU:1, one launch (start us, length us, event | category | flops | bytes accessed | tf_op | source)
XLA Modules:
  0.0 192.4 jit_solution(12604260700257021496)
XLA Ops:
  0.6 1.0 slice_bitcast_fusion.12
  1.6 3.5 %fusion.40 = (f32[128,1,128]{2,1,0:T(1,128)S(1)}, f32[128,1,128]{2,1,0:T(1,128)S(1)}, f32[128,1,128]{2,1,0:T(1,128)S(1)}, f32[128,1,128]{2,1,0:T(1,128)S(1)}, f3...) fusion(f32[128,8,128]{2,1,0:T(8,128)} %param.8), kind=kLoop, calls=%fused_computation.104 | loop fusion | bytes 1048576 | tf_op jit(solution)/shard_map/slice | solution.py:37
  5.6 1.4 add_add_fusion
  7.3 1.4 fusion.13
  8.6 13.0 %all-to-all-start = ((f32[64,8,256]{2,1,0:T(8,128)}), f32[64,8,256]{2,1,0:T(8,128)S(1)}, u32[]{:S(2)}, u32[]{:S(2)}) async-start(f32[64,8,256]{2,1,0:T(8,128)} %fusion.13), calls=%async_computation | async-start | bytes 1048576 | tf_op jit(solution)/shard_map/all_to_all | solution.py:94
  22.3 1.2 convert_reduce_fusion
  23.6 5.0 %gather_fusion.2 = f32[1536,512]{1,0:T(8,128)} fusion(f32[128,512]{1,0:T(8,128)S(1)} %broadcast_multiply_fusion, s32[2048]{0:T(1024)S(1)} %pad_clamp_fusion.1), kind=kCustom, calls=%fused_computation.2 | custom fusion | bytes 6297600 | tf_op jit(solution)/shard_map/gather | solution.py:88
  28.6 2.6 %gather_fusion = s32[1536,8]{1,0:T(8,128)S(1)} fusion(s32[128,8]{1,0:T(8,128)S(1)} %copy.26, s32[2048]{0:T(1024)S(1)} %pad_clamp_fusion.1), kind=kCustom, calls=%fused_computation | custom fusion | bytes 104448 | tf_op jit(solution)/shard_map/gather | solution.py:76
  31.2 1.2 select_reduce_fusion
  32.5 3.9 %broadcast_select_fusion = f32[64,24,512]{2,1,0:T(8,128)} fusion(f32[64,24,512]{2,1,0:T(8,128)} %bitcast.98, pred[64,24]{1,0:T(8,128)(4,1)S(1)} %iota_compare_fusion.19), kind=kLoop, calls=%fused_computation.7 | loop fusion | flops 786432 | bytes 6292992 | tf_op jit(solution)/shard_map/jit(_where)/select_n | solution.py:90
  36.5 2.5 %all-to-all-done = f32[64,8,256]{2,1,0:T(8,128)S(1)} async-done(((f32[64,8,256]{2,1,0:T(8,128)}), f32[64,8,256]{2,1,0:T(8,128)S(1)}, u32[]{:S(2)}, u32[]{:S(2)}) %all-to-all-start) | async-done | bytes 524320 | tf_op jit(solution)/shard_map/all_to_all | solution.py:94
  39.0 1.4 collective-permute-start
  40.4 2.6 %gather_fusion.1 = f32[1536,128]{1,0:T(8,128)S(1)} fusion(f32[1024,128]{1,0:T(8,128)S(1)} %bitcast.97, s32[2048]{0:T(1024)S(1)} %pad_clamp_fusion), kind=kCustom, calls=%fused_computation.1 | custom fusion | bytes 1579008 | tf_op jit(solution)/shard_map/gather | solution.py:82
  43.0 2.7 %collective-permute-start.1 = (f32[8,256]{1,0:T(8,128)S(1)}, f32[8,256]{1,0:T(8,128)S(1)}, u32[]{:S(2)}, u32[]{:S(2)}) collective-permute-start(f32[8,256]{1,0:T(8,128)S(1)} %add.120), channel_id=1, source_target_pairs={{0,128},{64,192},{128,0},{192,64},{1,129},{65,193},{129,1},{193,65... | collective-permute-start | bytes 24584 | tf_op jit(solution)/shard_map/ppermute | solution.py:46
  46.0 1.1 collective-permute-done.1
  47.2 1.4 pad_maximum_fusion.1
  48.5 9.3 %all-to-all-start.1 = ((f32[64,8,896]{2,1,0:T(8,128)}), f32[64,8,896]{2,1,0:T(8,128)S(1)}, u32[]{:S(2)}, u32[]{:S(2)}) async-start(f32[64,8,896]{2,1,0:T(8,128)} %pad_maximum_fusion.1), calls=%async_computation.1 | async-start | bytes 3670016 | tf_op jit(solution)/shard_map/all_to_all | solution.py:105
  57.9 1.5 slice-done.1
  59.4 1.8 pad_maximum_fusion
  61.2 42.0 %all-to-all-done.1 = f32[64,8,896]{2,1,0:T(8,128)S(1)} async-done(((f32[64,8,896]{2,1,0:T(8,128)}), f32[64,8,896]{2,1,0:T(8,128)S(1)}, u32[]{:S(2)}, u32[]{:S(2)}) %all-to-all-start.1) | async-done | bytes 1835040 | tf_op jit(solution)/shard_map/all_to_all | solution.py:105
  103.2 1.2 copy-done.1
  104.5 6.2 %all-to-all-start.2 = ((f32[64,16,640]{2,1,0:T(8,128)}), f32[64,16,640]{2,1,0:T(8,128)S(1)}, u32[]{:S(2)}, u32[]{:S(2)}) async-start(f32[64,16,640]{2,1,0:T(8,128)} %pad_maximum_fusion), calls=%async_computation.2 | async-start | bytes 5242880 | tf_op jit(solution)/shard_map/all_to_all | solution.py:108
  110.7 0.6 fusion.33
  112.0 1.1 fusion.7
  113.1 0.8 copy.27
  113.9 1.0 fusion.12
  115.0 11.7 %cholesky.44 = f32[128,128]{1,0:T(8,128)S(1)} custom-call(f32[128,128]{1,0:T(8,128)S(1)} %fusion.32), custom_call_target="Cholesky" | custom-call | tf_op jit(solution)/shard_map/jit(cholesky)/cholesky | solution.py:18
  126.8 0.6 compare_reduce_fusion.1
  127.4 0.7 fusion.25
  128.1 9.8 %custom-call.6 = f32[1,128,128]{1,2,0:T(8,128)S(1)} custom-call(f32[1,128,128]{2,1,0:T(8,128)S(1)} %fusion.25), custom_call_target="InvertDiagBlocksLowerTriangular" | custom-call | tf_op jit(solution)/shard_map/jit(_solve_triangular)/triangular_solve | solution.py:19
  138.5 0.9 convolution_subtract_fusion
  139.4 0.9 copy.30
  140.3 0.9 fusion.30
  141.2 11.7 %cholesky.55 = f32[128,128]{1,0:T(8,128)S(1)} custom-call(f32[128,128]{1,0:T(8,128)S(1)} %fusion.30), custom_call_target="Cholesky" | custom-call | tf_op jit(solution)/shard_map/jit(cholesky)/cholesky | solution.py:21
  152.9 0.6 compare_reduce_fusion
  153.6 0.7 fusion.26
  154.2 10.6 %custom-call.7 = f32[1,128,128]{1,2,0:T(8,128)} custom-call(f32[1,128,128]{2,1,0:T(8,128)S(1)} %fusion.26), custom_call_target="InvertDiagBlocksLowerTriangular" | custom-call | tf_op jit(solution)/shard_map/jit(_solve_triangular)/triangular_solve | solution.py:22
  164.8 1.4 slice_bitcast_fusion
  166.3 0.8 fusion.5
  167.0 5.7 %all-to-all-done.2 = f32[64,16,640]{2,1,0:T(8,128)S(1)} async-done(((f32[64,16,640]{2,1,0:T(8,128)}), f32[64,16,640]{2,1,0:T(8,128)S(1)}, u32[]{:S(2)}, u32[]{:S(2)}) %all-to-all-start.2) | async-done | bytes 2621472 | tf_op jit(solution)/shard_map/all_to_all | solution.py:108
  172.7 1.4 fusion.2
  174.1 0.7 collective-permute-start.2
  175.3 6.8 %collective-permute-done.2 = f32[128,512]{1,0:T(8,128)S(1)} collective-permute-done((f32[128,512]{1,0:T(8,128)S(1)}, f32[128,512]{1,0:T(8,128)S(1)}, u32[]{:S(2)}, u32[]{:S(2)}) %collective-permute-start.2) | collective-permute-done | bytes 262176 | tf_op jit(solution)/shard_map/ppermute | solution.py:46
  182.1 2.7 %collective-permute-start.3 = (f32[128,512]{1,0:T(8,128)S(1)}, f32[128,512]{1,0:T(8,128)S(1)}, u32[]{:S(2)}, u32[]{:S(2)}) collective-permute-start(f32[128,512]{1,0:T(8,128)S(1)} %add.127), channel_id=1, source_target_pairs={{0,128},{64,192},{128,0},{192,64},{1,129},{65,193},{129,1},{193,65... | collective-permute-start | bytes 786440 | tf_op jit(solution)/shard_map/ppermute | solution.py:46
  185.2 0.4 fusion.9
  185.6 5.1 %collective-permute-done.3 = f32[128,512]{1,0:T(8,128)S(1)} collective-permute-done((f32[128,512]{1,0:T(8,128)S(1)}, f32[128,512]{1,0:T(8,128)S(1)}, u32[]{:S(2)}, u32[]{:S(2)}) %collective-permute-start.3) | collective-permute-done | bytes 262176 | tf_op jit(solution)/shard_map/ppermute | solution.py:46
  190.9 0.4 fusion.15
  191.3 1.1 slice_subtract_fusion
  (65 shorter events, 3.8 us)
Async XLA Ops:
  0.6 6.4 %copy-start.6 = (f32[128]{0:T(128)S(1)}, f32[128]{0:T(128)}, u32[]{:S(2)}) copy-start(f32[128]{0:T(128)} %param.10) | copy-start | bytes 1540
  7.0 14.7 %copy-start.4 = (s32[128,8]{0,1:T(8,128)S(1)}, s32[128,8]{0,1:T(8,128)}, u32[]{:S(2)}) copy-start(s32[128,8]{0,1:T(8,128)} %param.9) | copy-start | bytes 12292
  7.0 14.7 %copy-start.7 = (s32[64]{0:T(128)S(1)}, s32[64]{0:T(128)}, u32[]{:S(2)}) copy-start(s32[64]{0:T(128)} %param.11) | copy-start | bytes 772
  8.6 30.3 %all-to-all-start = ((f32[64,8,256]{2,1,0:T(8,128)}), f32[64,8,256]{2,1,0:T(8,128)S(1)}, u32[]{:S(2)}, u32[]{:S(2)}) async-start(f32[64,8,256]{2,1,0:T(8,128)} %fusion.13), calls=%async_computation | async-start | bytes 1048576 | tf_op jit(solution)/shard_map/all_to_all | solution.py:94
  32.5 7.9 %copy-start = (f32[128,8,128]{2,1,0:T(8,128)S(1)}, f32[128,8,128]{2,1,0:T(8,128)}, u32[]{:S(2)}) copy-start(f32[128,8,128]{2,1,0:T(8,128)} %param.8) | copy-start | bytes 1572868
  39.0 4.0 %collective-permute-start = (f32[8,256]{1,0:T(8,128)S(1)}, f32[8,256]{1,0:T(8,128)S(1)}, u32[]{:S(2)}, u32[]{:S(2)}) collective-permute-start(f32[8,256]{1,0:T(8,128)S(1)} %reduce_sum.56), channel_id=1, source_target_pairs={{0,64},{64,0},{128,192},{192,128},{1,65},{65,1},{129,193},{193,129... | collective-permute-start | bytes 24584 | tf_op jit(solution)/shard_map/ppermute | solution.py:46
  43.0 4.1 %collective-permute-start.1 = (f32[8,256]{1,0:T(8,128)S(1)}, f32[8,256]{1,0:T(8,128)S(1)}, u32[]{:S(2)}, u32[]{:S(2)}) collective-permute-start(f32[8,256]{1,0:T(8,128)S(1)} %add.120), channel_id=1, source_target_pairs={{0,128},{64,192},{128,0},{192,64},{1,129},{65,193},{129,1},{193,65... | collective-permute-start | bytes 24584 | tf_op jit(solution)/shard_map/ppermute | solution.py:46
  45.7 1.4 slice-start
  48.5 54.7 %all-to-all-start.1 = ((f32[64,8,896]{2,1,0:T(8,128)}), f32[64,8,896]{2,1,0:T(8,128)S(1)}, u32[]{:S(2)}, u32[]{:S(2)}) async-start(f32[64,8,896]{2,1,0:T(8,128)} %pad_maximum_fusion.1), calls=%async_computation.1 | async-start | bytes 3670016 | tf_op jit(solution)/shard_map/all_to_all | solution.py:105
  57.8 1.6 slice-start.1
  61.2 50.8 %slice-start.2 = ((f32[512]{0:T(512)}), f32[256]{0:T(256)S(1)}, s32[]{:S(2)}) async-start(f32[512]{0:T(512)} %param.12), calls=%async_computation.5 | async-start | bytes 2048 | tf_op jit(solution)/shard_map/slice | solution.py:112
  103.2 1.2 copy-start.1
  104.5 68.2 %all-to-all-start.2 = ((f32[64,16,640]{2,1,0:T(8,128)}), f32[64,16,640]{2,1,0:T(8,128)S(1)}, u32[]{:S(2)}, u32[]{:S(2)}) async-start(f32[64,16,640]{2,1,0:T(8,128)} %pad_maximum_fusion), calls=%async_computation.2 | async-start | bytes 5242880 | tf_op jit(solution)/shard_map/all_to_all | solution.py:108
  172.7 2.1 %copy-start.3 = (f32[1,128,128]{1,2,0:T(8,128)S(1)}, f32[1,128,128]{1,2,0:T(8,128)}, u32[]{:S(2)}) copy-start(f32[1,128,128]{1,2,0:T(8,128)} %custom-call.7) | copy-start | bytes 196612
  172.7 18.1 %copy-start.5 = (f32[512]{0:T(512)S(1)}, f32[512]{0:T(512)}, u32[]{:S(2)}) copy-start(f32[512]{0:T(512)} %param.12) | copy-start | bytes 6148
  174.1 8.0 %collective-permute-start.2 = (f32[128,512]{1,0:T(8,128)S(1)}, f32[128,512]{1,0:T(8,128)S(1)}, u32[]{:S(2)}, u32[]{:S(2)}) collective-permute-start(f32[128,512]{1,0:T(8,128)S(1)} %fusion.2), channel_id=1, source_target_pairs={{0,64},{64,0},{128,192},{192,128},{1,65},{65,1},{129,193},{193,129... | collective-permute-start | bytes 786440 | tf_op jit(solution)/shard_map/ppermute | solution.py:46
  182.1 8.6 %collective-permute-start.3 = (f32[128,512]{1,0:T(8,128)S(1)}, f32[128,512]{1,0:T(8,128)S(1)}, u32[]{:S(2)}, u32[]{:S(2)}) collective-permute-start(f32[128,512]{1,0:T(8,128)S(1)} %add.127), channel_id=1, source_target_pairs={{0,128},{64,192},{128,0},{192,64},{1,129},{65,193},{129,1},{193,65... | collective-permute-start | bytes 786440 | tf_op jit(solution)/shard_map/ppermute | solution.py:46
  191.3 1.1 copy-start.2

commit v3 on v2

--- a/solution.py
+++ b/solution.py
@@ -40,12 +40,13 @@
 
 def obs_butterfly(x):
     n = lax.axis_size("obs")
-    step = 1
-    while step < n:
-        perm = [(i, i ^ step) for i in range(n)]
-        x = x + lax.ppermute(x, "obs", perm)
-        step *= 2
-    return x
+    me = lax.axis_index("obs")
+    got = [x] + [lax.ppermute(x, "obs", [(i, (i + s) % n) for i in range(n)]) for s in range(1, n)]
+    ordered = jnp.stack(got)
+    parts = [ordered[(me - src) % n] for src in range(n)]
+    while len(parts) > 1:
+        parts = [parts[i] + parts[i + 1] for i in range(0, len(parts), 2)]
+    return parts[0]
 
 
 def local(design_tiles, block_ids, obs_weight, block_owner, prior_weight):

time: 193 us -> 197 us (1.021)
  waiting for transfers between devices: 63.1 us -> 59.1 us
  other arithmetic: 62.4 us -> 65.4 us
  starting transfers between devices: 36 us -> 38.2 us
    all_to_all x1, waiting for transfers between devices: 2.45 us -> 0.38 us  [local(): lax.all_to_all(gram.reshape(nb, gram_rows, half), 'blk', 0, 0, tiled=True)]
    select_n x1, other arithmetic: 0.27 us -> 2.33 us  [local(): tile_rows = jnp.where(valid[:, :, None], tile_rows, 0.0)]
    ppermute x4 -> x6, waiting for transfers between devices: 13 us -> 11.7 us  [obs_butterfly(): lax.ppermute(x, 'obs', [(i, (i + s) % n) for i in range(n)])]
    ppermute x4 -> x6, starting transfers between devices: 7.53 us -> 7.85 us  [obs_butterfly(): lax.ppermute(x, 'obs', [(i, (i + s) % n) for i in range(n)])]
  transfers between devices with their start and end apart: 7 -> 9, of which waited for: 6 -> 6; matrix products, arithmetic and copies ran while one was open for 40% -> 41% of each run, Pallas kernels for 0% -> 0%
where the time goes in v3:
time: 197 us; the launch traced here: 196 us
  other arithmetic  65.4 us (33%)
  waiting for transfers between devices  59.1 us (30%)
  starting transfers between devices  38.2 us (19%)
  local copies, waits for them, and re-layouts  21.7 us (11%)
  matrix products  9.55 us (5%)
    all_to_all x1, waiting for transfers between devices, local(): lax.all_to_all(jnp.concatenate([spread] + routed(0, FIRST), axis=2), 'blk...  42.5 us
    all_to_all x1, starting transfers between devices, local(): lax.all_to_all(gram.reshape(nb, gram_rows, half), 'blk', 0, 0, tiled=True)  13.2 us
    another operation x3, other arithmetic, factor_inverse(): low = jnp.linalg.cholesky(mirrored[:n, :n])  12.4 us
    another operation x3, other arithmetic, factor_inverse(): high = jnp.linalg.cholesky(mirrored[n:, n:] - dot(left, left.T))  12.4 us
    ppermute x6, waiting for transfers between devices, obs_butterfly(): lax.ppermute(x, 'obs', [(i, (i + s) % n) for i in range(n)])  11.7 us
    all_to_all x1, starting transfers between devices, local(): lax.all_to_all(jnp.concatenate([spread] + routed(0, FIRST), axis=2), 'blk...  11 us
    another operation x2, other arithmetic, factor_inverse(): high_inv = jax.scipy.linalg.solve_triangular(high, eye, lower=True)  10.7 us
    another operation x2, other arithmetic, factor_inverse(): low_inv = jax.scipy.linalg.solve_triangular(low, eye, lower=True)  10.5 us
  transfers between devices with their start and end apart: 9, of which 6 were waited for; matrix products, arithmetic and copies ran while one was open for 41% of the time, Pallas kernels for 0%

profile of v3, /device:TPU:1, one launch (start us, length us, event | category | flops | bytes accessed | tf_op | source)
XLA Modules:
  0.0 195.6 jit_solution(11310569905718122350)
XLA Ops:
  0.6 1.0 slice_bitcast_fusion.12
  1.6 3.3 %fusion.40 = (f32[128,1,128]{2,1,0:T(1,128)S(1)}, f32[128,1,128]{2,1,0:T(1,128)S(1)}, f32[128,1,128]{2,1,0:T(1,128)S(1)}, f32[128,1,128]{2,1,0:T(1,128)S(1)}, f3...) fusion(f32[128,8,128]{2,1,0:T(8,128)} %param.8), kind=kLoop, calls=%fused_computation.107 | loop fusion | bytes 1048576 | tf_op jit(solution)/shard_map/slice | solution.py:37
  5.4 1.4 add_add_fusion
  7.1 1.4 fusion.13
  8.5 13.2 %all-to-all-start = ((f32[64,8,256]{2,1,0:T(8,128)}), f32[64,8,256]{2,1,0:T(8,128)}, u32[]{:S(2)}, u32[]{:S(2)}) async-start(f32[64,8,256]{2,1,0:T(8,128)} %fusion.13), calls=%async_computation | async-start | bytes 1048576 | tf_op jit(solution)/shard_map/all_to_all | solution.py:95
  22.3 1.2 convert_reduce_fusion
  23.6 2.6 %gather_fusion = s32[1536,8]{1,0:T(8,128)S(1)} fusion(s32[128,8]{1,0:T(8,128)S(1)} %copy.26, s32[2048]{0:T(1024)S(1)} %pad_clamp_fusion.1), kind=kCustom, calls=%fused_computation | custom fusion | bytes 104448 | tf_op jit(solution)/shard_map/gather | solution.py:77
  26.2 1.2 select_reduce_fusion
  27.4 5.0 %gather_fusion.2 = f32[1536,512]{1,0:T(8,128)} fusion(f32[128,512]{1,0:T(8,128)S(1)} %broadcast_multiply_fusion, s32[2048]{0:T(1024)S(1)} %pad_clamp_fusion.1), kind=kCustom, calls=%fused_computation.2 | custom fusion | bytes 6297600 | tf_op jit(solution)/shard_map/gather | solution.py:89
  32.5 3.7 %gather_fusion.1 = f32[1536,128]{1,0:T(8,128)} fusion(f32[1024,128]{1,0:T(8,128)S(1)} %bitcast.109, s32[2048]{0:T(1024)S(1)} %pad_clamp_fusion), kind=kCustom, calls=%fused_computation.1 | custom fusion | bytes 1579008 | tf_op jit(solution)/shard_map/gather | solution.py:83
  36.3 2.2 %broadcast_select_fusion = f32[64,24,512]{2,1,0:T(8,128)S(1)} fusion(f32[64,24,512]{2,1,0:T(8,128)} %bitcast.110, pred[64,24]{1,0:T(8,128)(4,1)S(1)} %iota_compare_fusion.19), kind=kLoop, calls=%fused_computation.7 | loop fusion | flops 786432 | bytes 6292992 | tf_op jit(solution)/shard_map/jit(_where)/select_n | solution.py:91
  38.9 1.1 reduce_sum.56
  40.0 1.4 collective-permute-start
  41.3 2.6 %collective-permute-start.1 = (f32[8,256]{1,0:T(8,128)S(1)}, f32[8,256]{1,0:T(8,128)S(1)}, u32[]{:S(2)}, u32[]{:S(2)}) collective-permute-start(f32[8,256]{1,0:T(8,128)S(1)} %reduce_sum.56), channel_id=1, source_target_pairs={{0,128},{64,192},{128,0},{192,64},{1,129},{65,193},{129,1},{193,65... | collective-permute-start | bytes 24584 | tf_op jit(solution)/shard_map/ppermute | solution.py:44
  44.0 1.1 collective-permute-start.2
  45.0 2.3 %broadcast_select_fusion.1 = f32[64,24,128]{2,1,0:T(8,128)} fusion(f32[64,24,128]{2,1,0:T(8,128)} %bitcast.115, pred[64,24]{1,0:T(8,128)(4,1)S(1)} %iota_compare_fusion.19), kind=kLoop, calls=%fused_computation.24 | loop fusion | flops 196608 | bytes 1574400 | tf_op jit(solution)/shard_map/jit(_where)/select_n | solution.py:90
  47.4 1.1 slice.186
  48.5 2.6 %pad_maximum_fusion.1 = f32[64,8,896]{2,1,0:T(8,128)} fusion(f32[64,8,512]{2,1,0:T(8,128)} %slice.186, f32[64,8,128]{2,1,0:T(8,128)S(1)} %slice-done, f32[64,8,256]{2,1,0:T(8,128)S(1)} %broadcast_in_dim.258), kind=kLoop, calls=%fused_computation.6 | loop fusion | flops 917504 | bytes 3670016 | tf_op jit(solution)/shard_map/concatenate | solution.py:106
  51.1 11.0 %all-to-all-start.1 = ((f32[64,8,896]{2,1,0:T(8,128)}), f32[64,8,896]{2,1,0:T(8,128)}, u32[]{:S(2)}, u32[]{:S(2)}) async-start(f32[64,8,896]{2,1,0:T(8,128)} %pad_maximum_fusion.1), calls=%async_computation.1 | async-start | bytes 3670016 | tf_op jit(solution)/shard_map/all_to_all | solution.py:106
  62.3 0.9 slice-done.1
  63.1 1.8 pad_maximum_fusion
  64.9 42.5 %all-to-all-done.1 = f32[64,8,896]{2,1,0:T(8,128)} async-done(((f32[64,8,896]{2,1,0:T(8,128)}), f32[64,8,896]{2,1,0:T(8,128)}, u32[]{:S(2)}, u32[]{:S(2)}) %all-to-all-start.1) | async-done | bytes 1835040 | tf_op jit(solution)/shard_map/all_to_all | solution.py:106
  107.4 6.2 %all-to-all-start.2 = ((f32[64,16,640]{2,1,0:T(8,128)}), f32[64,16,640]{2,1,0:T(8,128)S(1)}, u32[]{:S(2)}, u32[]{:S(2)}) async-start(f32[64,16,640]{2,1,0:T(8,128)} %pad_maximum_fusion), calls=%async_computation.2 | async-start | bytes 5242880 | tf_op jit(solution)/shard_map/all_to_all | solution.py:109
  114.9 1.1 fusion.7
  116.0 0.8 copy.27
  116.9 1.0 fusion.12
  118.0 11.7 %cholesky.44 = f32[128,128]{1,0:T(8,128)S(1)} custom-call(f32[128,128]{1,0:T(8,128)S(1)} %fusion.32), custom_call_target="Cholesky" | custom-call | tf_op jit(solution)/shard_map/jit(cholesky)/cholesky | solution.py:18
  129.7 0.6 compare_reduce_fusion.1
  130.4 0.7 fusion.25
  131.0 9.8 %custom-call.6 = f32[1,128,128]{1,2,0:T(8,128)S(1)} custom-call(f32[1,128,128]{2,1,0:T(8,128)S(1)} %fusion.25), custom_call_target="InvertDiagBlocksLowerTriangular" | custom-call | tf_op jit(solution)/shard_map/jit(_solve_triangular)/triangular_solve | solution.py:19
  141.4 0.9 convolution_subtract_fusion.1
  142.3 0.9 copy.30
  143.3 0.9 fusion.30
  144.1 11.7 %cholesky.55 = f32[128,128]{1,0:T(8,128)S(1)} custom-call(f32[128,128]{1,0:T(8,128)S(1)} %fusion.30), custom_call_target="Cholesky" | custom-call | tf_op jit(solution)/shard_map/jit(cholesky)/cholesky | solution.py:21
  155.9 0.6 compare_reduce_fusion
  156.5 0.7 fusion.26
  157.2 10.0 %custom-call.7 = f32[1,128,128]{1,2,0:T(8,128)S(1)} custom-call(f32[1,128,128]{2,1,0:T(8,128)S(1)} %fusion.26), custom_call_target="InvertDiagBlocksLowerTriangular" | custom-call | tf_op jit(solution)/shard_map/jit(_solve_triangular)/triangular_solve | solution.py:22
  167.2 0.9 fusion.21
  168.1 0.8 fusion.41
  168.9 1.4 slice_bitcast_fusion
  170.3 0.8 fusion.5
  171.1 4.6 %all-to-all-done.2 = f32[64,16,640]{2,1,0:T(8,128)S(1)} async-done(((f32[64,16,640]{2,1,0:T(8,128)}), f32[64,16,640]{2,1,0:T(8,128)S(1)}, u32[]{:S(2)}, u32[]{:S(2)}) %all-to-all-start.2) | async-done | bytes 2621472 | tf_op jit(solution)/shard_map/all_to_all | solution.py:109
  175.6 2.1 %fusion.2 = f32[128,512]{1,0:T(8,128)} fusion(f32[128,512]{1,0:T(8,128)S(1)} %fusion.5, f32[1024,640]{1,0:T(8,128)S(1)} %bitcast.111), kind=kOutput, calls=%fused_computation.9 | convolution fusion | flops 805371904 | bytes 3145728 | tf_op jit(solution)/shard_map/si,sp->ip/dot_general | solution.py:104
  178.1 1.9 collective-permute-start.4
  181.3 6.0 %collective-permute-done.3 = f32[128,512]{1,0:T(8,128)S(1)} collective-permute-done((f32[128,512]{1,0:T(8,128)}, f32[128,512]{1,0:T(8,128)S(1)}, u32[]{:S(2)}, u32[]{:S(2)}) %collective-permute-start.3) | collective-permute-done | bytes 262176 | tf_op jit(solution)/shard_map/ppermute | solution.py:44
  187.4 5.0 %collective-permute-done.4 = f32[128,512]{1,0:T(8,128)S(1)} collective-permute-done((f32[128,512]{1,0:T(8,128)}, f32[128,512]{1,0:T(8,128)S(1)}, u32[]{:S(2)}, u32[]{:S(2)}) %collective-permute-start.4) | collective-permute-done | bytes 262176 | tf_op jit(solution)/shard_map/ppermute | solution.py:44
  193.0 1.0 pad_maximum_fusion.2
  194.6 1.1 convolution_subtract_fusion
  (69 shorter events, 6.4 us)
Async XLA Ops:
  0.6 6.3 %copy-start.6 = (f32[128]{0:T(128)S(1)}, f32[128]{0:T(128)}, u32[]{:S(2)}) copy-start(f32[128]{0:T(128)} %param.10) | copy-start | bytes 1540
  6.8 14.9 %copy-start.4 = (s32[128,8]{0,1:T(8,128)S(1)}, s32[128,8]{0,1:T(8,128)}, u32[]{:S(2)}) copy-start(s32[128,8]{0,1:T(8,128)} %param.9) | copy-start | bytes 12292
  6.8 14.9 %copy-start.7 = (s32[64]{0:T(128)S(1)}, s32[64]{0:T(128)}, u32[]{:S(2)}) copy-start(s32[64]{0:T(128)} %param.11) | copy-start | bytes 772
  8.5 30.4 %all-to-all-start = ((f32[64,8,256]{2,1,0:T(8,128)}), f32[64,8,256]{2,1,0:T(8,128)}, u32[]{:S(2)}, u32[]{:S(2)}) async-start(f32[64,8,256]{2,1,0:T(8,128)} %fusion.13), calls=%async_computation | async-start | bytes 1048576 | tf_op jit(solution)/shard_map/all_to_all | solution.py:95
  27.4 5.1 %copy-start = (f32[128,8,128]{2,1,0:T(8,128)S(1)}, f32[128,8,128]{2,1,0:T(8,128)}, u32[]{:S(2)}) copy-start(f32[128,8,128]{2,1,0:T(8,128)} %param.8) | copy-start | bytes 1572868
  40.0 8.4 %collective-permute-start = (f32[8,256]{1,0:T(8,128)S(1)}, f32[8,256]{1,0:T(8,128)S(1)}, u32[]{:S(2)}, u32[]{:S(2)}) collective-permute-start(f32[8,256]{1,0:T(8,128)S(1)} %reduce_sum.56), channel_id=1, source_target_pairs={{0,64},{64,128},{128,192},{192,0},{1,65},{65,129},{129,193},{193,1... | collective-permute-start | bytes 24584 | tf_op jit(solution)/shard_map/ppermute | solution.py:44
  41.3 7.1 %collective-permute-start.1 = (f32[8,256]{1,0:T(8,128)S(1)}, f32[8,256]{1,0:T(8,128)S(1)}, u32[]{:S(2)}, u32[]{:S(2)}) collective-permute-start(f32[8,256]{1,0:T(8,128)S(1)} %reduce_sum.56), channel_id=1, source_target_pairs={{0,128},{64,192},{128,0},{192,64},{1,129},{65,193},{129,1},{193,65... | collective-permute-start | bytes 24584 | tf_op jit(solution)/shard_map/ppermute | solution.py:44
  44.0 4.5 %collective-permute-start.2 = (f32[8,256]{1,0:T(8,128)S(1)}, f32[8,256]{1,0:T(8,128)S(1)}, u32[]{:S(2)}, u32[]{:S(2)}) collective-permute-start(f32[8,256]{1,0:T(8,128)S(1)} %reduce_sum.56), channel_id=1, source_target_pairs={{0,192},{64,0},{128,64},{192,128},{1,193},{65,1},{129,65},{193,129... | collective-permute-start | bytes 24584 | tf_op jit(solution)/shard_map/ppermute | solution.py:44
  47.4 1.2 slice-start
  51.1 56.3 %all-to-all-start.1 = ((f32[64,8,896]{2,1,0:T(8,128)}), f32[64,8,896]{2,1,0:T(8,128)}, u32[]{:S(2)}, u32[]{:S(2)}) async-start(f32[64,8,896]{2,1,0:T(8,128)} %pad_maximum_fusion.1), calls=%async_computation.1 | async-start | bytes 3670016 | tf_op jit(solution)/shard_map/all_to_all | solution.py:106
  62.1 1.0 slice-start.1
  64.9 50.0 %slice-start.2 = ((f32[512]{0:T(512)}), f32[256]{0:T(256)S(1)}, s32[]{:S(2)}) async-start(f32[512]{0:T(512)} %param.12), calls=%async_computation.5 | async-start | bytes 2048 | tf_op jit(solution)/shard_map/slice | solution.py:113
  107.4 68.2 %all-to-all-start.2 = ((f32[64,16,640]{2,1,0:T(8,128)}), f32[64,16,640]{2,1,0:T(8,128)S(1)}, u32[]{:S(2)}, u32[]{:S(2)}) async-start(f32[64,16,640]{2,1,0:T(8,128)} %pad_maximum_fusion), calls=%async_computation.2 | async-start | bytes 5242880 | tf_op jit(solution)/shard_map/all_to_all | solution.py:109
  170.3 10.2 %copy-start.1 = (f32[128,128]{0,1:T(8,128)S(1)}, f32[128,128]{0,1:T(8,128)}, u32[]{:S(2)}) copy-start(f32[128,128]{0,1:T(8,128)} %fusion.21) | copy-start | bytes 196612
  175.6 4.9 %copy-start.2 = (f32[128,128]{1,0:T(8,128)S(1)}, f32[128,128]{1,0:T(8,128)}, u32[]{:S(2)}) copy-start(f32[128,128]{1,0:T(8,128)} %fusion.41) | copy-start | bytes 196612
  177.7 16.3 %copy-start.5 = (f32[512]{0:T(512)S(1)}, f32[512]{0:T(512)}, u32[]{:S(2)}) copy-start(f32[512]{0:T(512)} %param.12) | copy-start | bytes 6148
  177.7 9.7 %collective-permute-start.3 = (f32[128,512]{1,0:T(8,128)}, f32[128,512]{1,0:T(8,128)S(1)}, u32[]{:S(2)}, u32[]{:S(2)}) collective-permute-start(f32[128,512]{1,0:T(8,128)} %fusion.2), channel_id=1, source_target_pairs={{0,64},{64,128},{128,192},{192,0},{1,65},{65,129},{129,193},{193,1... | collective-permute-start | bytes 786440 | tf_op jit(solution)/shard_map/ppermute | solution.py:44
  178.1 14.3 %collective-permute-start.4 = (f32[128,512]{1,0:T(8,128)}, f32[128,512]{1,0:T(8,128)S(1)}, u32[]{:S(2)}, u32[]{:S(2)}) collective-permute-start(f32[128,512]{1,0:T(8,128)} %fusion.2), channel_id=1, source_target_pairs={{0,128},{64,192},{128,0},{192,64},{1,129},{65,193},{129,1},{193,65... | collective-permute-start | bytes 786440 | tf_op jit(solution)/shard_map/ppermute | solution.py:44
  180.1 13.0 %collective-permute-start.5 = (f32[128,512]{1,0:T(8,128)}, f32[128,512]{1,0:T(8,128)S(1)}, u32[]{:S(2)}, u32[]{:S(2)}) collective-permute-start(f32[128,512]{1,0:T(8,128)} %fusion.2), channel_id=1, source_target_pairs={{0,192},{64,0},{128,64},{192,128},{1,193},{65,1},{129,65},{193,129... | collective-permute-start | bytes 786440 | tf_op jit(solution)/shard_map/ppermute | solution.py:44
  194.6 1.1 copy-start.3

commit v4 on v2

--- a/solution.py
+++ b/solution.py
@@ -111,19 +111,40 @@
     square = square + jnp.where(
         diag[None, :] == jnp.arange(panel_cols, dtype=jnp.int32)[:, None], prior_weight[None, :half], 0.0
     )
-    owned = obs_butterfly(owned)
+    n_obs_dev = lax.axis_size("obs")
+    me = lax.axis_index("obs")
+    rows = bw // n_obs_dev
+    my_block = jnp.sum(jnp.where(block_owner == my_j, block_range, 0))
+    col_index = jnp.arange(panel_cols, dtype=jnp.int32)
 
-    my_block = jnp.sum(jnp.where(block_owner == my_j, block_range, 0))
-    row_index = my_block * bw + jnp.arange(bw, dtype=jnp.int32)
-    col_index = jnp.arange(panel_cols, dtype=jnp.int32)
-    owned = owned + jnp.where(col_index[None, :] == row_index[:, None], prior_weight[None, :], 0.0)
+    pieces = owned.reshape(n_obs_dev, rows, panel_cols)
+    got = [pieces[me]] + [
+        lax.ppermute(pieces[(me + s) % n_obs_dev], "obs", [(i, (i + s) % n_obs_dev) for i in range(n_obs_dev)])
+        for s in range(1, n_obs_dev)
+    ]
+    ordered = jnp.stack(got)
+    parts = [ordered[(me - src) % n_obs_dev] for src in range(n_obs_dev)]
+    while len(parts) > 1:
+        parts = [parts[i] + parts[i + 1] for i in range(0, len(parts), 2)]
+    slab = parts[0]
+    row_index = my_block * bw + me * rows + jnp.arange(rows, dtype=jnp.int32)
+    slab = slab + jnp.where(col_index[None, :] == row_index[:, None], prior_weight[None, :], 0.0)
 
     inverse = factor_inverse(0.5 * (square[:half] + square[:half].T))
     coupling = jnp.dot(square[half:], inverse.T, precision=HI, preferred_element_type=jnp.float32)
-    first_rows = jnp.dot(owned[:, :half], inverse.T, precision=HI, preferred_element_type=jnp.float32)
-    update_rows = owned[:, half:] - jnp.dot(
-        first_rows, coupling.T, precision=HI, preferred_element_type=jnp.float32
+    first_slab = jnp.dot(slab[:, :half], inverse.T, precision=HI, preferred_element_type=jnp.float32)
+    update_slab = slab[:, half:] - jnp.dot(
+        first_slab, coupling.T, precision=HI, preferred_element_type=jnp.float32
     )
+    done = jnp.concatenate([first_slab, update_slab], axis=1)
+    spread = [done] + [
+        lax.ppermute(done, "obs", [(i, (i + s) % n_obs_dev) for i in range(n_obs_dev)])
+        for s in range(1, n_obs_dev)
+    ]
+    ordered = jnp.stack(spread)
+    full = jnp.concatenate([ordered[(me - src) % n_obs_dev] for src in range(n_obs_dev)], axis=0)
+    first_rows = full[:, :half]
+    update_rows = full[:, half:]
     return (first_rows, update_rows)
 
 

time: 193 us -> 191 us (0.990)
  waiting for transfers between devices: 63.1 us -> 55 us
  starting transfers between devices: 36 us -> 41.4 us
    ppermute x4 -> x2, waiting for transfers between devices: 13 us -> 1.08 us  [obs_butterfly(): x = x + lax.ppermute(x, 'obs', perm)]
    ppermute x0 -> x6, starting transfers between devices: none -> 8.93 us  [the longest x3 4.77 us: local(): lax.ppermute(pieces[(me + s) % n_obs_dev], 'obs', [(i, (i + s) % n_obs_de...]
    ppermute x0 -> x6, waiting for transfers between devices: none -> 4.72 us  [the longest x3 2.93 us: local(): lax.ppermute(done, 'obs', [(i, (i + s) % n_obs_dev) for i in range(n_obs_...]
    ppermute x4 -> x2, starting transfers between devices: 7.53 us -> 4.09 us  [obs_butterfly(): x = x + lax.ppermute(x, 'obs', perm)]
  transfers between devices with their start and end apart: 7 -> 11, of which waited for: 6 -> 8; matrix products, arithmetic and copies ran while one was open for 40% -> 40% of each run, Pallas kernels for 0% -> 0%
where the time goes in v4:
time: 191 us; the launch traced here: 190 us
  other arithmetic  61.7 us (32%)
  waiting for transfers between devices  55 us (29%)
  starting transfers between devices  41.4 us (22%)
  local copies, waits for them, and re-layouts  22.9 us (12%)
  matrix products  6.83 us (4%)
  between operations  1.96 us (1%)
    all_to_all x1, waiting for transfers between devices, local(): lax.all_to_all(jnp.concatenate([spread] + routed(0, FIRST), axis=2), 'blk...  42 us
    all_to_all x1, starting transfers between devices, local(): lax.all_to_all(gram.reshape(nb, gram_rows, half), 'blk', 0, 0, tiled=True)  13 us
    another operation x3, other arithmetic, factor_inverse(): high = jnp.linalg.cholesky(mirrored[n:, n:] - dot(left, left.T))  12.4 us
    another operation x3, other arithmetic, factor_inverse(): low = jnp.linalg.cholesky(mirrored[:n, :n])  12.4 us
    another operation x2, other arithmetic, factor_inverse(): high_inv = jax.scipy.linalg.solve_triangular(high, eye, lower=True)  10.7 us
    another operation x2, other arithmetic, factor_inverse(): low_inv = jax.scipy.linalg.solve_triangular(low, eye, lower=True)  10.5 us
    all_to_all x1, starting transfers between devices, local(): lax.all_to_all(jnp.concatenate([spread] + routed(0, FIRST), axis=2), 'blk...  9.26 us
    all_to_all x1, starting transfers between devices, local(): lax.all_to_all(jnp.concatenate(routed(FIRST, CAP), axis=2), 'blk', 0, 0,...  6.19 us
  transfers between devices with their start and end apart: 11, of which 8 were waited for; matrix products, arithmetic and copies ran while one was open for 40% of the time, Pallas kernels for 0%

profile of v4, /device:TPU:1, one launch (start us, length us, event | category | flops | bytes accessed | tf_op | source)
XLA Modules:
  0.0 189.8 jit_solution(18054136832543434844)
XLA Ops:
  0.6 1.0 slice_bitcast_fusion.12
  1.6 3.5 %fusion.41 = (f32[128,1,128]{2,1,0:T(1,128)S(1)}, f32[128,1,128]{2,1,0:T(1,128)S(1)}, f32[128,1,128]{2,1,0:T(1,128)S(1)}, f32[128,1,128]{2,1,0:T(1,128)S(1)}, f3...) fusion(f32[128,8,128]{2,1,0:T(8,128)} %param.8), kind=kLoop, calls=%fused_computation.117 | loop fusion | bytes 1048576 | tf_op jit(solution)/shard_map/slice | solution.py:37
  5.6 1.4 add_add_fusion
  7.3 1.4 fusion.13
  8.7 13.0 %all-to-all-start = ((f32[64,8,256]{2,1,0:T(8,128)}), f32[64,8,256]{2,1,0:T(8,128)S(1)}, u32[]{:S(2)}, u32[]{:S(2)}) async-start(f32[64,8,256]{2,1,0:T(8,128)} %fusion.13), calls=%async_computation | async-start | bytes 1048576 | tf_op jit(solution)/shard_map/all_to_all | solution.py:94
  22.3 1.2 convert_reduce_fusion
  23.6 4.9 %gather_fusion.2 = f32[1536,512]{1,0:T(8,128)} fusion(f32[128,512]{1,0:T(8,128)S(1)} %broadcast_multiply_fusion, s32[2048]{0:T(1024)S(1)} %pad_clamp_fusion.1), kind=kCustom, calls=%fused_computation.2 | custom fusion | bytes 6297600 | tf_op jit(solution)/shard_map/gather | solution.py:88
  28.6 2.6 %gather_fusion = s32[1536,8]{1,0:T(8,128)S(1)} fusion(s32[128,8]{1,0:T(8,128)S(1)} %copy.26, s32[2048]{0:T(1024)S(1)} %pad_clamp_fusion.1), kind=kCustom, calls=%fused_computation | custom fusion | bytes 104448 | tf_op jit(solution)/shard_map/gather | solution.py:76
  31.2 1.2 select_reduce_fusion
  32.5 3.9 %broadcast_select_fusion = f32[64,24,512]{2,1,0:T(8,128)} fusion(f32[64,24,512]{2,1,0:T(8,128)} %bitcast.123, pred[64,24]{1,0:T(8,128)(4,1)S(1)} %iota_compare_fusion.19), kind=kLoop, calls=%fused_computation.7 | loop fusion | flops 786432 | bytes 6292992 | tf_op jit(solution)/shard_map/jit(_where)/select_n | solution.py:90
  36.4 2.5 %all-to-all-done = f32[64,8,256]{2,1,0:T(8,128)S(1)} async-done(((f32[64,8,256]{2,1,0:T(8,128)}), f32[64,8,256]{2,1,0:T(8,128)S(1)}, u32[]{:S(2)}, u32[]{:S(2)}) %all-to-all-start) | async-done | bytes 524320 | tf_op jit(solution)/shard_map/all_to_all | solution.py:94
  39.0 1.4 collective-permute-start
  40.4 2.6 %gather_fusion.1 = f32[1536,128]{1,0:T(8,128)S(1)} fusion(f32[1024,128]{1,0:T(8,128)S(1)} %bitcast.122, s32[2048]{0:T(1024)S(1)} %pad_clamp_fusion), kind=kCustom, calls=%fused_computation.1 | custom fusion | bytes 1579008 | tf_op jit(solution)/shard_map/gather | solution.py:82
  43.0 2.7 %collective-permute-start.1 = (f32[8,256]{1,0:T(8,128)S(1)}, f32[8,256]{1,0:T(8,128)S(1)}, u32[]{:S(2)}, u32[]{:S(2)}) collective-permute-start(f32[8,256]{1,0:T(8,128)S(1)} %add.197), channel_id=1, source_target_pairs={{0,128},{64,192},{128,0},{192,64},{1,129},{65,193},{129,1},{193,65... | collective-permute-start | bytes 24584 | tf_op jit(solution)/shard_map/ppermute | solution.py:46
  46.0 1.1 collective-permute-done.1
  47.2 1.4 pad_maximum_fusion.1
  48.5 9.3 %all-to-all-start.1 = ((f32[64,8,896]{2,1,0:T(8,128)}), f32[64,8,896]{2,1,0:T(8,128)S(1)}, u32[]{:S(2)}, u32[]{:S(2)}) async-start(f32[64,8,896]{2,1,0:T(8,128)} %pad_maximum_fusion.1), calls=%async_computation.1 | async-start | bytes 3670016 | tf_op jit(solution)/shard_map/all_to_all | solution.py:105
  57.8 1.5 slice-done.1
  59.4 1.8 pad_maximum_fusion
  61.1 42.0 %all-to-all-done.1 = f32[64,8,896]{2,1,0:T(8,128)S(1)} async-done(((f32[64,8,896]{2,1,0:T(8,128)}), f32[64,8,896]{2,1,0:T(8,128)S(1)}, u32[]{:S(2)}, u32[]{:S(2)}) %all-to-all-start.1) | async-done | bytes 1835040 | tf_op jit(solution)/shard_map/all_to_all | solution.py:105
  103.2 1.2 copy-done.1
  104.4 6.2 %all-to-all-start.2 = ((f32[64,16,640]{2,1,0:T(8,128)}), f32[64,16,640]{2,1,0:T(8,128)S(1)}, u32[]{:S(2)}, u32[]{:S(2)}) async-start(f32[64,16,640]{2,1,0:T(8,128)} %pad_maximum_fusion), calls=%async_computation.2 | async-start | bytes 5242880 | tf_op jit(solution)/shard_map/all_to_all | solution.py:108
  112.0 1.1 fusion.7
  113.2 0.9 copy.27
  114.0 1.0 fusion.12
  115.1 11.7 %cholesky.44 = f32[128,128]{1,0:T(8,128)S(1)} custom-call(f32[128,128]{1,0:T(8,128)S(1)} %fusion.31), custom_call_target="Cholesky" | custom-call | tf_op jit(solution)/shard_map/jit(cholesky)/cholesky | solution.py:18
  127.5 0.7 fusion.24
  128.2 9.8 %custom-call.6 = f32[1,128,128]{1,2,0:T(8,128)S(1)} custom-call(f32[1,128,128]{2,1,0:T(8,128)S(1)} %fusion.24), custom_call_target="InvertDiagBlocksLowerTriangular" | custom-call | tf_op jit(solution)/shard_map/jit(_solve_triangular)/triangular_solve | solution.py:19
  138.6 0.9 convolution_subtract_fusion
  139.5 0.9 copy.30
  140.4 0.9 fusion.29
  141.3 11.7 %cholesky.55 = f32[128,128]{1,0:T(8,128)S(1)} custom-call(f32[128,128]{1,0:T(8,128)S(1)} %fusion.29), custom_call_target="Cholesky" | custom-call | tf_op jit(solution)/shard_map/jit(cholesky)/cholesky | solution.py:21
  154.3 10.0 %custom-call.7 = f32[1,128,128]{1,2,0:T(8,128)S(1)} custom-call(f32[1,128,128]{2,1,0:T(8,128)S(1)} %fusion.25), custom_call_target="InvertDiagBlocksLowerTriangular" | custom-call | tf_op jit(solution)/shard_map/jit(_solve_triangular)/triangular_solve | solution.py:22
  164.6 0.7 copy.32
  165.8 1.4 slice_bitcast_fusion
  167.2 0.8 fusion.5
  168.0 4.6 %all-to-all-done.2 = f32[64,16,640]{2,1,0:T(8,128)S(1)} async-done(((f32[64,16,640]{2,1,0:T(8,128)}), f32[64,16,640]{2,1,0:T(8,128)S(1)}, u32[]{:S(2)}, u32[]{:S(2)}) %all-to-all-start.2) | async-done | bytes 2621472 | tf_op jit(solution)/shard_map/all_to_all | solution.py:108
  172.7 1.4 fusion.2
  174.1 0.7 collective-permute-start.2
  174.8 2.6 %collective-permute-start.3 = (f32[32,512]{1,0:T(8,128)S(1)}, f32[32,512]{1,0:T(8,128)S(1)}, u32[]{:S(2)}, u32[]{:S(2)}) collective-permute-start(f32[32,512]{1,0:T(8,128)S(1)} %get-tuple-element.20), channel_id=1, source_target_pairs={{0,128},{64,192},{128,0},{192,64},{1,129},{65,193},{129,1},{193,65... | collective-permute-start | bytes 196616 | tf_op jit(solution)/shard_map/ppermute | solution.py:122
  177.4 1.4 collective-permute-start.4
  179.3 1.8 collective-permute-done.3
  181.9 0.8 collective-permute-start.5
  182.7 2.6 %collective-permute-start.6 = (f32[32,512]{1,0:T(8,128)S(1)}, f32[32,512]{1,0:T(8,128)S(1)}, u32[]{:S(2)}, u32[]{:S(2)}) collective-permute-start(f32[32,512]{1,0:T(8,128)S(1)} %get-tuple-element.23), channel_id=1, source_target_pairs={{0,128},{64,192},{128,0},{192,64},{1,129},{65,193},{129,1},{193,65... | collective-permute-start | bytes 196616 | tf_op jit(solution)/shard_map/ppermute | solution.py:141
  185.3 0.8 collective-permute-start.7
  186.3 1.4 collective-permute-done.6
  187.7 1.3 collective-permute-done.7
  189.1 0.7 fusion.42
  (77 shorter events, 7.7 us)
Async XLA Ops:
  0.6 6.4 %copy-start.5 = (f32[128]{0:T(128)S(1)}, f32[128]{0:T(128)}, u32[]{:S(2)}) copy-start(f32[128]{0:T(128)} %param.10) | copy-start | bytes 1540
  7.0 14.7 %copy-start.3 = (s32[128,8]{0,1:T(8,128)S(1)}, s32[128,8]{0,1:T(8,128)}, u32[]{:S(2)}) copy-start(s32[128,8]{0,1:T(8,128)} %param.9) | copy-start | bytes 12292
  7.0 14.7 %copy-start.6 = (s32[64]{0:T(128)S(1)}, s32[64]{0:T(128)}, u32[]{:S(2)}) copy-start(s32[64]{0:T(128)} %param.11) | copy-start | bytes 772
  8.7 30.3 %all-to-all-start = ((f32[64,8,256]{2,1,0:T(8,128)}), f32[64,8,256]{2,1,0:T(8,128)S(1)}, u32[]{:S(2)}, u32[]{:S(2)}) async-start(f32[64,8,256]{2,1,0:T(8,128)} %fusion.13), calls=%async_computation | async-start | bytes 1048576 | tf_op jit(solution)/shard_map/all_to_all | solution.py:94
  32.5 7.9 %copy-start = (f32[128,8,128]{2,1,0:T(8,128)S(1)}, f32[128,8,128]{2,1,0:T(8,128)}, u32[]{:S(2)}) copy-start(f32[128,8,128]{2,1,0:T(8,128)} %param.8) | copy-start | bytes 1572868
  39.0 4.0 %collective-permute-start = (f32[8,256]{1,0:T(8,128)S(1)}, f32[8,256]{1,0:T(8,128)S(1)}, u32[]{:S(2)}, u32[]{:S(2)}) collective-permute-start(f32[8,256]{1,0:T(8,128)S(1)} %reduce_sum.56), channel_id=1, source_target_pairs={{0,64},{64,0},{128,192},{192,128},{1,65},{65,1},{129,193},{193,129... | collective-permute-start | bytes 24584 | tf_op jit(solution)/shard_map/ppermute | solution.py:46
  43.0 4.1 %collective-permute-start.1 = (f32[8,256]{1,0:T(8,128)S(1)}, f32[8,256]{1,0:T(8,128)S(1)}, u32[]{:S(2)}, u32[]{:S(2)}) collective-permute-start(f32[8,256]{1,0:T(8,128)S(1)} %add.197), channel_id=1, source_target_pairs={{0,128},{64,192},{128,0},{192,64},{1,129},{65,193},{129,1},{193,65... | collective-permute-start | bytes 24584 | tf_op jit(solution)/shard_map/ppermute | solution.py:46
  45.7 1.4 slice-start
  48.5 54.7 %all-to-all-start.1 = ((f32[64,8,896]{2,1,0:T(8,128)}), f32[64,8,896]{2,1,0:T(8,128)S(1)}, u32[]{:S(2)}, u32[]{:S(2)}) async-start(f32[64,8,896]{2,1,0:T(8,128)} %pad_maximum_fusion.1), calls=%async_computation.1 | async-start | bytes 3670016 | tf_op jit(solution)/shard_map/all_to_all | solution.py:105
  57.8 1.6 slice-start.1
  61.1 50.9 %slice-start.2 = ((f32[512]{0:T(512)}), f32[256]{0:T(256)S(1)}, s32[]{:S(2)}) async-start(f32[512]{0:T(512)} %param.12), calls=%async_computation.5 | async-start | bytes 2048 | tf_op jit(solution)/shard_map/slice | solution.py:112
  103.2 1.2 copy-start.1
  104.4 68.2 %all-to-all-start.2 = ((f32[64,16,640]{2,1,0:T(8,128)}), f32[64,16,640]{2,1,0:T(8,128)S(1)}, u32[]{:S(2)}, u32[]{:S(2)}) async-start(f32[64,16,640]{2,1,0:T(8,128)} %pad_maximum_fusion), calls=%async_computation.2 | async-start | bytes 5242880 | tf_op jit(solution)/shard_map/all_to_all | solution.py:108
  172.7 6.2 %copy-start.2 = (f32[128,128]{1,0:T(8,128)S(1)}, f32[128,128]{1,0:T(8,128)}, u32[]{:S(2)}) copy-start(f32[128,128]{1,0:T(8,128)} %copy.32) | copy-start | bytes 196612
  172.7 8.4 %copy-start.4 = (f32[512]{0:T(512)S(1)}, f32[512]{0:T(512)}, u32[]{:S(2)}) copy-start(f32[512]{0:T(512)} %param.12) | copy-start | bytes 6148
  174.1 5.2 %collective-permute-start.2 = (f32[32,512]{1,0:T(8,128)S(1)}, f32[32,512]{1,0:T(8,128)S(1)}, u32[]{:S(2)}, u32[]{:S(2)}) collective-permute-start(f32[32,512]{1,0:T(8,128)S(1)} %get-tuple-element.21), channel_id=1, source_target_pairs={{0,64},{64,128},{128,192},{192,0},{1,65},{65,129},{129,193},{193,1... | collective-permute-start | bytes 196616 | tf_op jit(solution)/shard_map/ppermute | solution.py:122
  174.8 6.3 %collective-permute-start.3 = (f32[32,512]{1,0:T(8,128)S(1)}, f32[32,512]{1,0:T(8,128)S(1)}, u32[]{:S(2)}, u32[]{:S(2)}) collective-permute-start(f32[32,512]{1,0:T(8,128)S(1)} %get-tuple-element.20), channel_id=1, source_target_pairs={{0,128},{64,192},{128,0},{192,64},{1,129},{65,193},{129,1},{193,65... | collective-permute-start | bytes 196616 | tf_op jit(solution)/shard_map/ppermute | solution.py:122
  177.4 3.6 %collective-permute-start.4 = (f32[32,512]{1,0:T(8,128)S(1)}, f32[32,512]{1,0:T(8,128)S(1)}, u32[]{:S(2)}, u32[]{:S(2)}) collective-permute-start(f32[32,512]{1,0:T(8,128)S(1)} %get-tuple-element.19), channel_id=1, source_target_pairs={{0,192},{64,0},{128,64},{192,128},{1,193},{65,1},{129,65},{193,129... | collective-permute-start | bytes 196616 | tf_op jit(solution)/shard_map/ppermute | solution.py:122
  181.9 4.4 %collective-permute-start.5 = (f32[32,512]{1,0:T(8,128)S(1)}, f32[32,512]{1,0:T(8,128)S(1)}, u32[]{:S(2)}, u32[]{:S(2)}) collective-permute-start(f32[32,512]{1,0:T(8,128)S(1)} %get-tuple-element.23), channel_id=1, source_target_pairs={{0,64},{64,128},{128,192},{192,0},{1,65},{65,129},{129,193},{193,1... | collective-permute-start | bytes 196616 | tf_op jit(solution)/shard_map/ppermute | solution.py:141
  182.7 5.0 %collective-permute-start.6 = (f32[32,512]{1,0:T(8,128)S(1)}, f32[32,512]{1,0:T(8,128)S(1)}, u32[]{:S(2)}, u32[]{:S(2)}) collective-permute-start(f32[32,512]{1,0:T(8,128)S(1)} %get-tuple-element.23), channel_id=1, source_target_pairs={{0,128},{64,192},{128,0},{192,64},{1,129},{65,193},{129,1},{193,65... | collective-permute-start | bytes 196616 | tf_op jit(solution)/shard_map/ppermute | solution.py:141
  185.3 3.7 %collective-permute-start.7 = (f32[32,512]{1,0:T(8,128)S(1)}, f32[32,512]{1,0:T(8,128)S(1)}, u32[]{:S(2)}, u32[]{:S(2)}) collective-permute-start(f32[32,512]{1,0:T(8,128)S(1)} %get-tuple-element.23), channel_id=1, source_target_pairs={{0,192},{64,0},{128,64},{192,128},{1,193},{65,1},{129,65},{193,129... | collective-permute-start | bytes 196616 | tf_op jit(solution)/shard_map/ppermute | solution.py:141

commit v5 on v4

--- a/solution.py
+++ b/solution.py
@@ -48,6 +48,15 @@
     return x
 
 
+def ranked(labels, wanted):
+    hit = jnp.sum((labels[:, :, None] == wanted[None, None, :]).astype(jnp.int32), axis=1)
+    cum = jnp.cumsum(hit, axis=0)
+    rank_range = jnp.arange(CAP, dtype=jnp.int32)
+    sel = jnp.sum((cum[:, :, None] <= rank_range[None, None, :]).astype(jnp.int32), axis=0)
+    valid = rank_range[None, :] < cum[-1][:, None]
+    return jnp.minimum(sel, labels.shape[0] - 1), valid
+
+
 def local(design_tiles, block_ids, obs_weight, block_owner, prior_weight):
     n_obs, touched, bw = design_tiles.shape
     nblk = block_owner.shape[0]
@@ -95,26 +104,42 @@
     gram_part = obs_butterfly(jnp.sum(got_gram, axis=0))
     spread = jnp.broadcast_to(gram_part[None], (nb, gram_rows, half))
 
-    def routed(lo, hi):
-        return [tile_rows[:, lo:hi], panel_rows[:, lo:hi]]
+    panel_range = jnp.arange(panel_blocks, dtype=jnp.int32)
+    panel_sel, panel_valid = ranked(block_ids, panel_range)
+    panel_tiles = weighted.reshape(n_obs, panel_blocks, bw)[panel_sel, panel_range[:, None]]
+    panel_tiles = jnp.where(panel_valid[:, :, None], panel_tiles, 0.0)
+    shared = lax.all_gather(panel_tiles.reshape(-1, bw), "blk", axis=0, tiled=False)
 
-    def owned_part(got):
-        got = got.reshape(-1, bw + panel_cols)
-        return jnp.einsum("si,sp->ip", got[:, :bw], got[:, bw:], precision=HI)
-
-    mixed = lax.all_to_all(jnp.concatenate([spread] + routed(0, FIRST), axis=2), "blk", 0, 0, tiled=True)
-    square = mixed[:, :, :half].reshape(panel_cols, half)
-    owned = owned_part(mixed[:, :, half:])
-    rest = lax.all_to_all(jnp.concatenate(routed(FIRST, CAP), axis=2), "blk", 0, 0, tiled=True)
-    owned = owned + owned_part(rest)
+    panel_hit = jnp.sum((block_ids[:, :, None] == panel_range[None, None, :]).astype(jnp.int32), axis=1)
+    panel_pos = jnp.where(panel_hit > 0, jnp.cumsum(panel_hit, axis=0) - 1, CAP)
+    slot_pos = jnp.where(valid[:, :, None], panel_pos[obs_sel], CAP).astype(jnp.float32)
+    index_width = CAP * panel_blocks // gram_rows
+    payload = jnp.concatenate(
+        [
+            spread,
+            tile_rows.reshape(nb, gram_rows, -1),
+            slot_pos.reshape(nb, gram_rows, index_width),
+        ],
+        axis=2,
+    )
+    got = lax.all_to_all(payload, "blk", 0, 0, tiled=True)
+    square = got[:, :, :half].reshape(panel_cols, half)
+    got_tiles = got[:, :, half : half + CAP * bw // gram_rows].reshape(nb * CAP, bw)
+    got_pos = got[:, :, half + CAP * bw // gram_rows :].reshape(nb, CAP, panel_blocks).astype(jnp.int32)
     diag = jnp.arange(half, dtype=jnp.int32)
     square = square + jnp.where(
         diag[None, :] == jnp.arange(panel_cols, dtype=jnp.int32)[:, None], prior_weight[None, :half], 0.0
     )
+
+    src_panel = shared.reshape(nb, panel_blocks, CAP, bw)
+    match = (got_pos[:, :, :, None] == jnp.arange(CAP, dtype=jnp.int32)[None, None, None, :]).astype(jnp.float32)
+    slot_panel = jnp.einsum("srpq,spqc->srpc", match, src_panel, precision=HI)
+    owned = jnp.einsum("si,sp->ip", got_tiles, slot_panel.reshape(nb * CAP, panel_cols), precision=HI)
+    my_block = jnp.sum(jnp.where(block_owner == my_j, block_range, 0))
+
     n_obs_dev = lax.axis_size("obs")
     me = lax.axis_index("obs")
     rows = bw // n_obs_dev
-    my_block = jnp.sum(jnp.where(block_owner == my_j, block_range, 0))
     col_index = jnp.arange(panel_cols, dtype=jnp.int32)
 
     pieces = owned.reshape(n_obs_dev, rows, panel_cols)

time: 191 us -> 199 us (1.042)
  between operations: 1.96 us -> 15.4 us
  starting transfers between devices: 41.4 us -> 29.8 us
  other arithmetic: 61.7 us -> 55.6 us
  matrix products: 6.83 us -> 12 us
  waiting for transfers between devices: 55 us -> 58.4 us
  local copies, waits for them, and re-layouts: 22.9 us -> 25.8 us
    all_to_all x2 -> x1, starting transfers between devices: 15.5 us -> 7.9 us  [local(): got = lax.all_to_all(payload, 'blk', 0, 0, tiled=True)]
    dot_general x2, matrix products: 2.13 us -> 7.94 us  [the longest x1 4.89 us: local(): slot_panel = jnp.einsum('srpq,spqc->srpc', match, src_panel, precision=HI)]
    all_to_all x2 -> x1, waiting for transfers between devices: 46.7 us -> 43.4 us  [local(): got = lax.all_to_all(payload, 'blk', 0, 0, tiled=True)]
    select_n x1 -> x2, other arithmetic: 3.91 us -> 0.71 us  [the longest x1 0.7 us: local(): panel_tiles = jnp.where(panel_valid[:, :, None], panel_tiles, 0.0)]
    all_to_all x1, waiting for transfers between devices: 2.49 us -> 5.66 us  [local(): lax.all_to_all(gram.reshape(nb, gram_rows, half), 'blk', 0, 0, tiled=True)]
    reshape x1 -> x2, local copies, waits for them, and re-layouts: 1.4 us -> 4.49 us  [the longest x1 3.31 us: local(): slot_panel.reshape(nb * CAP, panel_cols)]
    ppermute x3, starting transfers between devices: 4.17 us -> 1.57 us  [local(): lax.ppermute(done, 'obs', [(i, (i + s) % n_obs_dev) for i in range(n_obs_...]
    ppermute x3, waiting for transfers between devices: 1.79 us -> 4.33 us  [local(): lax.ppermute(pieces[(me + s) % n_obs_dev], 'obs', [(i, (i + s) % n_obs_de...]
  transfers between devices with their start and end apart: 11 -> 11, of which waited for: 8 -> 9; matrix products, arithmetic and copies ran while one was open for 40% -> 35% of each run, Pallas kernels for 0% -> 0%
where the time goes in v5:
time: 199 us; the launch traced here: 197 us
  waiting for transfers between devices  58.4 us (29%)
  other arithmetic  55.6 us (28%)
  starting transfers between devices  29.8 us (15%)
  local copies, waits for them, and re-layouts  25.8 us (13%)
  between operations  15.4 us (8%)
  matrix products  12 us (6%)
    all_to_all x1, waiting for transfers between devices, local(): got = lax.all_to_all(payload, 'blk', 0, 0, tiled=True)  43.4 us
    all_to_all x1, starting transfers between devices, local(): lax.all_to_all(gram.reshape(nb, gram_rows, half), 'blk', 0, 0, tiled=True)  13 us
    another operation x3, other arithmetic, factor_inverse(): low = jnp.linalg.cholesky(mirrored[:n, :n])  12.4 us
    another operation x3, other arithmetic, factor_inverse(): high = jnp.linalg.cholesky(mirrored[n:, n:] - dot(left, left.T))  12.4 us
    another operation x2, other arithmetic, factor_inverse(): high_inv = jax.scipy.linalg.solve_triangular(high, eye, lower=True)  10.6 us
    another operation x2, other arithmetic, factor_inverse(): low_inv = jax.scipy.linalg.solve_triangular(low, eye, lower=True)  10.5 us
    all_to_all x1, starting transfers between devices, local(): got = lax.all_to_all(payload, 'blk', 0, 0, tiled=True)  7.9 us
    all_to_all x1, waiting for transfers between devices, local(): lax.all_to_all(gram.reshape(nb, gram_rows, half), 'blk', 0, 0, tiled=True)  5.66 us
  transfers between devices with their start and end apart: 11, of which 9 were waited for; matrix products, arithmetic and copies ran while one was open for 35% of the time, Pallas kernels for 0%

profile of v5, /device:TPU:1, one launch (start us, length us, event | category | flops | bytes accessed | tf_op | source)
XLA Modules:
  0.0 197.1 jit_solution(14971848168315060994)
XLA Ops:
  7.2 3.3 %fusion.38 = (f32[128,1,128]{2,1,0:T(1,128)S(1)}, f32[128,1,128]{2,1,0:T(1,128)S(1)}, f32[128,1,128]{2,1,0:T(1,128)S(1)}, f32[128,1,128]{2,1,0:T(1,128)S(1)}, f3...) fusion(f32[128,8,128]{2,1,0:T(8,128)} %param.8), kind=kLoop, calls=%fused_computation.126 | loop fusion | bytes 1048576 | tf_op jit(solution)/shard_map/slice | solution.py:37
  10.5 1.0 slice_bitcast_fusion.12
  12.0 2.3 %broadcast_multiply_fusion = (f32[128,4,128]{2,1,0:T(4,128)S(1)}, f32[128,4,128]{2,1,0:T(4,128)S(1)}) fusion(f32[128]{0:T(128)} %param.10, f32[128,128]{1,0:T(8,128)S(1)} %bitcast.153, pred[128,4]{1,0:T(8,128)(4,1)S(1)} %get-tuple-element.34, f32[128,128]{1,0:T(8,128)S(1)} %bitcast.147, pred[128,4]{1,0:T(8,128)(4,1)S(1)} %get-tuple-element.35, ...), kind=kLoop, calls=%fused_computation.44 | loop fusion | flops 1048576 | bytes 1053184 | tf_op jit(solution)/shard_map/mul | solution.py:96
  14.2 0.7 multiply_bitcast_fusion
  15.1 1.4 fusion.7
  16.5 13.0 %all-to-all-start = ((f32[64,8,256]{2,1,0:T(8,128)}), f32[64,8,256]{2,1,0:T(8,128)S(1)}, u32[]{:S(2)}, u32[]{:S(2)}) async-start(f32[64,8,256]{2,1,0:T(8,128)} %fusion.7), calls=%async_computation | async-start | bytes 1048576 | tf_op jit(solution)/shard_map/all_to_all | solution.py:103
  30.3 1.2 gather_fusion.3
  31.6 0.7 bitcast_select_fusion
  32.9 1.2 convert_reduce_fusion
  34.2 2.6 %gather_fusion = s32[1536,8]{1,0:T(8,128)S(1)} fusion(s32[128,8]{1,0:T(8,128)S(1)} %copy.93, s32[2048]{0:T(1024)S(1)} %pad_clamp_fusion.1), kind=kCustom, calls=%fused_computation | custom fusion | bytes 104448 | tf_op jit(solution)/shard_map/gather | solution.py:85
  36.8 1.2 select_reduce_fusion
  38.2 2.6 %gather_fusion.1 = f32[1536,128]{1,0:T(8,128)S(1)} fusion(f32[1024,128]{1,0:T(8,128)S(1)} %bitcast.136, s32[2048]{0:T(1024)S(1)} %pad_clamp_fusion), kind=kCustom, calls=%fused_computation.1 | custom fusion | bytes 1579008 | tf_op jit(solution)/shard_map/gather | solution.py:91
  41.1 5.7 %all-to-all-done = f32[64,8,256]{2,1,0:T(8,128)S(1)} async-done(((f32[64,8,256]{2,1,0:T(8,128)}), f32[64,8,256]{2,1,0:T(8,128)S(1)}, u32[]{:S(2)}, u32[]{:S(2)}) %all-to-all-start) | async-done | bytes 524320 | tf_op jit(solution)/shard_map/all_to_all | solution.py:103
  46.8 1.4 collective-permute-start
  48.3 2.6 %gather_fusion.2 = s32[1536,4]{1,0:T(8,128)S(1)} fusion(s32[128,4]{1,0:T(8,128)S(1)} %copy.96, s32[2048]{0:T(1024)S(1)} %pad_clamp_fusion.1), kind=kCustom, calls=%fused_computation.2 | custom fusion | bytes 55296 | tf_op jit(solution)/shard_map/gather | solution.py:115
  51.3 2.7 %collective-permute-start.1 = (f32[8,256]{1,0:T(8,128)S(1)}, f32[8,256]{1,0:T(8,128)S(1)}, u32[]{:S(2)}, u32[]{:S(2)}) collective-permute-start(f32[8,256]{1,0:T(8,128)S(1)} %add.224), channel_id=1, source_target_pairs={{0,128},{64,192},{128,0},{192,64},{1,129},{65,193},{129,1},{193,65... | collective-permute-start | bytes 24584 | tf_op jit(solution)/shard_map/ppermute | solution.py:46
  54.4 1.0 collective-permute-done.1
  55.4 1.3 pad_maximum_fusion
  56.7 7.9 %all-to-all-start.1 = ((f32[64,8,652]{2,1,0:T(8,128)}), f32[64,8,652]{2,1,0:T(8,128)S(1)}, u32[]{:S(2)}, u32[]{:S(2)}) async-start(f32[64,8,652]{2,1,0:T(8,128)} %pad_maximum_fusion), calls=%async_computation.1 | async-start | bytes 3145728 | tf_op jit(solution)/shard_map/all_to_all | solution.py:125
  64.7 0.6 fusion.30
  66.0 43.4 %all-to-all-done.1 = f32[64,8,652]{2,1,0:T(8,128)S(1)} async-done(((f32[64,8,652]{2,1,0:T(8,128)}), f32[64,8,652]{2,1,0:T(8,128)S(1)}, u32[]{:S(2)}, u32[]{:S(2)}) %all-to-all-start.1) | async-done | bytes 1335328 | tf_op jit(solution)/shard_map/all_to_all | solution.py:125
  109.8 11.7 %cholesky.44 = f32[128,128]{1,0:T(8,128)S(1)} custom-call(f32[128,128]{1,0:T(8,128)S(1)} %fusion.25), custom_call_target="Cholesky" | custom-call | tf_op jit(solution)/shard_map/jit(cholesky)/cholesky | solution.py:18
  121.5 0.6 compare_reduce_fusion.1
  122.2 0.7 fusion.18
  122.9 9.8 %custom-call.8 = f32[1,128,128]{1,2,0:T(8,128)S(1)} custom-call(f32[1,128,128]{2,1,0:T(8,128)S(1)} %fusion.18), custom_call_target="InvertDiagBlocksLowerTriangular" | custom-call | tf_op jit(solution)/shard_map/jit(_solve_triangular)/triangular_solve | solution.py:19
  133.6 11.7 %cholesky.55 = f32[128,128]{1,0:T(8,128)S(1)} custom-call(f32[128,128]{1,0:T(8,128)S(1)} %fusion.23), custom_call_target="Cholesky" | custom-call | tf_op jit(solution)/shard_map/jit(cholesky)/cholesky | solution.py:21
  145.4 0.6 compare_reduce_fusion
  146.0 0.7 fusion.19
  146.7 10.0 %custom-call.9 = f32[1,128,128]{1,2,0:T(8,128)S(1)} custom-call(f32[1,128,128]{2,1,0:T(8,128)S(1)} %fusion.19), custom_call_target="InvertDiagBlocksLowerTriangular" | custom-call | tf_op jit(solution)/shard_map/jit(_solve_triangular)/triangular_solve | solution.py:22
  157.1 0.9 slice.171
  158.0 1.2 reshape.412
  159.2 1.1 copy.99
  161.2 4.9 %fusion.1 = f32[64,24,4,128]{3,1,2,0:T(8,128)S(1)} fusion(f32[64,4,24,128]{3,2,1,0:T(8,128)} %bitcast.141, s32[64,24,4]{1,2,0:T(4,128)S(1)} %copy.103), kind=kOutput, calls=%fused_computation.6 | convolution fusion | flops 226639872 | bytes 6316032 | tf_op jit(solution)/shard_map/srpq,spqc->srpc/dot_general | solution.py:136
  166.1 2.5 %copy.104 = f32[64,24,4,128]{3,2,1,0:T(4,128)} copy(f32[64,24,4,128]{3,1,2,0:T(8,128)S(1)} %fusion.1) | data formatting | bytes 6291456 | tf_op jit(solution)/shard_map/srpq,spqc->srpc/transpose | solution.py:136
  168.6 3.3 %reshape.455 = f32[1536,512,1]{1,0,2:T(8,128)S(1)} reshape(f32[64,24,4,128]{3,2,1,0:T(4,128)} %copy.104) | data formatting | bytes 6291456 | tf_op jit(solution)/shard_map/reshape | solution.py:137
  171.9 3.0 %fusion.40 = f32[4,32,512]{2,1,0:T(8,128)S(1)} fusion(f32[4,32,1536]{2,1,0:T(8,128)} %bitcast.137, f32[1536,512,1]{1,0,2:T(8,128)S(1)} %reshape.455), kind=kOutput, calls=%fused_computation.128 | convolution fusion | flops 1207959552 | bytes 4194304 | tf_op jit(solution)/shard_map/si,sp->ip/dot_general | solution.py:137
  175.0 1.7 collective-permute-start.4
  176.7 0.8 collective-permute-start.3
  177.5 0.8 collective-permute-start.2
  178.3 0.4 fusion.4
  178.9 2.4 %collective-permute-done.3 = f32[32,512]{1,0:T(8,128)S(1)} collective-permute-done((f32[32,512]{1,0:T(8,128)S(1)}, f32[32,512]{1,0:T(8,128)S(1)}, u32[]{:S(2)}, u32[]{:S(2)}) %collective-permute-start.3) | collective-permute-done | bytes 65568 | tf_op jit(solution)/shard_map/ppermute | solution.py:147
  181.3 1.7 collective-permute-done.2
  183.9 1.0 collective-permute-start.6
  185.0 0.5 collective-permute-start.5
  185.4 1.6 collective-permute-done.7
  187.1 1.6 collective-permute-done.6
  188.7 0.8 collective-permute-done.5
  189.5 0.7 fusion.39
  (97 shorter events, 7.3 us)
Async XLA Ops:
  7.2 22.4 %copy-start.3 = (s32[128,8]{0,1:T(8,128)S(1)}, s32[128,8]{0,1:T(8,128)}, u32[]{:S(2)}) copy-start(s32[128,8]{0,1:T(8,128)} %param.9) | copy-start | bytes 12292
  10.5 21.8 %copy-start.5 = (s32[64]{0:T(128)S(1)}, s32[64]{0:T(128)}, u32[]{:S(2)}) copy-start(s32[64]{0:T(128)} %param.11) | copy-start | bytes 772
  16.5 30.3 %all-to-all-start = ((f32[64,8,256]{2,1,0:T(8,128)}), f32[64,8,256]{2,1,0:T(8,128)S(1)}, u32[]{:S(2)}, u32[]{:S(2)}) async-start(f32[64,8,256]{2,1,0:T(8,128)} %fusion.7), calls=%async_computation | async-start | bytes 1048576 | tf_op jit(solution)/shard_map/all_to_all | solution.py:103
  29.5 131.8 %all-gather.2.cloned.1.call-start = ((), (), s32[]{:S(2)}) async-start(), calls=%async_computation.2 | async-start | bytes 3194880 | tf_op jit(solution)/shard_map/all_gather | solution.py:111
  34.2 4.0 %copy-start = (f32[128,8,128]{2,1,0:T(8,128)S(1)}, f32[128,8,128]{2,1,0:T(8,128)}, u32[]{:S(2)}) copy-start(f32[128,8,128]{2,1,0:T(8,128)} %param.8) | copy-start | bytes 1572868
  46.8 4.4 %collective-permute-start = (f32[8,256]{1,0:T(8,128)S(1)}, f32[8,256]{1,0:T(8,128)S(1)}, u32[]{:S(2)}, u32[]{:S(2)}) collective-permute-start(f32[8,256]{1,0:T(8,128)S(1)} %reduce_sum.78), channel_id=1, source_target_pairs={{0,64},{64,0},{128,192},{192,128},{1,65},{65,1},{129,193},{193,129... | collective-permute-start | bytes 24584 | tf_op jit(solution)/shard_map/ppermute | solution.py:46
  51.3 4.1 %collective-permute-start.1 = (f32[8,256]{1,0:T(8,128)S(1)}, f32[8,256]{1,0:T(8,128)S(1)}, u32[]{:S(2)}, u32[]{:S(2)}) collective-permute-start(f32[8,256]{1,0:T(8,128)S(1)} %add.224), channel_id=1, source_target_pairs={{0,128},{64,192},{128,0},{192,64},{1,129},{65,193},{129,1},{193,65... | collective-permute-start | bytes 24584 | tf_op jit(solution)/shard_map/ppermute | solution.py:46
  55.4 54.0 %slice-start = ((f32[512]{0:T(512)}), f32[256]{0:T(256)S(1)}, s32[]{:S(2)}) async-start(f32[512]{0:T(512)} %param.12), calls=%async_computation.3 | async-start | bytes 2048 | tf_op jit(solution)/shard_map/slice | solution.py:131
  56.7 52.7 %all-to-all-start.1 = ((f32[64,8,652]{2,1,0:T(8,128)}), f32[64,8,652]{2,1,0:T(8,128)S(1)}, u32[]{:S(2)}, u32[]{:S(2)}) async-start(f32[64,8,652]{2,1,0:T(8,128)} %pad_maximum_fusion), calls=%async_computation.1 | async-start | bytes 3145728 | tf_op jit(solution)/shard_map/all_to_all | solution.py:125
  109.5 49.7 %copy-start.1 = (f32[512,256]{1,0:T(8,128)}, f32[512,256]{1,0:T(8,128)S(1)}, u32[]{:S(2)}) copy-start(f32[512,256]{1,0:T(8,128)S(1)} %fusion.3) | copy-start | bytes 1572868
  171.9 6.4 %copy-start.2 = (f32[512,256]{1,0:T(8,128)S(1)}, f32[512,256]{1,0:T(8,128)}, u32[]{:S(2)}) copy-start(f32[512,256]{1,0:T(8,128)} %copy-done.1) | copy-start | bytes 1572868
  171.9 11.1 %copy-start.4 = (f32[512]{0:T(512)S(1)}, f32[512]{0:T(512)}, u32[]{:S(2)}) copy-start(f32[512]{0:T(512)} %param.12) | copy-start | bytes 6148
  175.0 3.9 %collective-permute-start.4 = (f32[32,512]{1,0:T(8,128)S(1)}, f32[32,512]{1,0:T(8,128)S(1)}, u32[]{:S(2)}, u32[]{:S(2)}) collective-permute-start(f32[32,512]{1,0:T(8,128)S(1)} %get-tuple-element.21), channel_id=1, source_target_pairs={{0,192},{64,0},{128,64},{192,128},{1,193},{65,1},{129,65},{193,129... | collective-permute-start | bytes 196616 | tf_op jit(solution)/shard_map/ppermute | solution.py:147
  176.7 4.6 %collective-permute-start.3 = (f32[32,512]{1,0:T(8,128)S(1)}, f32[32,512]{1,0:T(8,128)S(1)}, u32[]{:S(2)}, u32[]{:S(2)}) collective-permute-start(f32[32,512]{1,0:T(8,128)S(1)} %get-tuple-element.22), channel_id=1, source_target_pairs={{0,128},{64,192},{128,0},{192,64},{1,129},{65,193},{129,1},{193,65... | collective-permute-start | bytes 196616 | tf_op jit(solution)/shard_map/ppermute | solution.py:147
  177.5 5.5 %collective-permute-start.2 = (f32[32,512]{1,0:T(8,128)S(1)}, f32[32,512]{1,0:T(8,128)S(1)}, u32[]{:S(2)}, u32[]{:S(2)}) collective-permute-start(f32[32,512]{1,0:T(8,128)S(1)} %get-tuple-element.23), channel_id=1, source_target_pairs={{0,64},{64,128},{128,192},{192,0},{1,65},{65,129},{129,193},{193,1... | collective-permute-start | bytes 196616 | tf_op jit(solution)/shard_map/ppermute | solution.py:147
  183.9 3.2 %collective-permute-start.7 = (f32[32,512]{1,0:T(8,128)S(1)}, f32[32,512]{1,0:T(8,128)S(1)}, u32[]{:S(2)}, u32[]{:S(2)}) collective-permute-start(f32[32,512]{1,0:T(8,128)S(1)} %get-tuple-element.25), channel_id=1, source_target_pairs={{0,192},{64,0},{128,64},{192,128},{1,193},{65,1},{129,65},{193,129... | collective-permute-start | bytes 196616 | tf_op jit(solution)/shard_map/ppermute | solution.py:166
  183.9 4.7 %collective-permute-start.6 = (f32[32,512]{1,0:T(8,128)S(1)}, f32[32,512]{1,0:T(8,128)S(1)}, u32[]{:S(2)}, u32[]{:S(2)}) collective-permute-start(f32[32,512]{1,0:T(8,128)S(1)} %get-tuple-element.25), channel_id=1, source_target_pairs={{0,128},{64,192},{128,0},{192,64},{1,129},{65,193},{129,1},{193,65... | collective-permute-start | bytes 196616 | tf_op jit(solution)/shard_map/ppermute | solution.py:166
  185.0 4.5 %collective-permute-start.5 = (f32[32,512]{1,0:T(8,128)S(1)}, f32[32,512]{1,0:T(8,128)S(1)}, u32[]{:S(2)}, u32[]{:S(2)}) collective-permute-start(f32[32,512]{1,0:T(8,128)S(1)} %get-tuple-element.25), channel_id=1, source_target_pairs={{0,64},{64,128},{128,192},{192,0},{1,65},{65,129},{129,193},{193,1... | collective-permute-start | bytes 196616 | tf_op jit(solution)/shard_map/ppermute | solution.py:166
Sparse Core Ops, SparseCore 0:
  33.6 83.5 all-gather.1

commit v6 on v5

--- a/solution.py
+++ b/solution.py
@@ -114,18 +114,14 @@
     panel_pos = jnp.where(panel_hit > 0, jnp.cumsum(panel_hit, axis=0) - 1, CAP)
     slot_pos = jnp.where(valid[:, :, None], panel_pos[obs_sel], CAP).astype(jnp.float32)
     index_width = CAP * panel_blocks // gram_rows
+    square = lax.all_to_all(spread, "blk", 0, 0, tiled=True).reshape(panel_cols, half)
     payload = jnp.concatenate(
-        [
-            spread,
-            tile_rows.reshape(nb, gram_rows, -1),
-            slot_pos.reshape(nb, gram_rows, index_width),
-        ],
-        axis=2,
+        [tile_rows.reshape(nb, gram_rows, -1), slot_pos.reshape(nb, gram_rows, index_width)], axis=2
     )
+    square, payload = lax.optimization_barrier((square, payload))
     got = lax.all_to_all(payload, "blk", 0, 0, tiled=True)
-    square = got[:, :, :half].reshape(panel_cols, half)
-    got_tiles = got[:, :, half : half + CAP * bw // gram_rows].reshape(nb * CAP, bw)
-    got_pos = got[:, :, half + CAP * bw // gram_rows :].reshape(nb, CAP, panel_blocks).astype(jnp.int32)
+    got_tiles = got[:, :, : CAP * bw // gram_rows].reshape(nb * CAP, bw)
+    got_pos = got[:, :, CAP * bw // gram_rows :].reshape(nb, CAP, panel_blocks).astype(jnp.int32)
     diag = jnp.arange(half, dtype=jnp.int32)
     square = square + jnp.where(
         diag[None, :] == jnp.arange(panel_cols, dtype=jnp.int32)[:, None], prior_weight[None, :half], 0.0

time: 199 us -> 183 us (0.920)
  waiting for transfers between devices: 58.4 us -> 35.8 us
  starting transfers between devices: 29.8 us -> 37.3 us
    all_to_all x1, waiting for transfers between devices: 43.4 us -> 0.01 us  [local(): got = lax.all_to_all(payload, 'blk', 0, 0, tiled=True)]
    all_to_all x0 -> x1, waiting for transfers between devices: none -> 13.5 us  [local(): lax.all_to_all(spread, 'blk', 0, 0, tiled=True).reshape(panel_cols, half)]
    all_to_all x1, waiting for transfers between devices: 5.66 us -> 16.6 us  [local(): lax.all_to_all(gram.reshape(nb, gram_rows, half), 'blk', 0, 0, tiled=True)]
    all_to_all x0 -> x1, starting transfers between devices: none -> 6.82 us  [local(): lax.all_to_all(spread, 'blk', 0, 0, tiled=True).reshape(panel_cols, half)]
    ppermute x3, starting transfers between devices: 1.57 us -> 3.95 us  [local(): lax.ppermute(done, 'obs', [(i, (i + s) % n_obs_dev) for i in range(n_obs_...]
    ppermute x3, waiting for transfers between devices: 4.01 us -> 1.65 us  [local(): lax.ppermute(done, 'obs', [(i, (i + s) % n_obs_dev) for i in range(n_obs_...]
  transfers between devices with their start and end apart: 11 -> 12, of which waited for: 9 -> 6; matrix products, arithmetic and copies ran while one was open for 35% -> 37% of each run, Pallas kernels for 0% -> 0%
where the time goes in v6:
time: 183 us; the launch traced here: 181 us
  other arithmetic  55.5 us (30%)
  starting transfers between devices  37.3 us (20%)
  waiting for transfers between devices  35.8 us (20%)
  local copies, waits for them, and re-layouts  24.6 us (13%)
  between operations  15.5 us (8%)
  matrix products  12 us (7%)
    all_to_all x1, waiting for transfers between devices, local(): lax.all_to_all(gram.reshape(nb, gram_rows, half), 'blk', 0, 0, tiled=True)  16.6 us
    all_to_all x1, waiting for transfers between devices, local(): lax.all_to_all(spread, 'blk', 0, 0, tiled=True).reshape(panel_cols, half)  13.5 us
    all_to_all x1, starting transfers between devices, local(): lax.all_to_all(gram.reshape(nb, gram_rows, half), 'blk', 0, 0, tiled=True)  13 us
    another operation x3, other arithmetic, factor_inverse(): low = jnp.linalg.cholesky(mirrored[:n, :n])  12.4 us
    another operation x3, other arithmetic, factor_inverse(): high = jnp.linalg.cholesky(mirrored[n:, n:] - dot(left, left.T))  12.4 us
    another operation x2, other arithmetic, factor_inverse(): high_inv = jax.scipy.linalg.solve_triangular(high, eye, lower=True)  10.7 us
    another operation x2, other arithmetic, factor_inverse(): low_inv = jax.scipy.linalg.solve_triangular(low, eye, lower=True)  10.5 us
    all_to_all x1, starting transfers between devices, local(): lax.all_to_all(spread, 'blk', 0, 0, tiled=True).reshape(panel_cols, half)  6.82 us
  transfers between devices with their start and end apart: 12, of which 6 were waited for; matrix products, arithmetic and copies ran while one was open for 37% of the time, Pallas kernels for 0%

profile of v6, /device:TPU:1, one launch (start us, length us, event | category | flops | bytes accessed | tf_op | source)
XLA Modules:
  0.0 180.8 jit_solution(6788625337062228876)
XLA Ops:
  7.2 0.7 convert_reduce_fusion.3
  7.9 1.0 slice_bitcast_fusion.11
  9.7 3.4 %fusion.37 = (f32[128,1,128]{2,1,0:T(1,128)S(1)}, f32[128,1,128]{2,1,0:T(1,128)S(1)}, f32[128,1,128]{2,1,0:T(1,128)S(1)}, f32[128,1,128]{2,1,0:T(1,128)S(1)}, f3...) fusion(f32[128,8,128]{2,1,0:T(8,128)} %param.8), kind=kLoop, calls=%fused_computation.125 | loop fusion | bytes 1048576 | tf_op jit(solution)/shard_map/slice | solution.py:37
  13.5 2.3 %broadcast_multiply_fusion = (f32[128,4,128]{2,1,0:T(4,128)S(1)}, f32[128,4,128]{2,1,0:T(4,128)S(1)}) fusion(f32[128]{0:T(128)} %param.10, f32[128,128]{1,0:T(8,128)S(1)} %bitcast.151, pred[128,4]{1,0:T(8,128)(4,1)S(1)} %get-tuple-element.38, f32[128,128]{1,0:T(8,128)S(1)} %bitcast.145, pred[128,4]{1,0:T(8,128)(4,1)S(1)} %get-tuple-element.39, ...), kind=kLoop, calls=%fused_computation.43 | loop fusion | flops 1048576 | bytes 1053184 | tf_op jit(solution)/shard_map/mul | solution.py:96
  15.7 1.2 gather_fusion.3
  17.0 0.7 bitcast_select_fusion
  18.0 1.4 fusion.6
  19.3 13.0 %all-to-all-start = ((f32[64,8,256]{2,1,0:T(8,128)}), f32[64,8,256]{2,1,0:T(8,128)S(1)}, u32[]{:S(2)}, u32[]{:S(2)}) async-start(f32[64,8,256]{2,1,0:T(8,128)} %fusion.6), calls=%async_computation | async-start | bytes 1048576 | tf_op jit(solution)/shard_map/all_to_all | solution.py:103
  32.8 1.2 convert_reduce_fusion
  34.1 16.6 %all-to-all-done = f32[64,8,256]{2,1,0:T(8,128)S(1)} async-done(((f32[64,8,256]{2,1,0:T(8,128)}), f32[64,8,256]{2,1,0:T(8,128)S(1)}, u32[]{:S(2)}, u32[]{:S(2)}) %all-to-all-start) | async-done | bytes 524320 | tf_op jit(solution)/shard_map/all_to_all | solution.py:103
  50.8 1.4 collective-permute-start
  52.3 2.6 %gather_fusion.2 = s32[1536,4]{1,0:T(8,128)S(1)} fusion(s32[128,4]{1,0:T(8,128)S(1)} %copy.78, s32[2048]{0:T(1024)S(1)} %pad_clamp_fusion.1), kind=kCustom, calls=%fused_computation.2 | custom fusion | bytes 55296 | tf_op jit(solution)/shard_map/gather | solution.py:115
  55.2 2.7 %collective-permute-start.1 = (f32[8,256]{1,0:T(8,128)S(1)}, f32[8,256]{1,0:T(8,128)S(1)}, u32[]{:S(2)}, u32[]{:S(2)}) collective-permute-start(f32[8,256]{1,0:T(8,128)S(1)} %add.224), channel_id=1, source_target_pairs={{0,128},{64,192},{128,0},{192,64},{1,129},{65,193},{129,1},{193,65... | collective-permute-start | bytes 24584 | tf_op jit(solution)/shard_map/ppermute | solution.py:46
  58.0 2.6 %gather_fusion = s32[1536,8]{1,0:T(8,128)S(1)} fusion(s32[128,8]{1,0:T(8,128)S(1)} %copy.75, s32[2048]{0:T(1024)S(1)} %pad_clamp_fusion.1), kind=kCustom, calls=%fused_computation | custom fusion | bytes 104448 | tf_op jit(solution)/shard_map/gather | solution.py:85
  60.7 0.8 broadcast_in_dim.288
  61.5 6.8 %all-to-all-start.1 = ((f32[64,8,256]{2,1,0:T(8,128)}), f32[64,8,256]{2,1,0:T(8,128)S(1)}, u32[]{:S(2)}, u32[]{:S(2)}) async-start(f32[64,8,256]{2,1,0:T(8,128)} %broadcast_in_dim.288), calls=%async_computation.1 | async-start | bytes 1048576 | tf_op jit(solution)/shard_map/all_to_all | solution.py:117
  68.3 1.2 select_reduce_fusion
  70.0 2.6 %gather_fusion.1 = f32[1536,128]{1,0:T(8,128)S(1)} fusion(f32[1024,128]{1,0:T(8,128)S(1)} %bitcast.133, s32[2048]{0:T(1024)S(1)} %pad_clamp_fusion), kind=kCustom, calls=%fused_computation.1 | custom fusion | bytes 1579008 | tf_op jit(solution)/shard_map/gather | solution.py:91
  73.1 0.6 fusion.29
  74.4 1.1 pad_maximum_fusion
  75.5 13.5 %all-to-all-done.1 = f32[64,8,256]{2,1,0:T(8,128)S(1)} async-done(((f32[64,8,256]{2,1,0:T(8,128)}), f32[64,8,256]{2,1,0:T(8,128)S(1)}, u32[]{:S(2)}, u32[]{:S(2)}) %all-to-all-start.1) | async-done | bytes 524320 | tf_op jit(solution)/shard_map/all_to_all | solution.py:117
  89.0 6.6 %all-to-all-start.2 = ((f32[64,8,396]{2,1,0:T(8,128)}), f32[64,8,396]{2,1,0:T(8,128)S(1)}, u32[]{:S(2)}, u32[]{:S(2)}) async-start(f32[64,8,396]{2,1,0:T(8,128)} %pad_maximum_fusion), calls=%async_computation.2 | async-start | bytes 2097152 | tf_op jit(solution)/shard_map/all_to_all | solution.py:122
  96.0 11.7 %cholesky.44 = f32[128,128]{1,0:T(8,128)S(1)} custom-call(f32[128,128]{1,0:T(8,128)S(1)} %fusion.24), custom_call_target="Cholesky" | custom-call | tf_op jit(solution)/shard_map/jit(cholesky)/cholesky | solution.py:18
  107.8 0.6 compare_reduce_fusion.1
  108.4 0.7 fusion.17
  109.1 9.8 %custom-call.8 = f32[1,128,128]{1,2,0:T(8,128)S(1)} custom-call(f32[1,128,128]{2,1,0:T(8,128)S(1)} %fusion.17), custom_call_target="InvertDiagBlocksLowerTriangular" | custom-call | tf_op jit(solution)/shard_map/jit(_solve_triangular)/triangular_solve | solution.py:19
  119.8 11.7 %cholesky.55 = f32[128,128]{1,0:T(8,128)S(1)} custom-call(f32[128,128]{1,0:T(8,128)S(1)} %fusion.22), custom_call_target="Cholesky" | custom-call | tf_op jit(solution)/shard_map/jit(cholesky)/cholesky | solution.py:21
  131.6 0.6 compare_reduce_fusion
  132.2 0.7 fusion.18
  132.9 10.0 %custom-call.9 = f32[1,128,128]{1,2,0:T(8,128)S(1)} custom-call(f32[1,128,128]{2,1,0:T(8,128)S(1)} %fusion.18), custom_call_target="InvertDiagBlocksLowerTriangular" | custom-call | tf_op jit(solution)/shard_map/jit(_solve_triangular)/triangular_solve | solution.py:22
  144.2 1.1 copy.81
  145.5 4.9 %fusion.1 = f32[64,24,4,128]{3,1,2,0:T(8,128)S(1)} fusion(f32[64,4,24,128]{3,2,1,0:T(8,128)} %bitcast.138, s32[64,24,4]{1,2,0:T(4,128)S(1)} %copy.85), kind=kOutput, calls=%fused_computation.6 | convolution fusion | flops 226639872 | bytes 6316032 | tf_op jit(solution)/shard_map/srpq,spqc->srpc/dot_general | solution.py:132
  150.4 2.5 %copy.86 = f32[64,24,4,128]{3,2,1,0:T(4,128)} copy(f32[64,24,4,128]{3,1,2,0:T(8,128)S(1)} %fusion.1) | data formatting | bytes 6291456 | tf_op jit(solution)/shard_map/srpq,spqc->srpc/transpose | solution.py:132
  152.9 3.3 %reshape.455 = f32[1536,512,1]{1,0,2:T(8,128)S(1)} reshape(f32[64,24,4,128]{3,2,1,0:T(4,128)} %copy.86) | data formatting | bytes 6291456 | tf_op jit(solution)/shard_map/reshape | solution.py:133
  156.2 3.1 %fusion.39 = f32[4,32,512]{2,1,0:T(8,128)S(1)} fusion(f32[4,32,1536]{2,1,0:T(8,128)} %bitcast.134, f32[1536,512,1]{1,0,2:T(8,128)S(1)} %reshape.455), kind=kOutput, calls=%fused_computation.127 | convolution fusion | flops 1207959552 | bytes 4194304 | tf_op jit(solution)/shard_map/si,sp->ip/dot_general | solution.py:133
  159.3 0.9 collective-permute-start.4
  160.2 1.3 collective-permute-start.3
  161.5 0.8 collective-permute-start.2
  162.2 0.4 fusion.3
  162.7 2.1 %collective-permute-done.3 = f32[32,512]{1,0:T(8,128)S(1)} collective-permute-done((f32[32,512]{1,0:T(8,128)S(1)}, f32[32,512]{1,0:T(8,128)S(1)}, u32[]{:S(2)}, u32[]{:S(2)}) %collective-permute-start.3) | collective-permute-done | bytes 65568 | tf_op jit(solution)/shard_map/ppermute | solution.py:143
  164.8 1.9 %collective-permute-done.2 = f32[32,512]{1,0:T(8,128)S(1)} collective-permute-done((f32[32,512]{1,0:T(8,128)S(1)}, f32[32,512]{1,0:T(8,128)S(1)}, u32[]{:S(2)}, u32[]{:S(2)}) %collective-permute-start.2) | collective-permute-done | bytes 65568 | tf_op jit(solution)/shard_map/ppermute | solution.py:143
  166.8 0.3 fusion.8
  167.2 0.3 convolution_subtract_fusion.1
  167.6 1.3 collective-permute-start.6
  168.8 2.7 %collective-permute-start.7 = (f32[32,512]{1,0:T(8,128)S(1)}, f32[32,512]{1,0:T(8,128)S(1)}, u32[]{:S(2)}, u32[]{:S(2)}) collective-permute-start(f32[32,512]{1,0:T(8,128)S(1)} %get-tuple-element.29), channel_id=1, source_target_pairs={{0,192},{64,0},{128,64},{192,128},{1,193},{65,1},{129,65},{193,129... | collective-permute-start | bytes 196616 | tf_op jit(solution)/shard_map/ppermute | solution.py:162
  171.5 0.8 collective-permute-done.6
  172.3 0.9 collective-permute-done.5
  173.2 0.7 fusion.38
  (101 shorter events, 6.4 us)
Async XLA Ops:
  7.2 10.6 %copy-start.5 = (f32[128]{0:T(128)S(1)}, f32[128]{0:T(128)}, u32[]{:S(2)}) copy-start(f32[128]{0:T(128)} %param.10) | copy-start | bytes 1540
  7.2 138.3 %all-gather.2.cloned.1.call-start = ((), (), s32[]{:S(2)}) async-start(), calls=%async_computation.3 | async-start | bytes 3194880 | tf_op jit(solution)/shard_map/all_gather | solution.py:111
  9.7 22.6 %copy-start.3 = (s32[128,8]{0,1:T(8,128)S(1)}, s32[128,8]{0,1:T(8,128)}, u32[]{:S(2)}) copy-start(s32[128,8]{0,1:T(8,128)} %param.9) | copy-start | bytes 12292
  9.7 22.6 %copy-start.6 = (s32[64]{0:T(128)S(1)}, s32[64]{0:T(128)}, u32[]{:S(2)}) copy-start(s32[64]{0:T(128)} %param.11) | copy-start | bytes 772
  19.3 31.4 %all-to-all-start = ((f32[64,8,256]{2,1,0:T(8,128)}), f32[64,8,256]{2,1,0:T(8,128)S(1)}, u32[]{:S(2)}, u32[]{:S(2)}) async-start(f32[64,8,256]{2,1,0:T(8,128)} %fusion.6), calls=%async_computation | async-start | bytes 1048576 | tf_op jit(solution)/shard_map/all_to_all | solution.py:103
  50.8 4.4 %collective-permute-start = (f32[8,256]{1,0:T(8,128)S(1)}, f32[8,256]{1,0:T(8,128)S(1)}, u32[]{:S(2)}, u32[]{:S(2)}) collective-permute-start(f32[8,256]{1,0:T(8,128)S(1)} %reduce_sum.78), channel_id=1, source_target_pairs={{0,64},{64,0},{128,192},{192,128},{1,65},{65,1},{129,193},{193,129... | collective-permute-start | bytes 24584 | tf_op jit(solution)/shard_map/ppermute | solution.py:46
  55.2 5.4 %collective-permute-start.1 = (f32[8,256]{1,0:T(8,128)S(1)}, f32[8,256]{1,0:T(8,128)S(1)}, u32[]{:S(2)}, u32[]{:S(2)}) collective-permute-start(f32[8,256]{1,0:T(8,128)S(1)} %add.224), channel_id=1, source_target_pairs={{0,128},{64,192},{128,0},{192,64},{1,129},{65,193},{129,1},{193,65... | collective-permute-start | bytes 24584 | tf_op jit(solution)/shard_map/ppermute | solution.py:46
  60.6 9.4 %copy-start = (f32[128,8,128]{2,1,0:T(8,128)S(1)}, f32[128,8,128]{2,1,0:T(8,128)}, u32[]{:S(2)}) copy-start(f32[128,8,128]{2,1,0:T(8,128)} %param.8) | copy-start | bytes 1572868
  61.5 27.5 %all-to-all-start.1 = ((f32[64,8,256]{2,1,0:T(8,128)}), f32[64,8,256]{2,1,0:T(8,128)S(1)}, u32[]{:S(2)}, u32[]{:S(2)}) async-start(f32[64,8,256]{2,1,0:T(8,128)} %broadcast_in_dim.288), calls=%async_computation.1 | async-start | bytes 1048576 | tf_op jit(solution)/shard_map/all_to_all | solution.py:117
  72.9 22.7 %slice-start = ((f32[512]{0:T(512)}), f32[256]{0:T(256)S(1)}, s32[]{:S(2)}) async-start(f32[512]{0:T(512)} %param.12), calls=%async_computation.4 | async-start | bytes 2048 | tf_op jit(solution)/shard_map/slice | solution.py:127
  89.0 54.8 %all-to-all-start.2 = ((f32[64,8,396]{2,1,0:T(8,128)}), f32[64,8,396]{2,1,0:T(8,128)S(1)}, u32[]{:S(2)}, u32[]{:S(2)}) async-start(f32[64,8,396]{2,1,0:T(8,128)} %pad_maximum_fusion), calls=%async_computation.2 | async-start | bytes 2097152 | tf_op jit(solution)/shard_map/all_to_all | solution.py:122
  95.7 48.4 %copy-start.1 = (f32[512,256]{1,0:T(8,128)}, f32[512,256]{1,0:T(8,128)S(1)}, u32[]{:S(2)}) copy-start(f32[512,256]{1,0:T(8,128)S(1)} %select_add_fusion) | copy-start | bytes 1572868
  156.2 6.0 %copy-start.2 = (f32[512,256]{1,0:T(8,128)S(1)}, f32[512,256]{1,0:T(8,128)}, u32[]{:S(2)}) copy-start(f32[512,256]{1,0:T(8,128)} %copy-done.1) | copy-start | bytes 1572868
  156.2 10.5 %copy-start.4 = (f32[512]{0:T(512)S(1)}, f32[512]{0:T(512)}, u32[]{:S(2)}) copy-start(f32[512]{0:T(512)} %param.12) | copy-start | bytes 6148
  159.3 3.4 %collective-permute-start.4 = (f32[32,512]{1,0:T(8,128)S(1)}, f32[32,512]{1,0:T(8,128)S(1)}, u32[]{:S(2)}, u32[]{:S(2)}) collective-permute-start(f32[32,512]{1,0:T(8,128)S(1)} %get-tuple-element.25), channel_id=1, source_target_pairs={{0,192},{64,0},{128,64},{192,128},{1,193},{65,1},{129,65},{193,129... | collective-permute-start | bytes 196616 | tf_op jit(solution)/shard_map/ppermute | solution.py:143
  160.2 4.6 %collective-permute-start.3 = (f32[32,512]{1,0:T(8,128)S(1)}, f32[32,512]{1,0:T(8,128)S(1)}, u32[]{:S(2)}, u32[]{:S(2)}) collective-permute-start(f32[32,512]{1,0:T(8,128)S(1)} %get-tuple-element.26), channel_id=1, source_target_pairs={{0,128},{64,192},{128,0},{192,64},{1,129},{65,193},{129,1},{193,65... | collective-permute-start | bytes 196616 | tf_op jit(solution)/shard_map/ppermute | solution.py:143
  161.5 5.2 %collective-permute-start.2 = (f32[32,512]{1,0:T(8,128)S(1)}, f32[32,512]{1,0:T(8,128)S(1)}, u32[]{:S(2)}, u32[]{:S(2)}) collective-permute-start(f32[32,512]{1,0:T(8,128)S(1)} %get-tuple-element.27), channel_id=1, source_target_pairs={{0,64},{64,128},{128,192},{192,0},{1,65},{65,129},{129,193},{193,1... | collective-permute-start | bytes 196616 | tf_op jit(solution)/shard_map/ppermute | solution.py:143
  167.6 4.7 %collective-permute-start.6 = (f32[32,512]{1,0:T(8,128)S(1)}, f32[32,512]{1,0:T(8,128)S(1)}, u32[]{:S(2)}, u32[]{:S(2)}) collective-permute-start(f32[32,512]{1,0:T(8,128)S(1)} %get-tuple-element.29), channel_id=1, source_target_pairs={{0,128},{64,192},{128,0},{192,64},{1,129},{65,193},{129,1},{193,65... | collective-permute-start | bytes 196616 | tf_op jit(solution)/shard_map/ppermute | solution.py:162
  168.8 4.3 %collective-permute-start.5 = (f32[32,512]{1,0:T(8,128)S(1)}, f32[32,512]{1,0:T(8,128)S(1)}, u32[]{:S(2)}, u32[]{:S(2)}) collective-permute-start(f32[32,512]{1,0:T(8,128)S(1)} %get-tuple-element.29), channel_id=1, source_target_pairs={{0,64},{64,128},{128,192},{192,0},{1,65},{65,129},{129,193},{193,1... | collective-permute-start | bytes 196616 | tf_op jit(solution)/shard_map/ppermute | solution.py:162
  168.8 4.3 %collective-permute-start.7 = (f32[32,512]{1,0:T(8,128)S(1)}, f32[32,512]{1,0:T(8,128)S(1)}, u32[]{:S(2)}, u32[]{:S(2)}) collective-permute-start(f32[32,512]{1,0:T(8,128)S(1)} %get-tuple-element.29), channel_id=1, source_target_pairs={{0,192},{64,0},{128,64},{192,128},{1,193},{65,1},{129,65},{193,129... | collective-permute-start | bytes 196616 | tf_op jit(solution)/shard_map/ppermute | solution.py:162
Sparse Core Ops, SparseCore 0:
  17.8 85.7 all-gather.1

commit v7 on v1

--- a/solution.py
+++ b/solution.py
@@ -48,6 +48,15 @@
     return x
 
 
+def ranked(labels, wanted):
+    hit = jnp.sum((labels[:, :, None] == wanted[None, None, :]).astype(jnp.int32), axis=1)
+    cum = jnp.cumsum(hit, axis=0)
+    rank_range = jnp.arange(CAP, dtype=jnp.int32)
+    sel = jnp.sum((cum[:, :, None] <= rank_range[None, None, :]).astype(jnp.int32), axis=0)
+    valid = rank_range[None, :] < cum[-1][:, None]
+    return jnp.minimum(sel, labels.shape[0] - 1), valid, jnp.where(hit > 0, cum - 1, CAP)
+
+
 def local(design_tiles, block_ids, obs_weight, block_owner, prior_weight):
     n_obs, touched, bw = design_tiles.shape
     nblk = block_owner.shape[0]
@@ -94,20 +103,39 @@
     got_gram = lax.all_to_all(gram.reshape(nb, gram_rows, half), "blk", 0, 0, tiled=True)
     gram_part = obs_butterfly(jnp.sum(got_gram, axis=0))
     spread = jnp.broadcast_to(gram_part[None], (nb, gram_rows, half))
+
+    panel_range = jnp.arange(panel_blocks, dtype=jnp.int32)
+    panel_sel, panel_valid, panel_pos = ranked(block_ids, panel_range)
+    panel_tiles = weighted.reshape(n_obs, panel_blocks, bw)[panel_sel, panel_range[:, None]]
+    panel_tiles = jnp.where(panel_valid[:, :, None], panel_tiles, 0.0)
+    shared = lax.all_gather(panel_tiles.reshape(-1, bw), "blk", axis=0, tiled=False)
+
+    slot_pos = jnp.where(valid[:, :, None], panel_pos[obs_sel], CAP).astype(jnp.float32)
+    index_width = CAP * panel_blocks // gram_rows
     square = lax.all_to_all(spread, "blk", 0, 0, tiled=True).reshape(panel_cols, half)
+    payload = jnp.concatenate(
+        [tile_rows.reshape(nb, gram_rows, -1), slot_pos.reshape(nb, gram_rows, index_width)], axis=2
+    )
+    square, payload = lax.optimization_barrier((square, payload))
+    got = lax.all_to_all(payload, "blk", 0, 0, tiled=True)
+    got_tiles = got[:, :, : CAP * bw // gram_rows].reshape(nb * CAP, bw)
+    got_pos = got[:, :, CAP * bw // gram_rows :].reshape(nb, CAP, panel_blocks).astype(jnp.int32)
     diag = jnp.arange(half, dtype=jnp.int32)
     square = square + jnp.where(
         diag[None, :] == jnp.arange(panel_cols, dtype=jnp.int32)[:, None], prior_weight[None, :half], 0.0
     )
 
-    owned = 0.0
-    for lo, hi in ((0, FIRST), (FIRST, CAP)):
-        payload = jnp.concatenate([tile_rows[:, lo:hi], panel_rows[:, lo:hi]], axis=2)
-        got = lax.all_to_all(payload, "blk", 0, 0, tiled=True).reshape(nb * (hi - lo), bw + panel_cols)
-        owned = owned + jnp.einsum("si,sp->ip", got[:, :bw], got[:, bw:], precision=HI)
+    src_panel = jnp.concatenate(
+        [shared.reshape(nb, panel_blocks, CAP, bw), jnp.zeros((nb, panel_blocks, 1, bw), jnp.float32)], axis=2
+    ).reshape(nb * panel_blocks * (CAP + 1), bw)
+    row_of = (
+        jnp.arange(nb, dtype=jnp.int32)[:, None, None] * panel_blocks + panel_range[None, None, :]
+    ) * (CAP + 1) + got_pos
+    slot_panel = src_panel[row_of]
+    owned = jnp.einsum("si,sp->ip", got_tiles, slot_panel.reshape(nb * CAP, panel_cols), precision=HI)
+    my_block = jnp.sum(jnp.where(block_owner == my_j, block_range, 0))
+
     owned = obs_butterfly(owned)
-
-    my_block = jnp.sum(jnp.where(block_owner == my_j, block_range, 0))
     row_index = my_block * bw + jnp.arange(bw, dtype=jnp.int32)
     col_index = jnp.arange(panel_cols, dtype=jnp.int32)
     owned = owned + jnp.where(col_index[None, :] == row_index[:, None], prior_weight[None, :], 0.0)

time: 204 us -> 203 us (level)
  waiting for transfers between devices: 72.6 us -> 35.6 us
  local copies, waits for them, and re-layouts: 20.7 us -> 49.6 us
  between operations: 1.79 us -> 15.3 us
  other arithmetic: 60.2 us -> 55.6 us
  starting transfers between devices: 39.5 us -> 36.3 us
    all_to_all x2 -> x1, waiting for transfers between devices: 36.5 us -> 0.01 us  [local(): got = lax.all_to_all(payload, 'blk', 0, 0, tiled=True)]
    gather x1 -> x4, local copies, waits for them, and re-layouts: 3.76 us -> 25 us  [the longest x1 20.9 us: local(): slot_panel = src_panel[row_of]]
    all_to_all x1, waiting for transfers between devices: 5.84 us -> 14.6 us  [local(): lax.all_to_all(spread, 'blk', 0, 0, tiled=True).reshape(panel_cols, half)]
    reshape x0 -> x3, local copies, waits for them, and re-layouts: none -> 6.71 us  [the longest x1 2.92 us: local(): src_panel = jnp.concatenate([shared.reshape(nb, panel_blocks, CAP, bw), j...]
    all_to_all x2 -> x1, starting transfers between devices: 12.6 us -> 6.49 us  [local(): got = lax.all_to_all(payload, 'blk', 0, 0, tiled=True)]
    all_to_all x1, waiting for transfers between devices: 15.5 us -> 10.8 us  [local(): lax.all_to_all(gram.reshape(nb, gram_rows, half), 'blk', 0, 0, tiled=True)]
    ppermute x4, waiting for transfers between devices: 14.7 us -> 10.1 us  [obs_butterfly(): x = x + lax.ppermute(x, 'obs', perm)]
    concatenate x0 -> x2, local copies, waits for them, and re-layouts: none -> 4.47 us  [the longest x1 4.38 us: local(): jnp.concatenate([shared.reshape(nb, panel_blocks, CAP, bw), jnp.zeros((nb...]
  transfers between devices with their start and end apart: 8 -> 8, of which waited for: 7 -> 6; matrix products, arithmetic and copies ran while one was open for 37% -> 34% of each run, Pallas kernels for 0% -> 0%
where the time goes in v7:
time: 203 us; the launch traced here: 201 us
  other arithmetic  55.6 us (27%)
  local copies, waits for them, and re-layouts  49.6 us (24%)
  starting transfers between devices  36.3 us (18%)
  waiting for transfers between devices  35.6 us (18%)
  between operations  15.3 us (8%)
  matrix products  8.89 us (4%)
    gather x1, local copies, waits for them, and re-layouts, local(): slot_panel = src_panel[row_of]  20.9 us
    all_to_all x1, waiting for transfers between devices, local(): lax.all_to_all(spread, 'blk', 0, 0, tiled=True).reshape(panel_cols, half)  14.6 us
    all_to_all x1, starting transfers between devices, local(): lax.all_to_all(gram.reshape(nb, gram_rows, half), 'blk', 0, 0, tiled=True)  13 us
    another operation x3, other arithmetic, factor_inverse(): low = jnp.linalg.cholesky(mirrored[:n, :n])  12.4 us
    another operation x3, other arithmetic, factor_inverse(): high = jnp.linalg.cholesky(mirrored[n:, n:] - dot(left, left.T))  12.4 us
    all_to_all x1, waiting for transfers between devices, local(): lax.all_to_all(gram.reshape(nb, gram_rows, half), 'blk', 0, 0, tiled=True)  10.8 us
    another operation x2, other arithmetic, factor_inverse(): high_inv = jax.scipy.linalg.solve_triangular(high, eye, lower=True)  10.7 us
    another operation x2, other arithmetic, factor_inverse(): low_inv = jax.scipy.linalg.solve_triangular(low, eye, lower=True)  10.5 us
  transfers between devices with their start and end apart: 8, of which 6 were waited for; matrix products, arithmetic and copies ran while one was open for 34% of the time, Pallas kernels for 0%

profile of v7, /device:TPU:1, one launch (start us, length us, event | category | flops | bytes accessed | tf_op | source)
XLA Modules:
  0.0 201.3 jit_solution(1065185918314255458)
XLA Ops:
  7.2 0.7 convert_reduce_fusion.3
  7.9 1.0 slice_bitcast_fusion.11
  9.7 3.4 %fusion.33 = (f32[128,1,128]{2,1,0:T(1,128)S(1)}, f32[128,1,128]{2,1,0:T(1,128)S(1)}, f32[128,1,128]{2,1,0:T(1,128)S(1)}, f32[128,1,128]{2,1,0:T(1,128)S(1)}, f3...) fusion(f32[128,8,128]{2,1,0:T(8,128)} %param.8), kind=kLoop, calls=%fused_computation.113 | loop fusion | bytes 1048576 | tf_op jit(solution)/shard_map/slice | solution.py:37
  13.6 2.3 %broadcast_multiply_fusion = (f32[128,4,128]{2,1,0:T(4,128)S(1)}, f32[128,4,128]{2,1,0:T(4,128)S(1)}) fusion(f32[128]{0:T(128)} %param.10, f32[128,128]{1,0:T(8,128)S(1)} %bitcast.124, pred[128,4]{1,0:T(8,128)(4,1)S(1)} %get-tuple-element.26, f32[128,128]{1,0:T(8,128)S(1)} %bitcast.118, pred[128,4]{1,0:T(8,128)(4,1)S(1)} %get-tuple-element.27, ...), kind=kLoop, calls=%fused_computation.41 | loop fusion | flops 1048576 | bytes 1053184 | tf_op jit(solution)/shard_map/mul | solution.py:96
  15.8 1.2 gather_fusion.3
  17.1 0.7 bitcast_select_fusion
  18.1 1.4 fusion.3
  19.4 13.0 %all-to-all-start = ((f32[64,8,256]{2,1,0:T(8,128)}), f32[64,8,256]{2,1,0:T(8,128)S(1)}, u32[]{:S(2)}, u32[]{:S(2)}) async-start(f32[64,8,256]{2,1,0:T(8,128)} %fusion.3), calls=%async_computation | async-start | bytes 1048576 | tf_op jit(solution)/shard_map/all_to_all | solution.py:103
  32.9 1.2 convert_reduce_fusion
  34.4 2.6 %gather_fusion.2 = s32[1536,4]{1,0:T(8,128)S(1)} fusion(s32[128,4]{1,0:T(8,128)S(1)} %copy.85, s32[2048]{0:T(1024)S(1)} %pad_clamp_fusion.1), kind=kCustom, calls=%fused_computation.2 | custom fusion | bytes 55296 | tf_op jit(solution)/shard_map/gather | solution.py:113
  37.0 0.3 copy.86
  37.3 2.6 %gather_fusion = s32[1536,8]{1,0:T(8,128)S(1)} fusion(s32[128,8]{1,0:T(8,128)S(1)} %copy.82, s32[2048]{0:T(1024)S(1)} %pad_clamp_fusion.1), kind=kCustom, calls=%fused_computation | custom fusion | bytes 104448 | tf_op jit(solution)/shard_map/gather | solution.py:85
  40.0 10.8 %all-to-all-done = f32[64,8,256]{2,1,0:T(8,128)S(1)} async-done(((f32[64,8,256]{2,1,0:T(8,128)}), f32[64,8,256]{2,1,0:T(8,128)S(1)}, u32[]{:S(2)}, u32[]{:S(2)}) %all-to-all-start) | async-done | bytes 524320 | tf_op jit(solution)/shard_map/all_to_all | solution.py:103
  50.9 1.4 collective-permute-start
  52.2 1.2 select_reduce_fusion
  53.4 0.5 collective-permute-done
  53.9 2.9 %collective-permute-start.1 = (f32[8,256]{1,0:T(8,128)S(1)}, f32[8,256]{1,0:T(8,128)S(1)}, u32[]{:S(2)}, u32[]{:S(2)}) collective-permute-start(f32[8,256]{1,0:T(8,128)S(1)} %add.195), channel_id=1, source_target_pairs={{0,128},{64,192},{128,0},{192,64},{1,129},{65,193},{129,1},{193,65... | collective-permute-start | bytes 24584 | tf_op jit(solution)/shard_map/ppermute | solution.py:46
  57.2 0.7 collective-permute-done.1
  57.9 0.9 broadcast_in_dim.288
  58.8 8.1 %all-to-all-start.1 = ((f32[64,8,256]{2,1,0:T(8,128)}), f32[64,8,256]{2,1,0:T(8,128)S(1)}, u32[]{:S(2)}, u32[]{:S(2)}) async-start(f32[64,8,256]{2,1,0:T(8,128)} %broadcast_in_dim.288), calls=%async_computation.1 | async-start | bytes 1048576 | tf_op jit(solution)/shard_map/all_to_all | solution.py:115
  66.9 2.6 %gather_fusion.1 = f32[1536,128]{1,0:T(8,128)S(1)} fusion(f32[1024,128]{1,0:T(8,128)S(1)} %bitcast.108, s32[2048]{0:T(1024)S(1)} %pad_clamp_fusion), kind=kCustom, calls=%fused_computation.1 | custom fusion | bytes 1579008 | tf_op jit(solution)/shard_map/gather | solution.py:91
  69.9 0.6 fusion.26
  71.3 1.1 pad_maximum_fusion
  72.4 14.6 %all-to-all-done.1 = f32[64,8,256]{2,1,0:T(8,128)S(1)} async-done(((f32[64,8,256]{2,1,0:T(8,128)}), f32[64,8,256]{2,1,0:T(8,128)S(1)}, u32[]{:S(2)}, u32[]{:S(2)}) %all-to-all-start.1) | async-done | bytes 524320 | tf_op jit(solution)/shard_map/all_to_all | solution.py:115
  87.0 6.5 %all-to-all-start.2 = ((f32[64,8,396]{2,1,0:T(8,128)}), f32[64,8,396]{2,1,0:T(8,128)S(1)}, u32[]{:S(2)}, u32[]{:S(2)}) async-start(f32[64,8,396]{2,1,0:T(8,128)} %pad_maximum_fusion), calls=%async_computation.2 | async-start | bytes 2097152 | tf_op jit(solution)/shard_map/all_to_all | solution.py:120
  93.9 11.7 %cholesky.44 = f32[128,128]{1,0:T(8,128)S(1)} custom-call(f32[128,128]{1,0:T(8,128)S(1)} %fusion.22), custom_call_target="Cholesky" | custom-call | tf_op jit(solution)/shard_map/jit(cholesky)/cholesky | solution.py:18
  105.6 0.6 compare_reduce_fusion.1
  106.3 0.7 fusion.15
  107.0 9.8 %custom-call.8 = f32[1,128,128]{1,2,0:T(8,128)S(1)} custom-call(f32[1,128,128]{2,1,0:T(8,128)S(1)} %fusion.15), custom_call_target="InvertDiagBlocksLowerTriangular" | custom-call | tf_op jit(solution)/shard_map/jit(_solve_triangular)/triangular_solve | solution.py:19
  117.7 11.7 %cholesky.55 = f32[128,128]{1,0:T(8,128)S(1)} custom-call(f32[128,128]{1,0:T(8,128)S(1)} %fusion.20), custom_call_target="Cholesky" | custom-call | tf_op jit(solution)/shard_map/jit(cholesky)/cholesky | solution.py:21
  129.5 0.6 compare_reduce_fusion
  130.1 0.7 fusion.16
  130.8 10.0 %custom-call.9 = f32[1,128,128]{1,2,0:T(8,128)S(1)} custom-call(f32[1,128,128]{2,1,0:T(8,128)S(1)} %fusion.16), custom_call_target="InvertDiagBlocksLowerTriangular" | custom-call | tf_op jit(solution)/shard_map/jit(_solve_triangular)/triangular_solve | solution.py:22
  141.1 0.9 reshape.454
  142.1 0.4 copy.91
  142.5 0.4 reshape.494
  142.9 4.4 %concatenate.20 = f32[64,4,25,128]{3,2,1,0:T(8,128)} pad(f32[64,4,24,128]{3,2,1,0:T(8,128)} %bitcast.112, f32[]{:T(128)} %constant.65.clone.1), padding=0_0x0_0x0_1x0_0 | pad | bytes 6422532 | tf_op jit(solution)/shard_map/concatenate | solution.py:128
  147.3 2.9 %reshape.456 = f32[6400,128]{1,0:T(8,128)S(1)} reshape(f32[64,4,25,128]{3,2,1,0:T(8,128)} %concatenate.20) | data formatting | bytes 6553600 | tf_op jit(solution)/shard_map/reshape | solution.py:130
  150.2 20.9 %gather_fusion.4 = f32[6144,128]{1,0:T(8,128)} fusion(f32[6400,128]{1,0:T(8,128)S(1)} %reshape.456, s32[6144]{0:T(1024)S(1)} %broadcast_clamp_fusion), kind=kCustom, calls=%fused_computation.4 | custom fusion | bytes 6316032 | tf_op jit(solution)/shard_map/gather | solution.py:134
  171.1 2.9 %reshape.457 = f32[1536,512]{1,0:T(8,128)S(1)} reshape(f32[6144,128]{1,0:T(8,128)} %gather_fusion.4) | data formatting | bytes 6291456 | tf_op jit(solution)/shard_map/reshape | solution.py:135
  174.0 3.1 %fusion.34 = f32[128,512]{1,0:T(8,128)S(1)} fusion(f32[1536,128]{1,0:T(8,128)} %reshape.454, f32[1536,512]{1,0:T(8,128)S(1)} %reshape.457), kind=kOutput, calls=%fused_computation.114 | convolution fusion | flops 1207959552 | bytes 4194304 | tf_op jit(solution)/shard_map/si,sp->ip/dot_general | solution.py:135
  177.1 1.4 collective-permute-start.2
  179.1 5.6 %collective-permute-done.2 = f32[128,512]{1,0:T(8,128)S(1)} collective-permute-done((f32[128,512]{1,0:T(8,128)S(1)}, f32[128,512]{1,0:T(8,128)S(1)}, u32[]{:S(2)}, u32[]{:S(2)}) %collective-permute-start.2) | collective-permute-done | bytes 262176 | tf_op jit(solution)/shard_map/ppermute | solution.py:46
  184.7 3.1 %collective-permute-start.3 = (f32[128,512]{1,0:T(8,128)S(1)}, f32[128,512]{1,0:T(8,128)S(1)}, u32[]{:S(2)}, u32[]{:S(2)}) collective-permute-start(f32[128,512]{1,0:T(8,128)S(1)} %add.214), channel_id=1, source_target_pairs={{0,128},{64,192},{128,0},{192,64},{1,129},{65,193},{129,1},{193,65... | collective-permute-start | bytes 786440 | tf_op jit(solution)/shard_map/ppermute | solution.py:46
  188.1 1.4 fusion
  189.5 3.3 %collective-permute-done.3 = f32[128,512]{1,0:T(8,128)S(1)} collective-permute-done((f32[128,512]{1,0:T(8,128)S(1)}, f32[128,512]{1,0:T(8,128)S(1)}, u32[]{:S(2)}, u32[]{:S(2)}) %collective-permute-start.3) | collective-permute-done | bytes 262176 | tf_op jit(solution)/shard_map/ppermute | solution.py:46
  193.0 0.4 fusion.5
  193.4 1.1 slice_subtract_fusion
  (92 shorter events, 5.9 us)
Async XLA Ops:
  7.2 10.6 %copy-start.5 = (f32[128]{0:T(128)S(1)}, f32[128]{0:T(128)}, u32[]{:S(2)}) copy-start(f32[128]{0:T(128)} %param.10) | copy-start | bytes 1540
  7.2 135.7 %all-gather.2.cloned.1.call-start = ((), (), s32[]{:S(2)}) async-start(), calls=%async_computation.3 | async-start | bytes 3194880 | tf_op jit(solution)/shard_map/all_gather | solution.py:111
  9.7 22.7 %copy-start.3 = (s32[128,8]{0,1:T(8,128)S(1)}, s32[128,8]{0,1:T(8,128)}, u32[]{:S(2)}) copy-start(s32[128,8]{0,1:T(8,128)} %param.9) | copy-start | bytes 12292
  9.7 22.7 %copy-start.6 = (s32[64]{0:T(128)S(1)}, s32[64]{0:T(128)}, u32[]{:S(2)}) copy-start(s32[64]{0:T(128)} %param.11) | copy-start | bytes 772
  19.4 31.4 %all-to-all-start = ((f32[64,8,256]{2,1,0:T(8,128)}), f32[64,8,256]{2,1,0:T(8,128)S(1)}, u32[]{:S(2)}, u32[]{:S(2)}) async-start(f32[64,8,256]{2,1,0:T(8,128)} %fusion.3), calls=%async_computation | async-start | bytes 1048576 | tf_op jit(solution)/shard_map/all_to_all | solution.py:103
  39.9 26.9 %copy-start = (f32[128,8,128]{2,1,0:T(8,128)S(1)}, f32[128,8,128]{2,1,0:T(8,128)}, u32[]{:S(2)}) copy-start(f32[128,8,128]{2,1,0:T(8,128)} %param.8) | copy-start | bytes 1572868
  50.9 3.0 %collective-permute-start = (f32[8,256]{1,0:T(8,128)S(1)}, f32[8,256]{1,0:T(8,128)S(1)}, u32[]{:S(2)}, u32[]{:S(2)}) collective-permute-start(f32[8,256]{1,0:T(8,128)S(1)} %reduce_sum.74), channel_id=1, source_target_pairs={{0,64},{64,0},{128,192},{192,128},{1,65},{65,1},{129,193},{193,129... | collective-permute-start | bytes 24584 | tf_op jit(solution)/shard_map/ppermute | solution.py:46
  53.9 4.0 %collective-permute-start.1 = (f32[8,256]{1,0:T(8,128)S(1)}, f32[8,256]{1,0:T(8,128)S(1)}, u32[]{:S(2)}, u32[]{:S(2)}) collective-permute-start(f32[8,256]{1,0:T(8,128)S(1)} %add.195), channel_id=1, source_target_pairs={{0,128},{64,192},{128,0},{192,64},{1,129},{65,193},{129,1},{193,65... | collective-permute-start | bytes 24584 | tf_op jit(solution)/shard_map/ppermute | solution.py:46
  58.8 28.2 %all-to-all-start.1 = ((f32[64,8,256]{2,1,0:T(8,128)}), f32[64,8,256]{2,1,0:T(8,128)S(1)}, u32[]{:S(2)}, u32[]{:S(2)}) async-start(f32[64,8,256]{2,1,0:T(8,128)} %broadcast_in_dim.288), calls=%async_computation.1 | async-start | bytes 1048576 | tf_op jit(solution)/shard_map/all_to_all | solution.py:115
  69.7 23.8 %slice-start = ((f32[512]{0:T(512)}), f32[256]{0:T(256)S(1)}, s32[]{:S(2)}) async-start(f32[512]{0:T(512)} %param.12), calls=%async_computation.4 | async-start | bytes 2048 | tf_op jit(solution)/shard_map/slice | solution.py:125
  87.0 53.8 %all-to-all-start.2 = ((f32[64,8,396]{2,1,0:T(8,128)}), f32[64,8,396]{2,1,0:T(8,128)S(1)}, u32[]{:S(2)}, u32[]{:S(2)}) async-start(f32[64,8,396]{2,1,0:T(8,128)} %pad_maximum_fusion), calls=%async_computation.2 | async-start | bytes 2097152 | tf_op jit(solution)/shard_map/all_to_all | solution.py:120
  93.6 48.5 %copy-start.1 = (f32[512,256]{1,0:T(8,128)}, f32[512,256]{1,0:T(8,128)S(1)}, u32[]{:S(2)}) copy-start(f32[512,256]{1,0:T(8,128)S(1)} %select_add_fusion) | copy-start | bytes 1572868
  174.0 18.9 %copy-start.4 = (f32[512]{0:T(512)S(1)}, f32[512]{0:T(512)}, u32[]{:S(2)}) copy-start(f32[512]{0:T(512)} %param.12) | copy-start | bytes 6148
  177.1 7.5 %collective-permute-start.2 = (f32[128,512]{1,0:T(8,128)S(1)}, f32[128,512]{1,0:T(8,128)S(1)}, u32[]{:S(2)}, u32[]{:S(2)}) collective-permute-start(f32[128,512]{1,0:T(8,128)S(1)} %fusion.34), channel_id=1, source_target_pairs={{0,64},{64,0},{128,192},{192,128},{1,65},{65,1},{129,193},{193,129... | collective-permute-start | bytes 786440 | tf_op jit(solution)/shard_map/ppermute | solution.py:46
  184.7 8.2 %collective-permute-start.3 = (f32[128,512]{1,0:T(8,128)S(1)}, f32[128,512]{1,0:T(8,128)S(1)}, u32[]{:S(2)}, u32[]{:S(2)}) collective-permute-start(f32[128,512]{1,0:T(8,128)S(1)} %add.214), channel_id=1, source_target_pairs={{0,128},{64,192},{128,0},{192,64},{1,129},{65,193},{129,1},{193,65... | collective-permute-start | bytes 786440 | tf_op jit(solution)/shard_map/ppermute | solution.py:46
  193.4 1.1 copy-start.2
Sparse Core Ops, SparseCore 0:
  17.9 84.9 all-gather.1

commit v8 on v6

--- a/solution.py
+++ b/solution.py
@@ -54,7 +54,7 @@
     rank_range = jnp.arange(CAP, dtype=jnp.int32)
     sel = jnp.sum((cum[:, :, None] <= rank_range[None, None, :]).astype(jnp.int32), axis=0)
     valid = rank_range[None, :] < cum[-1][:, None]
-    return jnp.minimum(sel, labels.shape[0] - 1), valid
+    return jnp.minimum(sel, labels.shape[0] - 1), valid, jnp.where(hit > 0, cum - 1, CAP)
 
 
 def local(design_tiles, block_ids, obs_weight, block_owner, prior_weight):
@@ -105,13 +105,11 @@
     spread = jnp.broadcast_to(gram_part[None], (nb, gram_rows, half))
 
     panel_range = jnp.arange(panel_blocks, dtype=jnp.int32)
-    panel_sel, panel_valid = ranked(block_ids, panel_range)
+    panel_sel, panel_valid, panel_pos = ranked(block_ids, panel_range)
     panel_tiles = weighted.reshape(n_obs, panel_blocks, bw)[panel_sel, panel_range[:, None]]
     panel_tiles = jnp.where(panel_valid[:, :, None], panel_tiles, 0.0)
     shared = lax.all_gather(panel_tiles.reshape(-1, bw), "blk", axis=0, tiled=False)
 
-    panel_hit = jnp.sum((block_ids[:, :, None] == panel_range[None, None, :]).astype(jnp.int32), axis=1)
-    panel_pos = jnp.where(panel_hit > 0, jnp.cumsum(panel_hit, axis=0) - 1, CAP)
     slot_pos = jnp.where(valid[:, :, None], panel_pos[obs_sel], CAP).astype(jnp.float32)
     index_width = CAP * panel_blocks // gram_rows
     square = lax.all_to_all(spread, "blk", 0, 0, tiled=True).reshape(panel_cols, half)
@@ -129,7 +127,7 @@
 
     src_panel = shared.reshape(nb, panel_blocks, CAP, bw)
     match = (got_pos[:, :, :, None] == jnp.arange(CAP, dtype=jnp.int32)[None, None, None, :]).astype(jnp.float32)
-    slot_panel = jnp.einsum("srpq,spqc->srpc", match, src_panel, precision=HI)
+    slot_panel = jnp.einsum("srpq,spqc->srpc", match, src_panel, precision=lax.Precision.HIGH)
     owned = jnp.einsum("si,sp->ip", got_tiles, slot_panel.reshape(nb * CAP, panel_cols), precision=HI)
     my_block = jnp.sum(jnp.where(block_owner == my_j, block_range, 0))
 

time: 183 us -> 182 us (level)
  no operation moved by 1% of the time
where the time goes in v8:
time: 182 us; the launch traced here: 180 us
  other arithmetic  55.5 us (30%)
  starting transfers between devices  37.3 us (20%)
  waiting for transfers between devices  35.8 us (20%)
  local copies, waits for them, and re-layouts  24.6 us (14%)
  between operations  15.5 us (9%)
  matrix products  11.3 us (6%)
    all_to_all x1, waiting for transfers between devices, local(): lax.all_to_all(gram.reshape(nb, gram_rows, half), 'blk', 0, 0, tiled=True)  16.6 us
    all_to_all x1, waiting for transfers between devices, local(): lax.all_to_all(spread, 'blk', 0, 0, tiled=True).reshape(panel_cols, half)  13.5 us
    all_to_all x1, starting transfers between devices, local(): lax.all_to_all(gram.reshape(nb, gram_rows, half), 'blk', 0, 0, tiled=True)  13 us
    another operation x3, other arithmetic, factor_inverse(): high = jnp.linalg.cholesky(mirrored[n:, n:] - dot(left, left.T))  12.4 us
    another operation x3, other arithmetic, factor_inverse(): low = jnp.linalg.cholesky(mirrored[:n, :n])  12.4 us
    another operation x2, other arithmetic, factor_inverse(): high_inv = jax.scipy.linalg.solve_triangular(high, eye, lower=True)  10.7 us
    another operation x2, other arithmetic, factor_inverse(): low_inv = jax.scipy.linalg.solve_triangular(low, eye, lower=True)  10.5 us
    all_to_all x1, starting transfers between devices, local(): lax.all_to_all(spread, 'blk', 0, 0, tiled=True).reshape(panel_cols, half)  6.83 us
  transfers between devices with their start and end apart: 12, of which 6 were waited for; matrix products, arithmetic and copies ran while one was open for 37% of the time, Pallas kernels for 0%

profile of v8, /device:TPU:1, one launch (start us, length us, event | category | flops | bytes accessed | tf_op | source)
XLA Modules:
  0.0 180.2 jit_solution(13968318539321740701)
XLA Ops:
  7.2 0.7 convert_reduce_fusion.3
  7.9 1.0 slice_bitcast_fusion.11
  9.7 3.4 %fusion.37 = (f32[128,1,128]{2,1,0:T(1,128)S(1)}, f32[128,1,128]{2,1,0:T(1,128)S(1)}, f32[128,1,128]{2,1,0:T(1,128)S(1)}, f32[128,1,128]{2,1,0:T(1,128)S(1)}, f3...) fusion(f32[128,8,128]{2,1,0:T(8,128)} %param.8), kind=kLoop, calls=%fused_computation.125 | loop fusion | bytes 1048576 | tf_op jit(solution)/shard_map/slice | solution.py:37
  13.5 2.3 %broadcast_multiply_fusion = (f32[128,4,128]{2,1,0:T(4,128)S(1)}, f32[128,4,128]{2,1,0:T(4,128)S(1)}) fusion(f32[128]{0:T(128)} %param.10, f32[128,128]{1,0:T(8,128)S(1)} %bitcast.151, pred[128,4]{1,0:T(8,128)(4,1)S(1)} %get-tuple-element.38, f32[128,128]{1,0:T(8,128)S(1)} %bitcast.145, pred[128,4]{1,0:T(8,128)(4,1)S(1)} %get-tuple-element.39, ...), kind=kLoop, calls=%fused_computation.43 | loop fusion | flops 1048576 | bytes 1053184 | tf_op jit(solution)/shard_map/mul | solution.py:96
  15.7 1.2 gather_fusion.3
  17.0 0.7 bitcast_select_fusion
  18.0 1.4 fusion.6
  19.3 13.0 %all-to-all-start = ((f32[64,8,256]{2,1,0:T(8,128)}), f32[64,8,256]{2,1,0:T(8,128)S(1)}, u32[]{:S(2)}, u32[]{:S(2)}) async-start(f32[64,8,256]{2,1,0:T(8,128)} %fusion.6), calls=%async_computation | async-start | bytes 1048576 | tf_op jit(solution)/shard_map/all_to_all | solution.py:103
  32.8 1.2 convert_reduce_fusion
  34.1 16.6 %all-to-all-done = f32[64,8,256]{2,1,0:T(8,128)S(1)} async-done(((f32[64,8,256]{2,1,0:T(8,128)}), f32[64,8,256]{2,1,0:T(8,128)S(1)}, u32[]{:S(2)}, u32[]{:S(2)}) %all-to-all-start) | async-done | bytes 524320 | tf_op jit(solution)/shard_map/all_to_all | solution.py:103
  50.8 1.4 collective-permute-start
  52.3 2.6 %gather_fusion.2 = s32[1536,4]{1,0:T(8,128)S(1)} fusion(s32[128,4]{1,0:T(8,128)S(1)} %copy.78, s32[2048]{0:T(1024)S(1)} %pad_clamp_fusion.1), kind=kCustom, calls=%fused_computation.2 | custom fusion | bytes 55296 | tf_op jit(solution)/shard_map/gather | solution.py:113
  55.2 2.7 %collective-permute-start.1 = (f32[8,256]{1,0:T(8,128)S(1)}, f32[8,256]{1,0:T(8,128)S(1)}, u32[]{:S(2)}, u32[]{:S(2)}) collective-permute-start(f32[8,256]{1,0:T(8,128)S(1)} %add.224), channel_id=1, source_target_pairs={{0,128},{64,192},{128,0},{192,64},{1,129},{65,193},{129,1},{193,65... | collective-permute-start | bytes 24584 | tf_op jit(solution)/shard_map/ppermute | solution.py:46
  58.0 2.6 %gather_fusion = s32[1536,8]{1,0:T(8,128)S(1)} fusion(s32[128,8]{1,0:T(8,128)S(1)} %copy.75, s32[2048]{0:T(1024)S(1)} %pad_clamp_fusion.1), kind=kCustom, calls=%fused_computation | custom fusion | bytes 104448 | tf_op jit(solution)/shard_map/gather | solution.py:85
  60.7 0.8 broadcast_in_dim.286
  61.5 6.8 %all-to-all-start.1 = ((f32[64,8,256]{2,1,0:T(8,128)}), f32[64,8,256]{2,1,0:T(8,128)S(1)}, u32[]{:S(2)}, u32[]{:S(2)}) async-start(f32[64,8,256]{2,1,0:T(8,128)} %broadcast_in_dim.286), calls=%async_computation.1 | async-start | bytes 1048576 | tf_op jit(solution)/shard_map/all_to_all | solution.py:115
  68.3 1.2 select_reduce_fusion
  70.0 2.6 %gather_fusion.1 = f32[1536,128]{1,0:T(8,128)S(1)} fusion(f32[1024,128]{1,0:T(8,128)S(1)} %bitcast.133, s32[2048]{0:T(1024)S(1)} %pad_clamp_fusion), kind=kCustom, calls=%fused_computation.1 | custom fusion | bytes 1579008 | tf_op jit(solution)/shard_map/gather | solution.py:91
  73.1 0.6 fusion.29
  74.4 1.1 pad_maximum_fusion
  75.5 13.5 %all-to-all-done.1 = f32[64,8,256]{2,1,0:T(8,128)S(1)} async-done(((f32[64,8,256]{2,1,0:T(8,128)}), f32[64,8,256]{2,1,0:T(8,128)S(1)}, u32[]{:S(2)}, u32[]{:S(2)}) %all-to-all-start.1) | async-done | bytes 524320 | tf_op jit(solution)/shard_map/all_to_all | solution.py:115
  89.0 6.6 %all-to-all-start.2 = ((f32[64,8,396]{2,1,0:T(8,128)}), f32[64,8,396]{2,1,0:T(8,128)S(1)}, u32[]{:S(2)}, u32[]{:S(2)}) async-start(f32[64,8,396]{2,1,0:T(8,128)} %pad_maximum_fusion), calls=%async_computation.2 | async-start | bytes 2097152 | tf_op jit(solution)/shard_map/all_to_all | solution.py:120
  96.0 11.7 %cholesky.44 = f32[128,128]{1,0:T(8,128)S(1)} custom-call(f32[128,128]{1,0:T(8,128)S(1)} %fusion.24), custom_call_target="Cholesky" | custom-call | tf_op jit(solution)/shard_map/jit(cholesky)/cholesky | solution.py:18
  107.8 0.6 compare_reduce_fusion.1
  108.4 0.7 fusion.17
  109.1 9.8 %custom-call.8 = f32[1,128,128]{1,2,0:T(8,128)S(1)} custom-call(f32[1,128,128]{2,1,0:T(8,128)S(1)} %fusion.17), custom_call_target="InvertDiagBlocksLowerTriangular" | custom-call | tf_op jit(solution)/shard_map/jit(_solve_triangular)/triangular_solve | solution.py:19
  119.8 11.7 %cholesky.55 = f32[128,128]{1,0:T(8,128)S(1)} custom-call(f32[128,128]{1,0:T(8,128)S(1)} %fusion.22), custom_call_target="Cholesky" | custom-call | tf_op jit(solution)/shard_map/jit(cholesky)/cholesky | solution.py:21
  131.6 0.6 compare_reduce_fusion
  132.2 0.7 fusion.18
  132.9 10.0 %custom-call.9 = f32[1,128,128]{1,2,0:T(8,128)S(1)} custom-call(f32[1,128,128]{2,1,0:T(8,128)S(1)} %fusion.18), custom_call_target="InvertDiagBlocksLowerTriangular" | custom-call | tf_op jit(solution)/shard_map/jit(_solve_triangular)/triangular_solve | solution.py:22
  144.2 1.1 copy.81
  145.5 4.2 %fusion.1 = f32[64,24,4,128]{3,1,2,0:T(8,128)S(1)} fusion(f32[64,4,24,128]{3,2,1,0:T(8,128)} %bitcast.138, s32[64,24,4]{1,2,0:T(4,128)S(1)} %copy.85), kind=kOutput, calls=%fused_computation.6 | convolution fusion | flops 113393664 | bytes 6316032 | tf_op jit(solution)/shard_map/srpq,spqc->srpc/dot_general | solution.py:130
  149.8 2.5 %copy.86 = f32[64,24,4,128]{3,2,1,0:T(4,128)} copy(f32[64,24,4,128]{3,1,2,0:T(8,128)S(1)} %fusion.1) | data formatting | bytes 6291456 | tf_op jit(solution)/shard_map/srpq,spqc->srpc/transpose | solution.py:130
  152.2 3.3 %reshape.455 = f32[1536,512,1]{1,0,2:T(8,128)S(1)} reshape(f32[64,24,4,128]{3,2,1,0:T(4,128)} %copy.86) | data formatting | bytes 6291456 | tf_op jit(solution)/shard_map/reshape | solution.py:131
  155.6 3.0 %fusion.39 = f32[4,32,512]{2,1,0:T(8,128)S(1)} fusion(f32[4,32,1536]{2,1,0:T(8,128)} %bitcast.134, f32[1536,512,1]{1,0,2:T(8,128)S(1)} %reshape.455), kind=kOutput, calls=%fused_computation.127 | convolution fusion | flops 1207959552 | bytes 4194304 | tf_op jit(solution)/shard_map/si,sp->ip/dot_general | solution.py:131
  158.7 0.9 collective-permute-start.4
  159.6 1.3 collective-permute-start.3
  160.8 0.8 collective-permute-start.2
  161.6 0.4 fusion.3
  162.0 2.1 %collective-permute-done.3 = f32[32,512]{1,0:T(8,128)S(1)} collective-permute-done((f32[32,512]{1,0:T(8,128)S(1)}, f32[32,512]{1,0:T(8,128)S(1)}, u32[]{:S(2)}, u32[]{:S(2)}) %collective-permute-start.3) | collective-permute-done | bytes 65568 | tf_op jit(solution)/shard_map/ppermute | solution.py:141
  164.2 1.9 %collective-permute-done.2 = f32[32,512]{1,0:T(8,128)S(1)} collective-permute-done((f32[32,512]{1,0:T(8,128)S(1)}, f32[32,512]{1,0:T(8,128)S(1)}, u32[]{:S(2)}, u32[]{:S(2)}) %collective-permute-start.2) | collective-permute-done | bytes 65568 | tf_op jit(solution)/shard_map/ppermute | solution.py:141
  166.2 0.3 fusion.8
  166.5 0.3 convolution_subtract_fusion.1
  166.9 1.3 collective-permute-start.6
  168.2 2.7 %collective-permute-start.7 = (f32[32,512]{1,0:T(8,128)S(1)}, f32[32,512]{1,0:T(8,128)S(1)}, u32[]{:S(2)}, u32[]{:S(2)}) collective-permute-start(f32[32,512]{1,0:T(8,128)S(1)} %get-tuple-element.29), channel_id=1, source_target_pairs={{0,192},{64,0},{128,64},{192,128},{1,193},{65,1},{129,65},{193,129... | collective-permute-start | bytes 196616 | tf_op jit(solution)/shard_map/ppermute | solution.py:160
  170.9 0.8 collective-permute-done.6
  171.6 0.9 collective-permute-done.5
  172.6 0.7 fusion.38
  (101 shorter events, 6.4 us)
Async XLA Ops:
  7.2 10.6 %copy-start.5 = (f32[128]{0:T(128)S(1)}, f32[128]{0:T(128)}, u32[]{:S(2)}) copy-start(f32[128]{0:T(128)} %param.10) | copy-start | bytes 1540
  7.2 138.3 %all-gather.2.cloned.1.call-start = ((), (), s32[]{:S(2)}) async-start(), calls=%async_computation.3 | async-start | bytes 3194880 | tf_op jit(solution)/shard_map/all_gather | solution.py:111
  9.7 22.6 %copy-start.3 = (s32[128,8]{0,1:T(8,128)S(1)}, s32[128,8]{0,1:T(8,128)}, u32[]{:S(2)}) copy-start(s32[128,8]{0,1:T(8,128)} %param.9) | copy-start | bytes 12292
  9.7 22.6 %copy-start.6 = (s32[64]{0:T(128)S(1)}, s32[64]{0:T(128)}, u32[]{:S(2)}) copy-start(s32[64]{0:T(128)} %param.11) | copy-start | bytes 772
  19.3 31.4 %all-to-all-start = ((f32[64,8,256]{2,1,0:T(8,128)}), f32[64,8,256]{2,1,0:T(8,128)S(1)}, u32[]{:S(2)}, u32[]{:S(2)}) async-start(f32[64,8,256]{2,1,0:T(8,128)} %fusion.6), calls=%async_computation | async-start | bytes 1048576 | tf_op jit(solution)/shard_map/all_to_all | solution.py:103
  50.8 4.4 %collective-permute-start = (f32[8,256]{1,0:T(8,128)S(1)}, f32[8,256]{1,0:T(8,128)S(1)}, u32[]{:S(2)}, u32[]{:S(2)}) collective-permute-start(f32[8,256]{1,0:T(8,128)S(1)} %reduce_sum.74), channel_id=1, source_target_pairs={{0,64},{64,0},{128,192},{192,128},{1,65},{65,1},{129,193},{193,129... | collective-permute-start | bytes 24584 | tf_op jit(solution)/shard_map/ppermute | solution.py:46
  55.2 5.4 %collective-permute-start.1 = (f32[8,256]{1,0:T(8,128)S(1)}, f32[8,256]{1,0:T(8,128)S(1)}, u32[]{:S(2)}, u32[]{:S(2)}) collective-permute-start(f32[8,256]{1,0:T(8,128)S(1)} %add.224), channel_id=1, source_target_pairs={{0,128},{64,192},{128,0},{192,64},{1,129},{65,193},{129,1},{193,65... | collective-permute-start | bytes 24584 | tf_op jit(solution)/shard_map/ppermute | solution.py:46
  60.6 9.4 %copy-start = (f32[128,8,128]{2,1,0:T(8,128)S(1)}, f32[128,8,128]{2,1,0:T(8,128)}, u32[]{:S(2)}) copy-start(f32[128,8,128]{2,1,0:T(8,128)} %param.8) | copy-start | bytes 1572868
  61.5 27.6 %all-to-all-start.1 = ((f32[64,8,256]{2,1,0:T(8,128)}), f32[64,8,256]{2,1,0:T(8,128)S(1)}, u32[]{:S(2)}, u32[]{:S(2)}) async-start(f32[64,8,256]{2,1,0:T(8,128)} %broadcast_in_dim.286), calls=%async_computation.1 | async-start | bytes 1048576 | tf_op jit(solution)/shard_map/all_to_all | solution.py:115
  72.9 22.7 %slice-start = ((f32[512]{0:T(512)}), f32[256]{0:T(256)S(1)}, s32[]{:S(2)}) async-start(f32[512]{0:T(512)} %param.12), calls=%async_computation.4 | async-start | bytes 2048 | tf_op jit(solution)/shard_map/slice | solution.py:125
  89.0 54.8 %all-to-all-start.2 = ((f32[64,8,396]{2,1,0:T(8,128)}), f32[64,8,396]{2,1,0:T(8,128)S(1)}, u32[]{:S(2)}, u32[]{:S(2)}) async-start(f32[64,8,396]{2,1,0:T(8,128)} %pad_maximum_fusion), calls=%async_computation.2 | async-start | bytes 2097152 | tf_op jit(solution)/shard_map/all_to_all | solution.py:120
  95.7 48.4 %copy-start.1 = (f32[512,256]{1,0:T(8,128)}, f32[512,256]{1,0:T(8,128)S(1)}, u32[]{:S(2)}) copy-start(f32[512,256]{1,0:T(8,128)S(1)} %select_add_fusion) | copy-start | bytes 1572868
  155.5 6.0 %copy-start.2 = (f32[512,256]{1,0:T(8,128)S(1)}, f32[512,256]{1,0:T(8,128)}, u32[]{:S(2)}) copy-start(f32[512,256]{1,0:T(8,128)} %copy-done.1) | copy-start | bytes 1572868
  155.6 10.5 %copy-start.4 = (f32[512]{0:T(512)S(1)}, f32[512]{0:T(512)}, u32[]{:S(2)}) copy-start(f32[512]{0:T(512)} %param.12) | copy-start | bytes 6148
  158.7 3.4 %collective-permute-start.4 = (f32[32,512]{1,0:T(8,128)S(1)}, f32[32,512]{1,0:T(8,128)S(1)}, u32[]{:S(2)}, u32[]{:S(2)}) collective-permute-start(f32[32,512]{1,0:T(8,128)S(1)} %get-tuple-element.25), channel_id=1, source_target_pairs={{0,192},{64,0},{128,64},{192,128},{1,193},{65,1},{129,65},{193,129... | collective-permute-start | bytes 196616 | tf_op jit(solution)/shard_map/ppermute | solution.py:141
  159.6 4.6 %collective-permute-start.3 = (f32[32,512]{1,0:T(8,128)S(1)}, f32[32,512]{1,0:T(8,128)S(1)}, u32[]{:S(2)}, u32[]{:S(2)}) collective-permute-start(f32[32,512]{1,0:T(8,128)S(1)} %get-tuple-element.26), channel_id=1, source_target_pairs={{0,128},{64,192},{128,0},{192,64},{1,129},{65,193},{129,1},{193,65... | collective-permute-start | bytes 196616 | tf_op jit(solution)/shard_map/ppermute | solution.py:141
  160.8 5.2 %collective-permute-start.2 = (f32[32,512]{1,0:T(8,128)S(1)}, f32[32,512]{1,0:T(8,128)S(1)}, u32[]{:S(2)}, u32[]{:S(2)}) collective-permute-start(f32[32,512]{1,0:T(8,128)S(1)} %get-tuple-element.27), channel_id=1, source_target_pairs={{0,64},{64,128},{128,192},{192,0},{1,65},{65,129},{129,193},{193,1... | collective-permute-start | bytes 196616 | tf_op jit(solution)/shard_map/ppermute | solution.py:141
  166.9 4.7 %collective-permute-start.6 = (f32[32,512]{1,0:T(8,128)S(1)}, f32[32,512]{1,0:T(8,128)S(1)}, u32[]{:S(2)}, u32[]{:S(2)}) collective-permute-start(f32[32,512]{1,0:T(8,128)S(1)} %get-tuple-element.29), channel_id=1, source_target_pairs={{0,128},{64,192},{128,0},{192,64},{1,129},{65,193},{129,1},{193,65... | collective-permute-start | bytes 196616 | tf_op jit(solution)/shard_map/ppermute | solution.py:160
  168.2 4.3 %collective-permute-start.5 = (f32[32,512]{1,0:T(8,128)S(1)}, f32[32,512]{1,0:T(8,128)S(1)}, u32[]{:S(2)}, u32[]{:S(2)}) collective-permute-start(f32[32,512]{1,0:T(8,128)S(1)} %get-tuple-element.29), channel_id=1, source_target_pairs={{0,64},{64,128},{128,192},{192,0},{1,65},{65,129},{129,193},{193,1... | collective-permute-start | bytes 196616 | tf_op jit(solution)/shard_map/ppermute | solution.py:160
  168.2 4.3 %collective-permute-start.7 = (f32[32,512]{1,0:T(8,128)S(1)}, f32[32,512]{1,0:T(8,128)S(1)}, u32[]{:S(2)}, u32[]{:S(2)}) collective-permute-start(f32[32,512]{1,0:T(8,128)S(1)} %get-tuple-element.29), channel_id=1, source_target_pairs={{0,192},{64,0},{128,64},{192,128},{1,193},{65,1},{129,65},{193,129... | collective-permute-start | bytes 196616 | tf_op jit(solution)/shard_map/ppermute | solution.py:160
Sparse Core Ops, SparseCore 0:
  17.8 85.7 all-gather.1

commit v9 on v6

--- a/solution.py
+++ b/solution.py
@@ -130,7 +130,9 @@
     src_panel = shared.reshape(nb, panel_blocks, CAP, bw)
     match = (got_pos[:, :, :, None] == jnp.arange(CAP, dtype=jnp.int32)[None, None, None, :]).astype(jnp.float32)
     slot_panel = jnp.einsum("srpq,spqc->srpc", match, src_panel, precision=HI)
-    owned = jnp.einsum("si,sp->ip", got_tiles, slot_panel.reshape(nb * CAP, panel_cols), precision=HI)
+    owned = jnp.einsum(
+        "sri,srpc->ipc", got_tiles.reshape(nb, CAP, bw), slot_panel, precision=HI
+    ).reshape(bw, panel_cols)
     my_block = jnp.sum(jnp.where(block_owner == my_j, block_range, 0))
 
     n_obs_dev = lax.axis_size("obs")

time: 183 us -> 183 us (level)
    dot_general x1 -> x3, local copies, waits for them, and re-layouts: 1.15 us -> 5.28 us  [local(): jnp.einsum('sri,srpc->ipc', got_tiles.reshape(nb, CAP, bw), slot_panel, p...]
    reshape x2 -> x0, local copies, waits for them, and re-layouts: 3.36 us -> none  [the longest x1 3.31 us: local(): slot_panel.reshape(nb * CAP, panel_cols)]
    transpose x1 -> x0, local copies, waits for them, and re-layouts: 2.48 us -> none  [local(): slot_panel = jnp.einsum('srpq,spqc->srpc', match, src_panel, precision=HI)]
  transfers between devices with their start and end apart: 12 -> 12, of which waited for: 6 -> 7; matrix products, arithmetic and copies ran while one was open for 37% -> 37% of each run, Pallas kernels for 0% -> 0%
where the time goes in v9:
time: 183 us; the launch traced here: 180 us
  other arithmetic  55.5 us (30%)
  starting transfers between devices  37.1 us (20%)
  waiting for transfers between devices  35.6 us (19%)
  local copies, waits for them, and re-layouts  23.1 us (13%)
  between operations  15.5 us (8%)
  matrix products  13.6 us (7%)
    all_to_all x1, waiting for transfers between devices, local(): lax.all_to_all(gram.reshape(nb, gram_rows, half), 'blk', 0, 0, tiled=True)  16.6 us
    all_to_all x1, waiting for transfers between devices, local(): lax.all_to_all(spread, 'blk', 0, 0, tiled=True).reshape(panel_cols, half)  13.4 us
    all_to_all x1, starting transfers between devices, local(): lax.all_to_all(gram.reshape(nb, gram_rows, half), 'blk', 0, 0, tiled=True)  13 us
    another operation x3, other arithmetic, factor_inverse(): low = jnp.linalg.cholesky(mirrored[:n, :n])  12.4 us
    another operation x3, other arithmetic, factor_inverse(): high = jnp.linalg.cholesky(mirrored[n:, n:] - dot(left, left.T))  12.4 us
    another operation x2, other arithmetic, factor_inverse(): high_inv = jax.scipy.linalg.solve_triangular(high, eye, lower=True)  10.7 us
    another operation x2, other arithmetic, factor_inverse(): low_inv = jax.scipy.linalg.solve_triangular(low, eye, lower=True)  10.5 us
    all_to_all x1, starting transfers between devices, local(): got = lax.all_to_all(payload, 'blk', 0, 0, tiled=True)  6.75 us
  transfers between devices with their start and end apart: 12, of which 7 were waited for; matrix products, arithmetic and copies ran while one was open for 37% of the time, Pallas kernels for 0%

profile of v9, /device:TPU:1, one launch (start us, length us, event | category | flops | bytes accessed | tf_op | source)
XLA Modules:
  0.0 180.3 jit_solution(6759266238555404495)
XLA Ops:
  7.2 0.7 convert_reduce_fusion.3
  7.9 1.0 slice_bitcast_fusion.11
  9.7 3.5 %fusion.42 = (f32[128,1,128]{2,1,0:T(1,128)S(1)}, f32[128,1,128]{2,1,0:T(1,128)S(1)}, f32[128,1,128]{2,1,0:T(1,128)S(1)}, f32[128,1,128]{2,1,0:T(1,128)S(1)}, f3...) fusion(f32[128,8,128]{2,1,0:T(8,128)} %param.8), kind=kLoop, calls=%fused_computation.128 | loop fusion | bytes 1048576 | tf_op jit(solution)/shard_map/slice | solution.py:37
  13.6 2.3 %broadcast_multiply_fusion = (f32[128,4,128]{2,1,0:T(4,128)S(1)}, f32[128,4,128]{2,1,0:T(4,128)S(1)}) fusion(f32[128]{0:T(128)} %param.10, f32[128,128]{1,0:T(8,128)S(1)} %bitcast.155, pred[128,4]{1,0:T(8,128)(4,1)S(1)} %get-tuple-element.38, f32[128,128]{1,0:T(8,128)S(1)} %bitcast.149, pred[128,4]{1,0:T(8,128)(4,1)S(1)} %get-tuple-element.39, ...), kind=kLoop, calls=%fused_computation.46 | loop fusion | flops 1048576 | bytes 1053184 | tf_op jit(solution)/shard_map/mul | solution.py:96
  15.9 1.2 gather_fusion.3
  17.1 0.7 bitcast_select_fusion
  18.1 1.4 fusion.11
  19.5 13.0 %all-to-all-start = ((f32[64,8,256]{2,1,0:T(8,128)}), f32[64,8,256]{2,1,0:T(8,128)S(1)}, u32[]{:S(2)}, u32[]{:S(2)}) async-start(f32[64,8,256]{2,1,0:T(8,128)} %fusion.11), calls=%async_computation | async-start | bytes 1048576 | tf_op jit(solution)/shard_map/all_to_all | solution.py:103
  33.0 1.2 convert_reduce_fusion
  34.3 16.6 %all-to-all-done = f32[64,8,256]{2,1,0:T(8,128)S(1)} async-done(((f32[64,8,256]{2,1,0:T(8,128)}), f32[64,8,256]{2,1,0:T(8,128)S(1)}, u32[]{:S(2)}, u32[]{:S(2)}) %all-to-all-start) | async-done | bytes 524320 | tf_op jit(solution)/shard_map/all_to_all | solution.py:103
  50.9 1.4 collective-permute-start
  52.4 2.6 %gather_fusion.2 = s32[1536,4]{1,0:T(8,128)S(1)} fusion(s32[128,4]{1,0:T(8,128)S(1)} %copy.96, s32[2048]{0:T(1024)S(1)} %pad_clamp_fusion.1), kind=kCustom, calls=%fused_computation.2 | custom fusion | bytes 55296 | tf_op jit(solution)/shard_map/gather | solution.py:115
  55.4 2.7 %collective-permute-start.1 = (f32[8,256]{1,0:T(8,128)S(1)}, f32[8,256]{1,0:T(8,128)S(1)}, u32[]{:S(2)}, u32[]{:S(2)}) collective-permute-start(f32[8,256]{1,0:T(8,128)S(1)} %add.224), channel_id=1, source_target_pairs={{0,128},{64,192},{128,0},{192,64},{1,129},{65,193},{129,1},{193,65... | collective-permute-start | bytes 24584 | tf_op jit(solution)/shard_map/ppermute | solution.py:46
  58.2 2.6 %gather_fusion = s32[1536,8]{1,0:T(8,128)S(1)} fusion(s32[128,8]{1,0:T(8,128)S(1)} %copy.93, s32[2048]{0:T(1024)S(1)} %pad_clamp_fusion.1), kind=kCustom, calls=%fused_computation | custom fusion | bytes 104448 | tf_op jit(solution)/shard_map/gather | solution.py:85
  60.8 0.8 broadcast_in_dim.288
  61.6 6.7 %all-to-all-start.1 = ((f32[64,8,256]{2,1,0:T(8,128)}), f32[64,8,256]{2,1,0:T(8,128)S(1)}, u32[]{:S(2)}, u32[]{:S(2)}) async-start(f32[64,8,256]{2,1,0:T(8,128)} %broadcast_in_dim.288), calls=%async_computation.1 | async-start | bytes 1048576 | tf_op jit(solution)/shard_map/all_to_all | solution.py:117
  68.4 1.2 select_reduce_fusion
  70.1 2.6 %gather_fusion.1 = f32[1536,128]{1,0:T(8,128)S(1)} fusion(f32[1024,128]{1,0:T(8,128)S(1)} %bitcast.137, s32[2048]{0:T(1024)S(1)} %pad_clamp_fusion), kind=kCustom, calls=%fused_computation.1 | custom fusion | bytes 1579008 | tf_op jit(solution)/shard_map/gather | solution.py:91
  73.2 0.6 fusion.34
  74.5 1.1 pad_maximum_fusion
  75.6 13.4 %all-to-all-done.1 = f32[64,8,256]{2,1,0:T(8,128)S(1)} async-done(((f32[64,8,256]{2,1,0:T(8,128)}), f32[64,8,256]{2,1,0:T(8,128)S(1)}, u32[]{:S(2)}, u32[]{:S(2)}) %all-to-all-start.1) | async-done | bytes 524320 | tf_op jit(solution)/shard_map/all_to_all | solution.py:117
  89.0 6.8 %all-to-all-start.2 = ((f32[64,8,396]{2,1,0:T(8,128)}), f32[64,8,396]{2,1,0:T(8,128)S(1)}, u32[]{:S(2)}, u32[]{:S(2)}) async-start(f32[64,8,396]{2,1,0:T(8,128)} %pad_maximum_fusion), calls=%async_computation.2 | async-start | bytes 2097152 | tf_op jit(solution)/shard_map/all_to_all | solution.py:122
  96.2 11.7 %cholesky.44 = f32[128,128]{1,0:T(8,128)S(1)} custom-call(f32[128,128]{1,0:T(8,128)S(1)} %fusion.29), custom_call_target="Cholesky" | custom-call | tf_op jit(solution)/shard_map/jit(cholesky)/cholesky | solution.py:18
  107.9 0.6 compare_reduce_fusion.1
  108.6 0.7 fusion.22
  109.2 9.8 %custom-call.8 = f32[1,128,128]{1,2,0:T(8,128)S(1)} custom-call(f32[1,128,128]{2,1,0:T(8,128)S(1)} %fusion.22), custom_call_target="InvertDiagBlocksLowerTriangular" | custom-call | tf_op jit(solution)/shard_map/jit(_solve_triangular)/triangular_solve | solution.py:19
  120.0 11.7 %cholesky.55 = f32[128,128]{1,0:T(8,128)S(1)} custom-call(f32[128,128]{1,0:T(8,128)S(1)} %fusion.27), custom_call_target="Cholesky" | custom-call | tf_op jit(solution)/shard_map/jit(cholesky)/cholesky | solution.py:21
  131.8 0.6 compare_reduce_fusion
  132.4 0.7 fusion.23
  133.1 10.0 %custom-call.9 = f32[1,128,128]{1,2,0:T(8,128)S(1)} custom-call(f32[1,128,128]{2,1,0:T(8,128)S(1)} %fusion.23), custom_call_target="InvertDiagBlocksLowerTriangular" | custom-call | tf_op jit(solution)/shard_map/jit(_solve_triangular)/triangular_solve | solution.py:22
  144.5 1.6 copy.99
  146.1 4.9 %fusion.1 = f32[4,128,24,64]{1,2,0,3:T(8,128)S(1)} fusion(f32[64,4,24,128]{3,2,1,0:T(8,128)} %bitcast.142, s32[64,24,4]{1,2,0:T(4,128)S(1)} %copy.103), kind=kOutput, calls=%fused_computation.6 | convolution fusion | flops 226639872 | bytes 6316032 | tf_op jit(solution)/shard_map/srpq,spqc->srpc/dot_general | solution.py:132
  151.0 0.8 copy.104
  151.9 2.8 %reshape.447 = f32[512,24,64,1]{0,2,1,3:T(8,128)} reshape(f32[4,128,24,64]{1,0,3,2:T(4,128)S(1)} %copy.104) | data formatting | bytes 6291456 | tf_op jit(solution)/shard_map/sri,srpc->ipc/dot_general | solution.py:133
  154.7 4.6 %fusion.5 = f32[4,32,512]{2,1,0:T(8,128)S(1)} fusion(f32[512,24,64,1]{0,2,1,3:T(8,128)} %reshape.447, f32[4,32,24,64]{3,2,1,0:T(8,128)} %bitcast.138), kind=kOutput, calls=%fused_computation.10 | convolution fusion | flops 1207959552 | bytes 4194304 | tf_op jit(solution)/shard_map/sri,srpc->ipc/dot_general | solution.py:133
  159.4 0.8 collective-permute-start.4
  160.2 1.1 collective-permute-start.3
  161.3 0.8 collective-permute-start.2
  162.1 0.4 fusion.8
  162.6 2.3 %collective-permute-done.3 = f32[32,512]{1,0:T(8,128)S(1)} collective-permute-done((f32[32,512]{1,0:T(8,128)S(1)}, f32[32,512]{1,0:T(8,128)S(1)}, u32[]{:S(2)}, u32[]{:S(2)}) %collective-permute-start.3) | collective-permute-done | bytes 65568 | tf_op jit(solution)/shard_map/ppermute | solution.py:145
  164.8 1.5 collective-permute-done.2
  166.8 0.3 convolution_subtract_fusion.1
  167.2 1.2 collective-permute-start.6
  168.4 0.4 collective-permute-start.5
  168.8 2.2 %collective-permute-start.7 = (f32[32,512]{1,0:T(8,128)S(1)}, f32[32,512]{1,0:T(8,128)S(1)}, u32[]{:S(2)}, u32[]{:S(2)}) collective-permute-start(f32[32,512]{1,0:T(8,128)S(1)} %get-tuple-element.29), channel_id=1, source_target_pairs={{0,192},{64,0},{128,64},{192,128},{1,193},{65,1},{129,65},{193,129... | collective-permute-start | bytes 196616 | tf_op jit(solution)/shard_map/ppermute | solution.py:164
  171.0 0.8 collective-permute-done.6
  171.9 0.8 collective-permute-done.5
  172.8 0.7 fusion.43
  (101 shorter events, 6.8 us)
Async XLA Ops:
  7.2 10.7 %copy-start.5 = (f32[128]{0:T(128)S(1)}, f32[128]{0:T(128)}, u32[]{:S(2)}) copy-start(f32[128]{0:T(128)} %param.10) | copy-start | bytes 1540
  7.2 139.0 %all-gather.2.cloned.1.call-start = ((), (), s32[]{:S(2)}) async-start(), calls=%async_computation.3 | async-start | bytes 3194880 | tf_op jit(solution)/shard_map/all_gather | solution.py:111
  9.7 22.8 %copy-start.3 = (s32[128,8]{0,1:T(8,128)S(1)}, s32[128,8]{0,1:T(8,128)}, u32[]{:S(2)}) copy-start(s32[128,8]{0,1:T(8,128)} %param.9) | copy-start | bytes 12292
  9.7 22.8 %copy-start.6 = (s32[64]{0:T(128)S(1)}, s32[64]{0:T(128)}, u32[]{:S(2)}) copy-start(s32[64]{0:T(128)} %param.11) | copy-start | bytes 772
  19.5 31.4 %all-to-all-start = ((f32[64,8,256]{2,1,0:T(8,128)}), f32[64,8,256]{2,1,0:T(8,128)S(1)}, u32[]{:S(2)}, u32[]{:S(2)}) async-start(f32[64,8,256]{2,1,0:T(8,128)} %fusion.11), calls=%async_computation | async-start | bytes 1048576 | tf_op jit(solution)/shard_map/all_to_all | solution.py:103
  50.9 4.4 %collective-permute-start = (f32[8,256]{1,0:T(8,128)S(1)}, f32[8,256]{1,0:T(8,128)S(1)}, u32[]{:S(2)}, u32[]{:S(2)}) collective-permute-start(f32[8,256]{1,0:T(8,128)S(1)} %reduce_sum.78), channel_id=1, source_target_pairs={{0,64},{64,0},{128,192},{192,128},{1,65},{65,1},{129,193},{193,129... | collective-permute-start | bytes 24584 | tf_op jit(solution)/shard_map/ppermute | solution.py:46
  55.4 5.4 %collective-permute-start.1 = (f32[8,256]{1,0:T(8,128)S(1)}, f32[8,256]{1,0:T(8,128)S(1)}, u32[]{:S(2)}, u32[]{:S(2)}) collective-permute-start(f32[8,256]{1,0:T(8,128)S(1)} %add.224), channel_id=1, source_target_pairs={{0,128},{64,192},{128,0},{192,64},{1,129},{65,193},{129,1},{193,65... | collective-permute-start | bytes 24584 | tf_op jit(solution)/shard_map/ppermute | solution.py:46
  60.8 9.3 %copy-start = (f32[128,8,128]{2,1,0:T(8,128)S(1)}, f32[128,8,128]{2,1,0:T(8,128)}, u32[]{:S(2)}) copy-start(f32[128,8,128]{2,1,0:T(8,128)} %param.8) | copy-start | bytes 1572868
  61.6 27.4 %all-to-all-start.1 = ((f32[64,8,256]{2,1,0:T(8,128)}), f32[64,8,256]{2,1,0:T(8,128)S(1)}, u32[]{:S(2)}, u32[]{:S(2)}) async-start(f32[64,8,256]{2,1,0:T(8,128)} %broadcast_in_dim.288), calls=%async_computation.1 | async-start | bytes 1048576 | tf_op jit(solution)/shard_map/all_to_all | solution.py:117
  72.9 22.8 %slice-start = ((f32[512]{0:T(512)}), f32[256]{0:T(256)S(1)}, s32[]{:S(2)}) async-start(f32[512]{0:T(512)} %param.12), calls=%async_computation.4 | async-start | bytes 2048 | tf_op jit(solution)/shard_map/slice | solution.py:127
  89.0 55.0 %all-to-all-start.2 = ((f32[64,8,396]{2,1,0:T(8,128)}), f32[64,8,396]{2,1,0:T(8,128)S(1)}, u32[]{:S(2)}, u32[]{:S(2)}) async-start(f32[64,8,396]{2,1,0:T(8,128)} %pad_maximum_fusion), calls=%async_computation.2 | async-start | bytes 2097152 | tf_op jit(solution)/shard_map/all_to_all | solution.py:122
  95.8 48.4 %copy-start.1 = (f32[512,256]{1,0:T(8,128)}, f32[512,256]{1,0:T(8,128)S(1)}, u32[]{:S(2)}) copy-start(f32[512,256]{1,0:T(8,128)S(1)} %select_add_fusion) | copy-start | bytes 1572868
  154.7 7.4 %copy-start.2 = (f32[512,256]{1,0:T(8,128)S(1)}, f32[512,256]{1,0:T(8,128)}, u32[]{:S(2)}) copy-start(f32[512,256]{1,0:T(8,128)} %copy-done.1) | copy-start | bytes 1572868
  154.7 11.7 %copy-start.4 = (f32[512]{0:T(512)S(1)}, f32[512]{0:T(512)}, u32[]{:S(2)}) copy-start(f32[512]{0:T(512)} %param.12) | copy-start | bytes 6148
  159.4 3.2 %collective-permute-start.4 = (f32[32,512]{1,0:T(8,128)S(1)}, f32[32,512]{1,0:T(8,128)S(1)}, u32[]{:S(2)}, u32[]{:S(2)}) collective-permute-start(f32[32,512]{1,0:T(8,128)S(1)} %get-tuple-element.25), channel_id=1, source_target_pairs={{0,192},{64,0},{128,64},{192,128},{1,193},{65,1},{129,65},{193,129... | collective-permute-start | bytes 196616 | tf_op jit(solution)/shard_map/ppermute | solution.py:145
  160.2 4.6 %collective-permute-start.3 = (f32[32,512]{1,0:T(8,128)S(1)}, f32[32,512]{1,0:T(8,128)S(1)}, u32[]{:S(2)}, u32[]{:S(2)}) collective-permute-start(f32[32,512]{1,0:T(8,128)S(1)} %get-tuple-element.26), channel_id=1, source_target_pairs={{0,128},{64,192},{128,0},{192,64},{1,129},{65,193},{129,1},{193,65... | collective-permute-start | bytes 196616 | tf_op jit(solution)/shard_map/ppermute | solution.py:145
  161.3 5.0 %collective-permute-start.2 = (f32[32,512]{1,0:T(8,128)S(1)}, f32[32,512]{1,0:T(8,128)S(1)}, u32[]{:S(2)}, u32[]{:S(2)}) collective-permute-start(f32[32,512]{1,0:T(8,128)S(1)} %get-tuple-element.27), channel_id=1, source_target_pairs={{0,64},{64,128},{128,192},{192,0},{1,65},{65,129},{129,193},{193,1... | collective-permute-start | bytes 196616 | tf_op jit(solution)/shard_map/ppermute | solution.py:145
  167.2 4.7 %collective-permute-start.6 = (f32[32,512]{1,0:T(8,128)S(1)}, f32[32,512]{1,0:T(8,128)S(1)}, u32[]{:S(2)}, u32[]{:S(2)}) collective-permute-start(f32[32,512]{1,0:T(8,128)S(1)} %get-tuple-element.29), channel_id=1, source_target_pairs={{0,128},{64,192},{128,0},{192,64},{1,129},{65,193},{129,1},{193,65... | collective-permute-start | bytes 196616 | tf_op jit(solution)/shard_map/ppermute | solution.py:164
  168.4 4.3 %collective-permute-start.5 = (f32[32,512]{1,0:T(8,128)S(1)}, f32[32,512]{1,0:T(8,128)S(1)}, u32[]{:S(2)}, u32[]{:S(2)}) collective-permute-start(f32[32,512]{1,0:T(8,128)S(1)} %get-tuple-element.29), channel_id=1, source_target_pairs={{0,64},{64,128},{128,192},{192,0},{1,65},{65,129},{129,193},{193,1... | collective-permute-start | bytes 196616 | tf_op jit(solution)/shard_map/ppermute | solution.py:164
  168.8 3.9 %collective-permute-start.7 = (f32[32,512]{1,0:T(8,128)S(1)}, f32[32,512]{1,0:T(8,128)S(1)}, u32[]{:S(2)}, u32[]{:S(2)}) collective-permute-start(f32[32,512]{1,0:T(8,128)S(1)} %get-tuple-element.29), channel_id=1, source_target_pairs={{0,192},{64,0},{128,64},{192,128},{1,193},{65,1},{129,65},{193,129... | collective-permute-start | bytes 196616 | tf_op jit(solution)/shard_map/ppermute | solution.py:164
Sparse Core Ops, SparseCore 0:
  18.0 85.8 all-gather.1

commit v10 on v9

--- a/solution.py
+++ b/solution.py
@@ -40,12 +40,13 @@
 
 def obs_butterfly(x):
     n = lax.axis_size("obs")
-    step = 1
-    while step < n:
-        perm = [(i, i ^ step) for i in range(n)]
-        x = x + lax.ppermute(x, "obs", perm)
-        step *= 2
-    return x
+    me = lax.axis_index("obs")
+    got = [x] + [lax.ppermute(x, "obs", [(i, (i + s) % n) for i in range(n)]) for s in range(1, n)]
+    ordered = jnp.stack(got)
+    parts = [ordered[(me - src) % n] for src in range(n)]
+    while len(parts) > 1:
+        parts = [parts[i] + parts[i + 1] for i in range(0, len(parts), 2)]
+    return parts[0]
 
 
 def ranked(labels, wanted):

time: 183 us -> 180 us (0.984)
  waiting for transfers between devices: 35.6 us -> 33.3 us
    all_to_all x1, waiting for transfers between devices: 16.6 us -> 13.5 us  [local(): lax.all_to_all(gram.reshape(nb, gram_rows, half), 'blk', 0, 0, tiled=True)]
    ppermute x2 -> x3, starting transfers between devices: 4.06 us -> 3.82 us  [obs_butterfly(): lax.ppermute(x, 'obs', [(i, (i + s) % n) for i in range(n)])]
  transfers between devices with their start and end apart: 12 -> 13, of which waited for: 7 -> 9; matrix products, arithmetic and copies ran while one was open for 37% -> 38% of each run, Pallas kernels for 0% -> 0%
where the time goes in v10:
time: 180 us; the launch traced here: 178 us
  other arithmetic  55.5 us (31%)
  starting transfers between devices  36.6 us (20%)
  waiting for transfers between devices  33.3 us (18%)
  local copies, waits for them, and re-layouts  23.1 us (13%)
  between operations  15.5 us (9%)
  matrix products  13.6 us (8%)
    all_to_all x1, waiting for transfers between devices, local(): lax.all_to_all(gram.reshape(nb, gram_rows, half), 'blk', 0, 0, tiled=True)  13.5 us
    all_to_all x1, starting transfers between devices, local(): lax.all_to_all(gram.reshape(nb, gram_rows, half), 'blk', 0, 0, tiled=True)  13 us
    all_to_all x1, waiting for transfers between devices, local(): lax.all_to_all(spread, 'blk', 0, 0, tiled=True).reshape(panel_cols, half)  12.9 us
    another operation x3, other arithmetic, factor_inverse(): high = jnp.linalg.cholesky(mirrored[n:, n:] - dot(left, left.T))  12.4 us
    another operation x3, other arithmetic, factor_inverse(): low = jnp.linalg.cholesky(mirrored[:n, :n])  12.4 us
    another operation x2, other arithmetic, factor_inverse(): high_inv = jax.scipy.linalg.solve_triangular(high, eye, lower=True)  10.7 us
    another operation x2, other arithmetic, factor_inverse(): low_inv = jax.scipy.linalg.solve_triangular(low, eye, lower=True)  10.5 us
    all_to_all x1, starting transfers between devices, local(): lax.all_to_all(spread, 'blk', 0, 0, tiled=True).reshape(panel_cols, half)  7.7 us
  transfers between devices with their start and end apart: 13, of which 9 were waited for; matrix products, arithmetic and copies ran while one was open for 38% of the time, Pallas kernels for 0%

profile of v10, /device:TPU:1, one launch (start us, length us, event | category | flops | bytes accessed | tf_op | source)
XLA Modules:
  0.0 177.6 jit_solution(3907939632282147872)
XLA Ops:
  7.2 0.7 convert_reduce_fusion.3
  7.9 1.0 slice_bitcast_fusion.11
  9.7 3.5 %fusion.42 = (f32[128,1,128]{2,1,0:T(1,128)S(1)}, f32[128,1,128]{2,1,0:T(1,128)S(1)}, f32[128,1,128]{2,1,0:T(1,128)S(1)}, f32[128,1,128]{2,1,0:T(1,128)S(1)}, f3...) fusion(f32[128,8,128]{2,1,0:T(8,128)} %param.8), kind=kLoop, calls=%fused_computation.130 | loop fusion | bytes 1048576 | tf_op jit(solution)/shard_map/slice | solution.py:37
  13.6 2.3 %broadcast_multiply_fusion = (f32[128,4,128]{2,1,0:T(4,128)S(1)}, f32[128,4,128]{2,1,0:T(4,128)S(1)}) fusion(f32[128]{0:T(128)} %param.10, f32[128,128]{1,0:T(8,128)S(1)} %bitcast.161, pred[128,4]{1,0:T(8,128)(4,1)S(1)} %get-tuple-element.38, f32[128,128]{1,0:T(8,128)S(1)} %bitcast.155, pred[128,4]{1,0:T(8,128)(4,1)S(1)} %get-tuple-element.39, ...), kind=kLoop, calls=%fused_computation.46 | loop fusion | flops 1048576 | bytes 1053184 | tf_op jit(solution)/shard_map/mul | solution.py:97
  15.9 1.2 gather_fusion.3
  17.1 0.7 bitcast_select_fusion
  18.1 1.4 fusion.11
  19.5 13.0 %all-to-all-start = ((f32[64,8,256]{2,1,0:T(8,128)}), f32[64,8,256]{2,1,0:T(8,128)S(1)}, u32[]{:S(2)}, u32[]{:S(2)}) async-start(f32[64,8,256]{2,1,0:T(8,128)} %fusion.11), calls=%async_computation | async-start | bytes 1048576 | tf_op jit(solution)/shard_map/all_to_all | solution.py:104
  33.0 1.2 convert_reduce_fusion
  34.4 2.6 %gather_fusion.2 = s32[1536,4]{1,0:T(8,128)S(1)} fusion(s32[128,4]{1,0:T(8,128)S(1)} %copy.96, s32[2048]{0:T(1024)S(1)} %pad_clamp_fusion.1), kind=kCustom, calls=%fused_computation.2 | custom fusion | bytes 55296 | tf_op jit(solution)/shard_map/gather | solution.py:116
  37.3 13.5 %all-to-all-done = f32[64,8,256]{2,1,0:T(8,128)S(1)} async-done(((f32[64,8,256]{2,1,0:T(8,128)}), f32[64,8,256]{2,1,0:T(8,128)S(1)}, u32[]{:S(2)}, u32[]{:S(2)}) %all-to-all-start) | async-done | bytes 524320 | tf_op jit(solution)/shard_map/all_to_all | solution.py:104
  50.9 2.8 %collective-permute-start.2 = (f32[8,256]{1,0:T(8,128)S(1)}, f32[8,256]{1,0:T(8,128)S(1)}, u32[]{:S(2)}, u32[]{:S(2)}) collective-permute-start(f32[8,256]{1,0:T(8,128)S(1)} %reduce_sum.78), channel_id=1, source_target_pairs={{0,192},{64,0},{128,64},{192,128},{1,193},{65,1},{129,65},{193,129... | collective-permute-start | bytes 24584 | tf_op jit(solution)/shard_map/ppermute | solution.py:44
  53.7 0.4 collective-permute-start.1
  54.1 0.7 collective-permute-start
  55.0 2.6 %gather_fusion = s32[1536,8]{1,0:T(8,128)S(1)} fusion(s32[128,8]{1,0:T(8,128)S(1)} %copy.93, s32[2048]{0:T(1024)S(1)} %pad_clamp_fusion.1), kind=kCustom, calls=%fused_computation | custom fusion | bytes 104448 | tf_op jit(solution)/shard_map/gather | solution.py:86
  58.0 0.8 broadcast_in_dim.291
  58.8 7.7 %all-to-all-start.1 = ((f32[64,8,256]{2,1,0:T(8,128)}), f32[64,8,256]{2,1,0:T(8,128)S(1)}, u32[]{:S(2)}, u32[]{:S(2)}) async-start(f32[64,8,256]{2,1,0:T(8,128)} %broadcast_in_dim.291), calls=%async_computation.1 | async-start | bytes 1048576 | tf_op jit(solution)/shard_map/all_to_all | solution.py:118
  66.5 1.2 select_reduce_fusion
  68.1 2.6 %gather_fusion.1 = f32[1536,128]{1,0:T(8,128)S(1)} fusion(f32[1024,128]{1,0:T(8,128)S(1)} %bitcast.143, s32[2048]{0:T(1024)S(1)} %pad_clamp_fusion), kind=kCustom, calls=%fused_computation.1 | custom fusion | bytes 1579008 | tf_op jit(solution)/shard_map/gather | solution.py:92
  71.2 0.6 fusion.34
  72.5 1.1 pad_maximum_fusion
  73.6 12.9 %all-to-all-done.1 = f32[64,8,256]{2,1,0:T(8,128)S(1)} async-done(((f32[64,8,256]{2,1,0:T(8,128)}), f32[64,8,256]{2,1,0:T(8,128)S(1)}, u32[]{:S(2)}, u32[]{:S(2)}) %all-to-all-start.1) | async-done | bytes 524320 | tf_op jit(solution)/shard_map/all_to_all | solution.py:118
  86.5 6.5 %all-to-all-start.2 = ((f32[64,8,396]{2,1,0:T(8,128)}), f32[64,8,396]{2,1,0:T(8,128)S(1)}, u32[]{:S(2)}, u32[]{:S(2)}) async-start(f32[64,8,396]{2,1,0:T(8,128)} %pad_maximum_fusion), calls=%async_computation.2 | async-start | bytes 2097152 | tf_op jit(solution)/shard_map/all_to_all | solution.py:123
  93.4 11.7 %cholesky.44 = f32[128,128]{1,0:T(8,128)S(1)} custom-call(f32[128,128]{1,0:T(8,128)S(1)} %fusion.29), custom_call_target="Cholesky" | custom-call | tf_op jit(solution)/shard_map/jit(cholesky)/cholesky | solution.py:18
  105.2 0.6 compare_reduce_fusion.1
  105.8 0.7 fusion.22
  106.5 9.8 %custom-call.8 = f32[1,128,128]{1,2,0:T(8,128)S(1)} custom-call(f32[1,128,128]{2,1,0:T(8,128)S(1)} %fusion.22), custom_call_target="InvertDiagBlocksLowerTriangular" | custom-call | tf_op jit(solution)/shard_map/jit(_solve_triangular)/triangular_solve | solution.py:19
  117.3 11.7 %cholesky.55 = f32[128,128]{1,0:T(8,128)S(1)} custom-call(f32[128,128]{1,0:T(8,128)S(1)} %fusion.27), custom_call_target="Cholesky" | custom-call | tf_op jit(solution)/shard_map/jit(cholesky)/cholesky | solution.py:21
  129.0 0.6 compare_reduce_fusion
  129.7 0.7 fusion.23
  130.3 10.0 %custom-call.9 = f32[1,128,128]{1,2,0:T(8,128)S(1)} custom-call(f32[1,128,128]{2,1,0:T(8,128)S(1)} %fusion.23), custom_call_target="InvertDiagBlocksLowerTriangular" | custom-call | tf_op jit(solution)/shard_map/jit(_solve_triangular)/triangular_solve | solution.py:22
  141.8 1.6 copy.99
  143.4 4.9 %fusion.1 = f32[4,128,24,64]{1,2,0,3:T(8,128)S(1)} fusion(f32[64,4,24,128]{3,2,1,0:T(8,128)} %bitcast.148, s32[64,24,4]{1,2,0:T(4,128)S(1)} %copy.103), kind=kOutput, calls=%fused_computation.6 | convolution fusion | flops 226639872 | bytes 6316032 | tf_op jit(solution)/shard_map/srpq,spqc->srpc/dot_general | solution.py:133
  148.3 0.8 copy.104
  149.1 2.8 %reshape.446 = f32[512,24,64,1]{0,2,1,3:T(8,128)} reshape(f32[4,128,24,64]{1,0,3,2:T(4,128)S(1)} %copy.104) | data formatting | bytes 6291456 | tf_op jit(solution)/shard_map/sri,srpc->ipc/dot_general | solution.py:134
  151.9 4.6 %fusion.5 = f32[4,32,512]{2,1,0:T(8,128)S(1)} fusion(f32[512,24,64,1]{0,2,1,3:T(8,128)} %reshape.446, f32[4,32,24,64]{3,2,1,0:T(8,128)} %bitcast.144), kind=kOutput, calls=%fused_computation.10 | convolution fusion | flops 1207959552 | bytes 4194304 | tf_op jit(solution)/shard_map/sri,srpc->ipc/dot_general | solution.py:134
  156.6 0.5 collective-permute-start.5
  157.2 1.7 collective-permute-start.4
  158.8 0.4 fusion.8
  159.2 0.6 collective-permute-done.5
  159.8 2.0 %collective-permute-done.4 = f32[32,512]{1,0:T(8,128)S(1)} collective-permute-done((f32[32,512]{1,0:T(8,128)S(1)}, f32[32,512]{1,0:T(8,128)S(1)}, u32[]{:S(2)}, u32[]{:S(2)}) %collective-permute-start.4) | collective-permute-done | bytes 65568 | tf_op jit(solution)/shard_map/ppermute | solution.py:146
  161.8 1.9 %collective-permute-done.3 = f32[32,512]{1,0:T(8,128)S(1)} collective-permute-done((f32[32,512]{1,0:T(8,128)S(1)}, f32[32,512]{1,0:T(8,128)S(1)}, u32[]{:S(2)}, u32[]{:S(2)}) %collective-permute-start.3) | collective-permute-done | bytes 65568 | tf_op jit(solution)/shard_map/ppermute | solution.py:146
  164.5 0.7 collective-permute-start.7
  165.2 0.6 collective-permute-start.6
  165.7 2.1 %collective-permute-start.8 = (f32[32,512]{1,0:T(8,128)S(1)}, f32[32,512]{1,0:T(8,128)S(1)}, u32[]{:S(2)}, u32[]{:S(2)}) collective-permute-start(f32[32,512]{1,0:T(8,128)S(1)} %get-tuple-element.29), channel_id=1, source_target_pairs={{0,192},{64,0},{128,64},{192,128},{1,193},{65,1},{129,65},{193,129... | collective-permute-start | bytes 196616 | tf_op jit(solution)/shard_map/ppermute | solution.py:165
  167.8 1.4 collective-permute-done.7
  169.2 0.7 collective-permute-done.6
  170.0 0.7 fusion.43
  (103 shorter events, 7.5 us)
Async XLA Ops:
  7.2 10.7 %copy-start.5 = (f32[128]{0:T(128)S(1)}, f32[128]{0:T(128)}, u32[]{:S(2)}) copy-start(f32[128]{0:T(128)} %param.10) | copy-start | bytes 1540
  7.2 136.2 %all-gather.2.cloned.1.call-start = ((), (), s32[]{:S(2)}) async-start(), calls=%async_computation.3 | async-start | bytes 3194880 | tf_op jit(solution)/shard_map/all_gather | solution.py:112
  9.7 22.8 %copy-start.3 = (s32[128,8]{0,1:T(8,128)S(1)}, s32[128,8]{0,1:T(8,128)}, u32[]{:S(2)}) copy-start(s32[128,8]{0,1:T(8,128)} %param.9) | copy-start | bytes 12292
  9.7 22.8 %copy-start.6 = (s32[64]{0:T(128)S(1)}, s32[64]{0:T(128)}, u32[]{:S(2)}) copy-start(s32[64]{0:T(128)} %param.11) | copy-start | bytes 772
  19.5 31.4 %all-to-all-start = ((f32[64,8,256]{2,1,0:T(8,128)}), f32[64,8,256]{2,1,0:T(8,128)S(1)}, u32[]{:S(2)}, u32[]{:S(2)}) async-start(f32[64,8,256]{2,1,0:T(8,128)} %fusion.11), calls=%async_computation | async-start | bytes 1048576 | tf_op jit(solution)/shard_map/all_to_all | solution.py:104
  50.9 6.7 %collective-permute-start.2 = (f32[8,256]{1,0:T(8,128)S(1)}, f32[8,256]{1,0:T(8,128)S(1)}, u32[]{:S(2)}, u32[]{:S(2)}) collective-permute-start(f32[8,256]{1,0:T(8,128)S(1)} %reduce_sum.78), channel_id=1, source_target_pairs={{0,192},{64,0},{128,64},{192,128},{1,193},{65,1},{129,65},{193,129... | collective-permute-start | bytes 24584 | tf_op jit(solution)/shard_map/ppermute | solution.py:44
  53.7 4.0 %collective-permute-start.1 = (f32[8,256]{1,0:T(8,128)S(1)}, f32[8,256]{1,0:T(8,128)S(1)}, u32[]{:S(2)}, u32[]{:S(2)}) collective-permute-start(f32[8,256]{1,0:T(8,128)S(1)} %reduce_sum.78), channel_id=1, source_target_pairs={{0,128},{64,192},{128,0},{192,64},{1,129},{65,193},{129,1},{193,65... | collective-permute-start | bytes 24584 | tf_op jit(solution)/shard_map/ppermute | solution.py:44
  54.1 3.9 %collective-permute-start = (f32[8,256]{1,0:T(8,128)S(1)}, f32[8,256]{1,0:T(8,128)S(1)}, u32[]{:S(2)}, u32[]{:S(2)}) collective-permute-start(f32[8,256]{1,0:T(8,128)S(1)} %reduce_sum.78), channel_id=1, source_target_pairs={{0,64},{64,128},{128,192},{192,0},{1,65},{65,129},{129,193},{193,1... | collective-permute-start | bytes 24584 | tf_op jit(solution)/shard_map/ppermute | solution.py:44
  57.6 10.6 %copy-start = (f32[128,8,128]{2,1,0:T(8,128)S(1)}, f32[128,8,128]{2,1,0:T(8,128)}, u32[]{:S(2)}) copy-start(f32[128,8,128]{2,1,0:T(8,128)} %param.8) | copy-start | bytes 1572868
  58.8 27.7 %all-to-all-start.1 = ((f32[64,8,256]{2,1,0:T(8,128)}), f32[64,8,256]{2,1,0:T(8,128)S(1)}, u32[]{:S(2)}, u32[]{:S(2)}) async-start(f32[64,8,256]{2,1,0:T(8,128)} %broadcast_in_dim.291), calls=%async_computation.1 | async-start | bytes 1048576 | tf_op jit(solution)/shard_map/all_to_all | solution.py:118
  71.0 22.0 %slice-start = ((f32[512]{0:T(512)}), f32[256]{0:T(256)S(1)}, s32[]{:S(2)}) async-start(f32[512]{0:T(512)} %param.12), calls=%async_computation.4 | async-start | bytes 2048 | tf_op jit(solution)/shard_map/slice | solution.py:128
  86.5 54.7 %all-to-all-start.2 = ((f32[64,8,396]{2,1,0:T(8,128)}), f32[64,8,396]{2,1,0:T(8,128)S(1)}, u32[]{:S(2)}, u32[]{:S(2)}) async-start(f32[64,8,396]{2,1,0:T(8,128)} %pad_maximum_fusion), calls=%async_computation.2 | async-start | bytes 2097152 | tf_op jit(solution)/shard_map/all_to_all | solution.py:123
  93.1 48.4 %copy-start.1 = (f32[512,256]{1,0:T(8,128)}, f32[512,256]{1,0:T(8,128)S(1)}, u32[]{:S(2)}) copy-start(f32[512,256]{1,0:T(8,128)S(1)} %select_add_fusion) | copy-start | bytes 1572868
  151.9 6.9 %copy-start.2 = (f32[512,256]{1,0:T(8,128)S(1)}, f32[512,256]{1,0:T(8,128)}, u32[]{:S(2)}) copy-start(f32[512,256]{1,0:T(8,128)} %copy-done.1) | copy-start | bytes 1572868
  151.9 11.8 %copy-start.4 = (f32[512]{0:T(512)S(1)}, f32[512]{0:T(512)}, u32[]{:S(2)}) copy-start(f32[512]{0:T(512)} %param.12) | copy-start | bytes 6148
  156.6 3.2 %collective-permute-start.5 = (f32[32,512]{1,0:T(8,128)S(1)}, f32[32,512]{1,0:T(8,128)S(1)}, u32[]{:S(2)}, u32[]{:S(2)}) collective-permute-start(f32[32,512]{1,0:T(8,128)S(1)} %get-tuple-element.25), channel_id=1, source_target_pairs={{0,192},{64,0},{128,64},{192,128},{1,193},{65,1},{129,65},{193,129... | collective-permute-start | bytes 196616 | tf_op jit(solution)/shard_map/ppermute | solution.py:146
  157.2 4.6 %collective-permute-start.4 = (f32[32,512]{1,0:T(8,128)S(1)}, f32[32,512]{1,0:T(8,128)S(1)}, u32[]{:S(2)}, u32[]{:S(2)}) collective-permute-start(f32[32,512]{1,0:T(8,128)S(1)} %get-tuple-element.26), channel_id=1, source_target_pairs={{0,128},{64,192},{128,0},{192,64},{1,129},{65,193},{129,1},{193,65... | collective-permute-start | bytes 196616 | tf_op jit(solution)/shard_map/ppermute | solution.py:146
  158.8 4.8 %collective-permute-start.3 = (f32[32,512]{1,0:T(8,128)S(1)}, f32[32,512]{1,0:T(8,128)S(1)}, u32[]{:S(2)}, u32[]{:S(2)}) collective-permute-start(f32[32,512]{1,0:T(8,128)S(1)} %get-tuple-element.27), channel_id=1, source_target_pairs={{0,64},{64,128},{128,192},{192,0},{1,65},{65,129},{129,193},{193,1... | collective-permute-start | bytes 196616 | tf_op jit(solution)/shard_map/ppermute | solution.py:146
  164.5 4.8 %collective-permute-start.7 = (f32[32,512]{1,0:T(8,128)S(1)}, f32[32,512]{1,0:T(8,128)S(1)}, u32[]{:S(2)}, u32[]{:S(2)}) collective-permute-start(f32[32,512]{1,0:T(8,128)S(1)} %get-tuple-element.29), channel_id=1, source_target_pairs={{0,128},{64,192},{128,0},{192,64},{1,129},{65,193},{129,1},{193,65... | collective-permute-start | bytes 196616 | tf_op jit(solution)/shard_map/ppermute | solution.py:165
  165.2 4.7 %collective-permute-start.6 = (f32[32,512]{1,0:T(8,128)S(1)}, f32[32,512]{1,0:T(8,128)S(1)}, u32[]{:S(2)}, u32[]{:S(2)}) collective-permute-start(f32[32,512]{1,0:T(8,128)S(1)} %get-tuple-element.29), channel_id=1, source_target_pairs={{0,64},{64,128},{128,192},{192,0},{1,65},{65,129},{129,193},{193,1... | collective-permute-start | bytes 196616 | tf_op jit(solution)/shard_map/ppermute | solution.py:165
  165.7 4.2 %collective-permute-start.8 = (f32[32,512]{1,0:T(8,128)S(1)}, f32[32,512]{1,0:T(8,128)S(1)}, u32[]{:S(2)}, u32[]{:S(2)}) collective-permute-start(f32[32,512]{1,0:T(8,128)S(1)} %get-tuple-element.29), channel_id=1, source_target_pairs={{0,192},{64,0},{128,64},{192,128},{1,193},{65,1},{129,65},{193,129... | collective-permute-start | bytes 196616 | tf_op jit(solution)/shard_map/ppermute | solution.py:165
Sparse Core Ops, SparseCore 0:
  18.0 85.3 all-gather.1

commit v11 on v10

--- a/solution.py
+++ b/solution.py
@@ -109,6 +109,7 @@
     panel_sel, panel_valid = ranked(block_ids, panel_range)
     panel_tiles = weighted.reshape(n_obs, panel_blocks, bw)[panel_sel, panel_range[:, None]]
     panel_tiles = jnp.where(panel_valid[:, :, None], panel_tiles, 0.0)
+    got_gram, panel_tiles = lax.optimization_barrier((got_gram, panel_tiles))
     shared = lax.all_gather(panel_tiles.reshape(-1, bw), "blk", axis=0, tiled=False)
 
     panel_hit = jnp.sum((block_ids[:, :, None] == panel_range[None, None, :]).astype(jnp.int32), axis=1)

time: 180 us -> 180 us (level)
    all_to_all x1, waiting for transfers between devices: 12.9 us -> 11 us  [local(): lax.all_to_all(spread, 'blk', 0, 0, tiled=True).reshape(panel_cols, half)]
where the time goes in v11:
time: 180 us; the launch traced here: 178 us
  other arithmetic  55.5 us (31%)
  starting transfers between devices  37.8 us (21%)
  waiting for transfers between devices  32.1 us (18%)
  local copies, waits for them, and re-layouts  23 us (13%)
  between operations  15.5 us (9%)
  matrix products  13.6 us (8%)
    all_to_all x1, waiting for transfers between devices, local(): lax.all_to_all(gram.reshape(nb, gram_rows, half), 'blk', 0, 0, tiled=True)  14.6 us
    all_to_all x1, starting transfers between devices, local(): lax.all_to_all(gram.reshape(nb, gram_rows, half), 'blk', 0, 0, tiled=True)  13 us
    another operation x3, other arithmetic, factor_inverse(): low = jnp.linalg.cholesky(mirrored[:n, :n])  12.4 us
    another operation x3, other arithmetic, factor_inverse(): high = jnp.linalg.cholesky(mirrored[n:, n:] - dot(left, left.T))  12.4 us
    all_to_all x1, waiting for transfers between devices, local(): lax.all_to_all(spread, 'blk', 0, 0, tiled=True).reshape(panel_cols, half)  11 us
    another operation x2, other arithmetic, factor_inverse(): high_inv = jax.scipy.linalg.solve_triangular(high, eye, lower=True)  10.7 us
    another operation x2, other arithmetic, factor_inverse(): low_inv = jax.scipy.linalg.solve_triangular(low, eye, lower=True)  10.5 us
    all_to_all x1, starting transfers between devices, local(): lax.all_to_all(spread, 'blk', 0, 0, tiled=True).reshape(panel_cols, half)  7.96 us
  transfers between devices with their start and end apart: 13, of which 9 were waited for; matrix products, arithmetic and copies ran while one was open for 38% of the time, Pallas kernels for 0%

profile of v11, /device:TPU:1, one launch (start us, length us, event | category | flops | bytes accessed | tf_op | source)
XLA Modules:
  0.0 177.5 jit_solution(15180218994620347737)
XLA Ops:
  7.2 1.0 slice_bitcast_fusion.11
  8.2 3.5 %fusion.42 = (f32[128,1,128]{2,1,0:T(1,128)S(1)}, f32[128,1,128]{2,1,0:T(1,128)S(1)}, f32[128,1,128]{2,1,0:T(1,128)S(1)}, f32[128,1,128]{2,1,0:T(1,128)S(1)}, f3...) fusion(f32[128,8,128]{2,1,0:T(8,128)} %param.8), kind=kLoop, calls=%fused_computation.130 | loop fusion | bytes 1048576 | tf_op jit(solution)/shard_map/slice | solution.py:37
  12.1 2.3 %broadcast_multiply_fusion = (f32[128,4,128]{2,1,0:T(4,128)S(1)}, f32[128,4,128]{2,1,0:T(4,128)S(1)}) fusion(f32[128]{0:T(128)} %param.10, f32[128,128]{1,0:T(8,128)S(1)} %bitcast.161, pred[128,4]{1,0:T(8,128)(4,1)S(1)} %get-tuple-element.40, f32[128,128]{1,0:T(8,128)S(1)} %bitcast.155, pred[128,4]{1,0:T(8,128)(4,1)S(1)} %get-tuple-element.41, ...), kind=kLoop, calls=%fused_computation.46 | loop fusion | flops 1048576 | bytes 1053184 | tf_op jit(solution)/shard_map/mul | solution.py:97
  14.4 0.7 multiply_bitcast_fusion
  15.3 1.4 fusion.11
  16.7 13.0 %all-to-all-start = ((f32[64,8,256]{2,1,0:T(8,128)}), f32[64,8,256]{2,1,0:T(8,128)S(1)}, u32[]{:S(2)}, u32[]{:S(2)}) async-start(f32[64,8,256]{2,1,0:T(8,128)} %fusion.11), calls=%async_computation | async-start | bytes 1048576 | tf_op jit(solution)/shard_map/all_to_all | solution.py:104
  30.3 1.2 gather_fusion.3
  31.7 0.7 broadcast_select_fusion.1
  32.4 14.6 %all-to-all-done = f32[64,8,256]{2,1,0:T(8,128)S(1)} async-done(((f32[64,8,256]{2,1,0:T(8,128)}), f32[64,8,256]{2,1,0:T(8,128)S(1)}, u32[]{:S(2)}, u32[]{:S(2)}) %all-to-all-start) | async-done | bytes 524320 | tf_op jit(solution)/shard_map/all_to_all | solution.py:104
  47.4 1.2 convert_reduce_fusion
  48.9 2.6 %gather_fusion.2 = s32[1536,4]{1,0:T(8,128)S(1)} fusion(s32[128,4]{1,0:T(8,128)S(1)} %copy.96, s32[2048]{0:T(1024)S(1)} %pad_clamp_fusion.1), kind=kCustom, calls=%fused_computation.2 | custom fusion | bytes 55296 | tf_op jit(solution)/shard_map/gather | solution.py:117
  51.9 2.8 %collective-permute-start.2 = (f32[8,256]{1,0:T(8,128)S(1)}, f32[8,256]{1,0:T(8,128)S(1)}, u32[]{:S(2)}, u32[]{:S(2)}) collective-permute-start(f32[8,256]{1,0:T(8,128)S(1)} %reduce_sum.78), channel_id=1, source_target_pairs={{0,192},{64,0},{128,64},{192,128},{1,193},{65,1},{129,65},{193,129... | collective-permute-start | bytes 24584 | tf_op jit(solution)/shard_map/ppermute | solution.py:44
  54.7 0.3 collective-permute-start.1
  55.0 0.7 collective-permute-start
  55.9 2.6 %gather_fusion = s32[1536,8]{1,0:T(8,128)S(1)} fusion(s32[128,8]{1,0:T(8,128)S(1)} %copy.93, s32[2048]{0:T(1024)S(1)} %pad_clamp_fusion.1), kind=kCustom, calls=%fused_computation | custom fusion | bytes 104448 | tf_op jit(solution)/shard_map/gather | solution.py:86
  58.8 0.8 broadcast_in_dim.291
  59.6 8.0 %all-to-all-start.1 = ((f32[64,8,256]{2,1,0:T(8,128)}), f32[64,8,256]{2,1,0:T(8,128)S(1)}, u32[]{:S(2)}, u32[]{:S(2)}) async-start(f32[64,8,256]{2,1,0:T(8,128)} %broadcast_in_dim.291), calls=%async_computation.1 | async-start | bytes 1048576 | tf_op jit(solution)/shard_map/all_to_all | solution.py:119
  67.6 1.2 select_reduce_fusion
  69.2 2.6 %gather_fusion.1 = f32[1536,128]{1,0:T(8,128)S(1)} fusion(f32[1024,128]{1,0:T(8,128)S(1)} %bitcast.143, s32[2048]{0:T(1024)S(1)} %pad_clamp_fusion), kind=kCustom, calls=%fused_computation.1 | custom fusion | bytes 1579008 | tf_op jit(solution)/shard_map/gather | solution.py:92
  72.3 0.6 fusion.34
  73.6 1.1 pad_maximum_fusion
  74.7 11.0 %all-to-all-done.1 = f32[64,8,256]{2,1,0:T(8,128)S(1)} async-done(((f32[64,8,256]{2,1,0:T(8,128)}), f32[64,8,256]{2,1,0:T(8,128)S(1)}, u32[]{:S(2)}, u32[]{:S(2)}) %all-to-all-start.1) | async-done | bytes 524320 | tf_op jit(solution)/shard_map/all_to_all | solution.py:119
  85.7 6.5 %all-to-all-start.2 = ((f32[64,8,396]{2,1,0:T(8,128)}), f32[64,8,396]{2,1,0:T(8,128)S(1)}, u32[]{:S(2)}, u32[]{:S(2)}) async-start(f32[64,8,396]{2,1,0:T(8,128)} %pad_maximum_fusion), calls=%async_computation.2 | async-start | bytes 2097152 | tf_op jit(solution)/shard_map/all_to_all | solution.py:124
  92.6 11.7 %cholesky.44 = f32[128,128]{1,0:T(8,128)S(1)} custom-call(f32[128,128]{1,0:T(8,128)S(1)} %fusion.29), custom_call_target="Cholesky" | custom-call | tf_op jit(solution)/shard_map/jit(cholesky)/cholesky | solution.py:18
  104.3 0.6 compare_reduce_fusion.1
  105.0 0.7 fusion.22
  105.6 9.8 %custom-call.8 = f32[1,128,128]{1,2,0:T(8,128)S(1)} custom-call(f32[1,128,128]{2,1,0:T(8,128)S(1)} %fusion.22), custom_call_target="InvertDiagBlocksLowerTriangular" | custom-call | tf_op jit(solution)/shard_map/jit(_solve_triangular)/triangular_solve | solution.py:19
  116.4 11.7 %cholesky.55 = f32[128,128]{1,0:T(8,128)S(1)} custom-call(f32[128,128]{1,0:T(8,128)S(1)} %fusion.27), custom_call_target="Cholesky" | custom-call | tf_op jit(solution)/shard_map/jit(cholesky)/cholesky | solution.py:21
  128.1 0.6 compare_reduce_fusion
  128.8 0.7 fusion.23
  129.5 10.0 %custom-call.9 = f32[1,128,128]{1,2,0:T(8,128)S(1)} custom-call(f32[1,128,128]{2,1,0:T(8,128)S(1)} %fusion.23), custom_call_target="InvertDiagBlocksLowerTriangular" | custom-call | tf_op jit(solution)/shard_map/jit(_solve_triangular)/triangular_solve | solution.py:22
  140.9 1.6 copy.99
  142.5 4.9 %fusion.1 = f32[4,128,24,64]{1,2,0,3:T(8,128)S(1)} fusion(f32[64,4,24,128]{3,2,1,0:T(8,128)} %bitcast.148, s32[64,24,4]{1,2,0:T(4,128)S(1)} %copy.103), kind=kOutput, calls=%fused_computation.6 | convolution fusion | flops 226639872 | bytes 6316032 | tf_op jit(solution)/shard_map/srpq,spqc->srpc/dot_general | solution.py:134
  147.4 0.8 copy.104
  148.2 2.8 %reshape.425 = f32[512,24,64,1]{0,2,1,3:T(8,128)} reshape(f32[4,128,24,64]{1,0,3,2:T(4,128)S(1)} %copy.104) | data formatting | bytes 6291456 | tf_op jit(solution)/shard_map/sri,srpc->ipc/dot_general | solution.py:135
  151.1 4.6 %fusion.5 = f32[4,32,512]{2,1,0:T(8,128)S(1)} fusion(f32[512,24,64,1]{0,2,1,3:T(8,128)} %reshape.425, f32[4,32,24,64]{3,2,1,0:T(8,128)} %bitcast.144), kind=kOutput, calls=%fused_computation.10 | convolution fusion | flops 1207959552 | bytes 4194304 | tf_op jit(solution)/shard_map/sri,srpc->ipc/dot_general | solution.py:135
  155.7 1.1 collective-permute-start.5
  156.9 1.4 collective-permute-start.4
  158.3 0.4 fusion.8
  158.9 2.5 %collective-permute-done.4 = f32[32,512]{1,0:T(8,128)S(1)} collective-permute-done((f32[32,512]{1,0:T(8,128)S(1)}, f32[32,512]{1,0:T(8,128)S(1)}, u32[]{:S(2)}, u32[]{:S(2)}) %collective-permute-start.4) | collective-permute-done | bytes 65568 | tf_op jit(solution)/shard_map/ppermute | solution.py:147
  161.5 2.0 %collective-permute-done.3 = f32[32,512]{1,0:T(8,128)S(1)} collective-permute-done((f32[32,512]{1,0:T(8,128)S(1)}, f32[32,512]{1,0:T(8,128)S(1)}, u32[]{:S(2)}, u32[]{:S(2)}) %collective-permute-start.3) | collective-permute-done | bytes 65568 | tf_op jit(solution)/shard_map/ppermute | solution.py:147
  163.6 0.3 fusion.13
  163.9 0.3 convolution_subtract_fusion.1
  164.3 1.3 collective-permute-start.7
  165.6 2.7 %collective-permute-start.8 = (f32[32,512]{1,0:T(8,128)S(1)}, f32[32,512]{1,0:T(8,128)S(1)}, u32[]{:S(2)}, u32[]{:S(2)}) collective-permute-start(f32[32,512]{1,0:T(8,128)S(1)} %get-tuple-element.31), channel_id=1, source_target_pairs={{0,192},{64,0},{128,64},{192,128},{1,193},{65,1},{129,65},{193,129... | collective-permute-start | bytes 196616 | tf_op jit(solution)/shard_map/ppermute | solution.py:166
  168.2 0.7 collective-permute-done.7
  169.0 0.9 collective-permute-done.6
  170.0 0.7 fusion.43
  (100 shorter events, 6.7 us)
Async XLA Ops:
  7.2 22.5 %copy-start.3 = (s32[128,8]{0,1:T(8,128)S(1)}, s32[128,8]{0,1:T(8,128)}, u32[]{:S(2)}) copy-start(s32[128,8]{0,1:T(8,128)} %param.9) | copy-start | bytes 12292
  11.7 35.3 %copy-start.5 = (s32[64]{0:T(128)S(1)}, s32[64]{0:T(128)}, u32[]{:S(2)}) copy-start(s32[64]{0:T(128)} %param.11) | copy-start | bytes 772
  16.7 30.3 %all-to-all-start = ((f32[64,8,256]{2,1,0:T(8,128)}), f32[64,8,256]{2,1,0:T(8,128)S(1)}, u32[]{:S(2)}, u32[]{:S(2)}) async-start(f32[64,8,256]{2,1,0:T(8,128)} %fusion.11), calls=%async_computation | async-start | bytes 1048576 | tf_op jit(solution)/shard_map/all_to_all | solution.py:104
  29.6 112.9 %all-gather.2.cloned.1.call-start = ((), (), s32[]{:S(2)}) async-start(), calls=%async_computation.3 | async-start | bytes 3194880 | tf_op jit(solution)/shard_map/all_gather | solution.py:113
  51.9 6.7 %collective-permute-start.2 = (f32[8,256]{1,0:T(8,128)S(1)}, f32[8,256]{1,0:T(8,128)S(1)}, u32[]{:S(2)}, u32[]{:S(2)}) collective-permute-start(f32[8,256]{1,0:T(8,128)S(1)} %reduce_sum.78), channel_id=1, source_target_pairs={{0,192},{64,0},{128,64},{192,128},{1,193},{65,1},{129,65},{193,129... | collective-permute-start | bytes 24584 | tf_op jit(solution)/shard_map/ppermute | solution.py:44
  54.7 4.0 %collective-permute-start.1 = (f32[8,256]{1,0:T(8,128)S(1)}, f32[8,256]{1,0:T(8,128)S(1)}, u32[]{:S(2)}, u32[]{:S(2)}) collective-permute-start(f32[8,256]{1,0:T(8,128)S(1)} %reduce_sum.78), channel_id=1, source_target_pairs={{0,128},{64,192},{128,0},{192,64},{1,129},{65,193},{129,1},{193,65... | collective-permute-start | bytes 24584 | tf_op jit(solution)/shard_map/ppermute | solution.py:44
  55.0 3.8 %collective-permute-start = (f32[8,256]{1,0:T(8,128)S(1)}, f32[8,256]{1,0:T(8,128)S(1)}, u32[]{:S(2)}, u32[]{:S(2)}) collective-permute-start(f32[8,256]{1,0:T(8,128)S(1)} %reduce_sum.78), channel_id=1, source_target_pairs={{0,64},{64,128},{128,192},{192,0},{1,65},{65,129},{129,193},{193,1... | collective-permute-start | bytes 24584 | tf_op jit(solution)/shard_map/ppermute | solution.py:44
  58.5 10.7 %copy-start = (f32[128,8,128]{2,1,0:T(8,128)S(1)}, f32[128,8,128]{2,1,0:T(8,128)}, u32[]{:S(2)}) copy-start(f32[128,8,128]{2,1,0:T(8,128)} %param.8) | copy-start | bytes 1572868
  59.6 26.1 %all-to-all-start.1 = ((f32[64,8,256]{2,1,0:T(8,128)}), f32[64,8,256]{2,1,0:T(8,128)S(1)}, u32[]{:S(2)}, u32[]{:S(2)}) async-start(f32[64,8,256]{2,1,0:T(8,128)} %broadcast_in_dim.291), calls=%async_computation.1 | async-start | bytes 1048576 | tf_op jit(solution)/shard_map/all_to_all | solution.py:119
  72.1 20.0 %slice-start = ((f32[512]{0:T(512)}), f32[256]{0:T(256)S(1)}, s32[]{:S(2)}) async-start(f32[512]{0:T(512)} %param.12), calls=%async_computation.4 | async-start | bytes 2048 | tf_op jit(solution)/shard_map/slice | solution.py:129
  85.7 54.7 %all-to-all-start.2 = ((f32[64,8,396]{2,1,0:T(8,128)}), f32[64,8,396]{2,1,0:T(8,128)S(1)}, u32[]{:S(2)}, u32[]{:S(2)}) async-start(f32[64,8,396]{2,1,0:T(8,128)} %pad_maximum_fusion), calls=%async_computation.2 | async-start | bytes 2097152 | tf_op jit(solution)/shard_map/all_to_all | solution.py:124
  92.2 48.4 %copy-start.1 = (f32[512,256]{1,0:T(8,128)}, f32[512,256]{1,0:T(8,128)S(1)}, u32[]{:S(2)}) copy-start(f32[512,256]{1,0:T(8,128)S(1)} %select_add_fusion) | copy-start | bytes 1572868
  151.1 7.2 %copy-start.2 = (f32[512,256]{1,0:T(8,128)S(1)}, f32[512,256]{1,0:T(8,128)}, u32[]{:S(2)}) copy-start(f32[512,256]{1,0:T(8,128)} %copy-done.1) | copy-start | bytes 1572868
  151.1 12.4 %copy-start.4 = (f32[512]{0:T(512)S(1)}, f32[512]{0:T(512)}, u32[]{:S(2)}) copy-start(f32[512]{0:T(512)} %param.12) | copy-start | bytes 6148
  155.7 3.2 %collective-permute-start.5 = (f32[32,512]{1,0:T(8,128)S(1)}, f32[32,512]{1,0:T(8,128)S(1)}, u32[]{:S(2)}, u32[]{:S(2)}) collective-permute-start(f32[32,512]{1,0:T(8,128)S(1)} %get-tuple-element.27), channel_id=1, source_target_pairs={{0,192},{64,0},{128,64},{192,128},{1,193},{65,1},{129,65},{193,129... | collective-permute-start | bytes 196616 | tf_op jit(solution)/shard_map/ppermute | solution.py:147
  156.9 4.6 %collective-permute-start.4 = (f32[32,512]{1,0:T(8,128)S(1)}, f32[32,512]{1,0:T(8,128)S(1)}, u32[]{:S(2)}, u32[]{:S(2)}) collective-permute-start(f32[32,512]{1,0:T(8,128)S(1)} %get-tuple-element.28), channel_id=1, source_target_pairs={{0,128},{64,192},{128,0},{192,64},{1,129},{65,193},{129,1},{193,65... | collective-permute-start | bytes 196616 | tf_op jit(solution)/shard_map/ppermute | solution.py:147
  158.3 5.2 %collective-permute-start.3 = (f32[32,512]{1,0:T(8,128)S(1)}, f32[32,512]{1,0:T(8,128)S(1)}, u32[]{:S(2)}, u32[]{:S(2)}) collective-permute-start(f32[32,512]{1,0:T(8,128)S(1)} %get-tuple-element.29), channel_id=1, source_target_pairs={{0,64},{64,128},{128,192},{192,0},{1,65},{65,129},{129,193},{193,1... | collective-permute-start | bytes 196616 | tf_op jit(solution)/shard_map/ppermute | solution.py:147
  164.3 4.7 %collective-permute-start.7 = (f32[32,512]{1,0:T(8,128)S(1)}, f32[32,512]{1,0:T(8,128)S(1)}, u32[]{:S(2)}, u32[]{:S(2)}) collective-permute-start(f32[32,512]{1,0:T(8,128)S(1)} %get-tuple-element.31), channel_id=1, source_target_pairs={{0,128},{64,192},{128,0},{192,64},{1,129},{65,193},{129,1},{193,65... | collective-permute-start | bytes 196616 | tf_op jit(solution)/shard_map/ppermute | solution.py:166
  165.6 4.3 %collective-permute-start.6 = (f32[32,512]{1,0:T(8,128)S(1)}, f32[32,512]{1,0:T(8,128)S(1)}, u32[]{:S(2)}, u32[]{:S(2)}) collective-permute-start(f32[32,512]{1,0:T(8,128)S(1)} %get-tuple-element.31), channel_id=1, source_target_pairs={{0,64},{64,128},{128,192},{192,0},{1,65},{65,129},{129,193},{193,1... | collective-permute-start | bytes 196616 | tf_op jit(solution)/shard_map/ppermute | solution.py:166
  165.6 4.3 %collective-permute-start.8 = (f32[32,512]{1,0:T(8,128)S(1)}, f32[32,512]{1,0:T(8,128)S(1)}, u32[]{:S(2)}, u32[]{:S(2)}) collective-permute-start(f32[32,512]{1,0:T(8,128)S(1)} %get-tuple-element.31), channel_id=1, source_target_pairs={{0,192},{64,0},{128,64},{192,128},{1,193},{65,1},{129,65},{193,129... | collective-permute-start | bytes 196616 | tf_op jit(solution)/shard_map/ppermute | solution.py:166
Sparse Core Ops, SparseCore 0:
  47.1 80.4 all-gather.1
